TPU v7x, 256 devices: a whole 4x4x8 slice. The times are simulated.
256 devices in a mesh: seq: 64 (over z_hi, x, y, core), tp: 4 (over z_lo).
Axes of the slice: x: 4, y: 4, z: 8 (z_hi: 2, z_lo: 4; z = z_hi * 4 + z_lo), core: 2. Of those that a mesh axis runs over, the one named last changes fastest.
Arguments:
- query_rows: bfloat16 [16384, 4096], P('seq', 'tp'), may hold values from -6 to 6
- key_rows: bfloat16 [16384, 4096], P('seq', 'tp'), may hold values from -6 to 6
- value_rows: bfloat16 [16384, 4096], P('seq', 'tp'), may hold values from -6 to 6
- short_filter: float32 [3, 3, 4096], P(None, None, 'tp'), may hold values from -3 to 3
- long_filter: bfloat16 [16384, 4096], P('seq', 'tp'), may hold values from -1.1 to 1.1, as said below
- skip_gain: float32 [4096], P('tp'), may hold values from -4 to 4
- out_weight: bfloat16 [4096, 4096], P('seq', 'tp'), may hold values from -0.09375 to 0.09375
Outputs:
- projected: bfloat16 [16384, 4096], P('seq', 'tp')
Inputs may be any that keep to these rules, and one draw needn't show every extreme that they name: `long_filter`: taps of the long filter.
All inputs are finite; a program needn't handle non-finite values.
Results may differ from a plain program's by a relative error of at most 0.0061.
Values may be sent and summed in bfloat16 or wider, within the bound.
No kernel may reach another device: no remote copies, remote signals or barrier semaphores. Data moves between devices by JAX's collectives and lax.ppermute only.
A program may use at most 64 MiB of HBM per device.

v0:
```python
import math

import jax
import jax.numpy as jnp
from jax import lax
from jax.sharding import PartitionSpec as P

TRANSFORM_PRECISION = lax.Precision.HIGH


def shifted(value, axis, by):
    size = lax.axis_size(axis)
    pairs = [(i, i + by) for i in range(size) if 0 <= i + by < size]
    return lax.ppermute(value, axis, pairs)


def split_factor(period):
    factor = 2
    for candidate in range(2, math.isqrt(period) + 1, 2):
        if period % candidate == 0:
            factor = candidate
    return factor


def angle_table(rows_count, cols_count, modulus):
    first = jnp.arange(rows_count, dtype=jnp.int32)[:, None]
    second = jnp.arange(cols_count, dtype=jnp.int32)[None, :]
    turns = (first * second % modulus).astype(jnp.float32)
    phase = turns * (2.0 * math.pi / modulus)
    return (jnp.cos(phase), jnp.sin(phase))


def make_tables(length):
    period = 2 * length
    factor_a = split_factor(period)
    factor_b = period // factor_a
    half = factor_a // 2
    a_cos, a_sin = angle_table(factor_a, factor_a, factor_a)
    b_cos, b_sin = angle_table(factor_b, factor_b, factor_b)
    t_cos, t_sin = angle_table(factor_a, factor_b, period)
    return (
        half,
        factor_b,
        period,
        a_cos[:, :half],
        a_sin[:, :half],
        a_cos[:half],
        a_sin[:half],
        b_cos,
        b_sin,
        t_cos,
        t_sin,
    )


def product_table(t_real, t_imag, x_real, x_imag, form):
    first = jnp.einsum(form, t_real + t_imag, x_real, precision=TRANSFORM_PRECISION)
    second = jnp.einsum(form, t_real, x_imag - x_real, precision=TRANSFORM_PRECISION)
    third = jnp.einsum(form, t_imag, x_real + x_imag, precision=TRANSFORM_PRECISION)
    return (first - third, first + second)


def spectrum(signal, tables):
    half, factor_b, period, fa_cos, fa_sin, ia_cos, ia_sin, b_cos, b_sin, t_cos, t_sin = tables
    count = signal.shape[0]
    values = signal.astype(jnp.float32).reshape(count, half, factor_b)
    s_real = jnp.einsum("kn,cnb->ckb", fa_cos, values, precision=TRANSFORM_PRECISION)
    s_imag = -jnp.einsum("kn,cnb->ckb", fa_sin, values, precision=TRANSFORM_PRECISION)
    w_real = s_real * t_cos + s_imag * t_sin
    w_imag = s_imag * t_cos - s_real * t_sin
    return product_table(b_cos, -b_sin, w_real, w_imag, "qb,ckb->ckq")


def convolve(signal, filter_spec, tables):
    half, factor_b, period, fa_cos, fa_sin, ia_cos, ia_sin, b_cos, b_sin, t_cos, t_sin = tables
    count = signal.shape[0]
    u_real, u_imag = spectrum(signal, tables)
    f_real, f_imag = filter_spec
    p_real = u_real * f_real - u_imag * f_imag
    p_imag = u_real * f_imag + u_imag * f_real
    q_real, q_imag = product_table(b_cos, b_sin, p_real, p_imag, "bq,ckq->ckb")
    r_real = q_real * t_cos - q_imag * t_sin
    r_imag = q_imag * t_cos + q_real * t_sin
    result = jnp.einsum("nk,ckb->cnb", ia_cos, r_real, precision=TRANSFORM_PRECISION) - jnp.einsum(
        "nk,ckb->cnb", ia_sin, r_imag, precision=TRANSFORM_PRECISION
    )
    return (result / period).reshape(count, half * factor_b).astype(jnp.bfloat16)


def causal_short(rows, tail, taps):
    extended = jnp.concatenate([tail, rows], 0)
    return (
        taps[0] * extended[2:].astype(jnp.float32)
        + taps[1] * extended[1:-1].astype(jnp.float32)
        + taps[2] * extended[:-2].astype(jnp.float32)
    )


def body(query_rows, key_rows, value_rows, short_filter, long_filter, skip_gain, out_weight):
    tokens_here, channels = query_rows.shape
    groups = lax.axis_size("seq")
    per_device = channels // groups
    length = tokens_here * groups
    tables = make_tables(length)
    tails = shifted((query_rows[-2:], key_rows[-2:], value_rows[-2:]), "seq", 1)
    query_mix = causal_short(query_rows, tails[0], short_filter[:, 0, :])
    key_mix = causal_short(key_rows, tails[1], short_filter[:, 1, :])
    value_mix = causal_short(value_rows, tails[2], short_filter[:, 2, :])
    gated = (key_mix * value_mix).astype(jnp.bfloat16)
    gated_cols = gated.T.reshape(groups, per_device, tokens_here)
    filter_cols = long_filter.T.reshape(groups, per_device, tokens_here)
    signal_piece = lax.all_to_all(gated_cols, "seq", split_axis=0, concat_axis=2, tiled=True)
    filter_piece = lax.all_to_all(filter_cols, "seq", split_axis=0, concat_axis=2, tiled=True)
    mixed = convolve(signal_piece[0], spectrum(filter_piece[0], tables), tables)[None]
    returned = lax.all_to_all(mixed, "seq", split_axis=2, concat_axis=0, tiled=True)
    conv = returned.reshape(channels, tokens_here).T
    inner = (query_mix * (conv.astype(jnp.float32) + skip_gain * gated.astype(jnp.float32))).astype(
        jnp.bfloat16
    )
    weights = lax.all_gather(out_weight, "seq", axis=0, tiled=True)
    total = jnp.dot(
        lax.all_gather(inner, "tp", axis=1, tiled=True), weights, preferred_element_type=jnp.float32
    )
    return total.astype(jnp.bfloat16)


def solution(mesh):
    placed = (
        P("seq", "tp"),
        P("seq", "tp"),
        P("seq", "tp"),
        P(None, None, "tp"),
        P("seq", "tp"),
        P("tp"),
        P("seq", "tp"),
    )
    return jax.shard_map(
        body, mesh=mesh, in_specs=placed, out_specs=P("seq", "tp"), check_vma=False
    )
```

profile of v0, /device:TPU:1, one launch (start us, length us, event | category | flops | bytes accessed | tf_op | source)
XLA Modules:
  0.0 448.5 jit_solution(3382491522677879347)
XLA Ops:
  6.5 2.1 copy.113
  8.7 15.6 %all-to-all-start.1 = ((bf16[64,16,256]{2,1,0:T(8,128)(2,1)}), bf16[64,16,256]{2,1,0:T(8,128)(2,1)S(1)}, u32[]{:S(2)}, u32[]{:S(2)}) async-start(bf16[64,16,256]{2,1,0:T(8,128)(2,1)} %bitcast.23), calls=%async_computation.1 | async-start | bytes 1048576 | tf_op jit(solution)/shard_map/all_to_all | solution.py:113
  24.3 0.0 copy-done.1
  24.3 0.2 copy.105
  24.5 3.5 collective-permute-start.1
  28.1 0.0 copy-done.2
  28.1 0.2 copy.108
  28.3 2.0 collective-permute-start.2
  30.3 0.3 fusion.117
  30.6 0.5 fusion.112
  31.1 0.6 fusion.155
  31.8 0.3 fusion.118
  32.0 0.2 copy.104
  32.2 0.2 copy.107
  32.4 0.1 copy.115
  32.5 0.1 copy.116
  32.6 0.4 collective-permute-done.1
  33.0 4.4 collective-permute-done.2
  37.4 3.9 multiply_convert_fusion
  41.3 0.2 all-to-all-done.1
  41.5 18.9 %all-to-all-start = ((bf16[64,16,256]{2,1,0:T(8,128)(2,1)}), bf16[64,16,256]{2,1,0:T(8,128)(2,1)S(1)}, u32[]{:S(2)}, u32[]{:S(2)}) async-start(bf16[64,16,256]{2,1,0:T(8,128)(2,1)} %bitcast.10), calls=%async_computation | async-start | bytes 1048576 | tf_op jit(solution)/shard_map/all_to_all | solution.py:112
  60.4 0.8 fusion.59
  61.1 1.0 multiply_add_fusion.1
  62.2 2.1 fusion.4
  64.3 2.4 fusion.36
  66.6 3.6 fusion.37
  70.3 10.0 %all-to-all-done = bf16[64,16,256]{2,1,0:T(8,128)(2,1)S(1)} async-done(((bf16[64,16,256]{2,1,0:T(8,128)(2,1)}), bf16[64,16,256]{2,1,0:T(8,128)(2,1)S(1)}, u32[]{:S(2)}, u32[]{:S(2)}) %all-to-all-start) | async-done | bytes 524320 | tf_op jit(solution)/shard_map/all_to_all | solution.py:112
  80.2 1.0 fusion.63
  81.2 1.2 fusion.6
  82.4 2.9 fusion.85
  85.3 2.9 fusion.24
  88.3 0.0 copy-done
  88.3 3.3 multiply_add_fusion
  91.6 2.1 fusion.77
  93.7 2.1 fusion.33
  95.8 2.3 fusion.30
  98.1 1.4 fusion.8
  99.5 1.5 fusion.47
  101.0 0.2 convert_element_type.151
  101.2 12.7 %copy.126 = bf16[1,16,16384]{1,0,2:T(2,128)(2,1)} copy(bf16[1,16,16384]{2,1,0:T(8,128)(2,1)S(1)} %convert_element_type.151) | data formatting | bytes 1048576 | tf_op jit(solution)/shard_map/convert_element_type | solution.py:87
  113.9 0.5 broadcast.130
  114.4 90.8 %reduce = bf16[16384,16]{1,0:T(8,128)(2,1)} reduce(bf16[16384,1,16]{2,1,0:T(2,128)(2,1)} %bitcast.159, bf16[]{:T(256)} %broadcast.130), dimensions={1}, to_apply=%bitcast.138.reduce_sub_computation | reduce | bytes 1048578
  205.2 7.1 %reshape.104 = bf16[64,2,2048]{2,1,0:T(2,128)(2,1)} reshape(bf16[16384,16]{1,0:T(8,128)(2,1)} %reduce) | data formatting | bytes 1048576
  212.3 5.0 %all-to-all-start.2 = ((bf16[64,2,2048]{2,1,0:T(2,128)(2,1)}), bf16[64,2,2048]{2,1,0:T(2,128)(2,1)S(1)}, u32[]{:S(2)}, u32[]{:S(2)}) async-start(bf16[64,2,2048]{2,1,0:T(2,128)(2,1)} %reshape.104), calls=%async_computation.2 | async-start | bytes 1048576 | tf_op jit(solution)/shard_map/all_to_all | solution.py:115
  217.4 0.0 all-gather.3.cloned.1.call-start
  217.4 0.0 copy-done.3
  217.4 0.2 copy.102
  217.6 3.5 collective-permute-start
  221.2 0.2 copy.101
  221.4 16.4 %all-to-all-done.2 = bf16[64,2,2048]{2,1,0:T(2,128)(2,1)S(1)} async-done(((bf16[64,2,2048]{2,1,0:T(2,128)(2,1)}), bf16[64,2,2048]{2,1,0:T(2,128)(2,1)S(1)}, u32[]{:S(2)}, u32[]{:S(2)}) %all-to-all-start.2) | async-done | bytes 524320 | tf_op jit(solution)/shard_map/all_to_all | solution.py:115
  237.8 14.9 %reshape.105 = bf16[16384,1,16]{2,1,0:T(2,128)(2,1)} reshape(bf16[64,2,2048]{2,1,0:T(2,128)(2,1)S(1)} %all-to-all-done.2) | data formatting | bytes 1048576
  252.7 14.9 %copy.127 = bf16[1,16,16384]{2,1,0:T(8,128)(2,1)S(1)} copy(bf16[1,16,16384]{1,0,2:T(2,128)(2,1)} %bitcast.160) | data formatting | bytes 1048576 | tf_op jit(solution)/shard_map/all_to_all | solution.py:115
  267.6 0.1 copy.141
  267.7 0.0 copy-start.5
  267.7 0.1 bitcast_bitcast_fusion
  267.8 0.6 copy.128
  268.4 0.0 collective-permute-done
  268.5 2.9 fusion.51
  271.3 0.0 all-gather.3.cloned.1.call-update
  271.4 0.0 all-gather.5.cloned.1.call-start
  271.4 0.7 all-gather.5.cloned.1.call-update
  272.1 45.5 %all-gather.3.cloned.1.call-done = bf16[256,4096]{0,1:T(8,128)(2,1)} async-done(((bf16[256,1024]{0,1:T(8,128)(2,1)}), bf16[256,4096]{0,1:T(8,128)(2,1)}) %all-gather.3.cloned.1.call-update) | async-done | bytes 2097168 | tf_op jit(solution)/shard_map/all_gather | solution.py:122
  317.6 116.6 %all-gather.5.cloned.1.call-done = bf16[4096,1024]{1,0:T(8,128)(2,1)} async-done(((bf16[64,1024]{1,0:T(8,128)(2,1)}), bf16[4096,1024]{1,0:T(8,128)(2,1)}) %all-gather.5.cloned.1.call-update) | async-done | bytes 8388624 | tf_op jit(solution)/shard_map/all_gather | solution.py:120
  434.3 7.2 %convolution_convert_fusion = bf16[256,1024]{1,0:T(8,128)(2,1)} fusion(bf16[256,4096]{0,1:T(8,128)(2,1)} %all-gather.3.cloned.1.call-done, bf16[4096,1024]{1,0:T(8,128)(2,1)} %all-gather.5.cloned.1.call-done), kind=kOutput, calls=%fused_computation.43 | convolution fusion | flops 2147745792 | bytes 11010048 | tf_op jit(solution)/shard_map/dot_general | solution.py:121
  (10 shorter events, 0.0 us)
Async XLA Ops:
  6.5 17.7 %copy-start.1 = (bf16[256,1024]{1,0:T(8,128)(2,1)S(1)}, bf16[256,1024]{1,0:T(8,128)(2,1)}, u32[]{:S(2)}) copy-start(bf16[256,1024]{1,0:T(8,128)(2,1)} %param.8) | copy-start | bytes 1572868
  6.5 21.5 %copy-start.2 = (bf16[256,1024]{1,0:T(8,128)(2,1)S(1)}, bf16[256,1024]{1,0:T(8,128)(2,1)}, u32[]{:S(2)}) copy-start(bf16[256,1024]{1,0:T(8,128)(2,1)} %param.9) | copy-start | bytes 1572868
  6.5 24.6 %copy-start.4 = (f32[3,3,1024]{2,1,0:T(4,128)S(1)}, f32[3,3,1024]{2,1,0:T(4,128)}, u32[]{:S(2)}) copy-start(f32[3,3,1024]{2,1,0:T(4,128)} %param.10) | copy-start | bytes 110596
  8.7 32.8 %all-to-all-start.1 = ((bf16[64,16,256]{2,1,0:T(8,128)(2,1)}), bf16[64,16,256]{2,1,0:T(8,128)(2,1)S(1)}, u32[]{:S(2)}, u32[]{:S(2)}) async-start(bf16[64,16,256]{2,1,0:T(8,128)(2,1)} %bitcast.23), calls=%async_computation.1 | async-start | bytes 1048576 | tf_op jit(solution)/shard_map/all_to_all | solution.py:113
  24.5 8.5 %collective-permute-start.1 = (bf16[2,1024]{0,1:T(8,128)(2,1)S(1)}, bf16[2,1024]{0,1:T(8,128)(2,1)S(1)}, u32[]{:S(2)}, u32[]{:S(2)}) collective-permute-start(bf16[2,1024]{0,1:T(8,128)(2,1)S(1)} %copy.105), channel_id=1, source_target_pairs={{0,4},{4,8},{8,12},{12,16},{16,20},{20,24},{24,28},{28,32},{32,36}... | collective-permute-start | bytes 12296 | tf_op jit(solution)/shard_map/ppermute | solution.py:14
  28.3 9.1 %collective-permute-start.2 = (bf16[2,1024]{0,1:T(8,128)(2,1)S(1)}, bf16[2,1024]{0,1:T(8,128)(2,1)}, u32[]{:S(2)}, u32[]{:S(2)}) collective-permute-start(bf16[2,1024]{0,1:T(8,128)(2,1)S(1)} %copy.108), channel_id=1, source_target_pairs={{0,4},{4,8},{8,12},{12,16},{16,20},{20,24},{24,28},{28,32},{32,36}... | collective-permute-start | bytes 12296 | tf_op jit(solution)/shard_map/ppermute | solution.py:14
  41.5 38.8 %all-to-all-start = ((bf16[64,16,256]{2,1,0:T(8,128)(2,1)}), bf16[64,16,256]{2,1,0:T(8,128)(2,1)S(1)}, u32[]{:S(2)}, u32[]{:S(2)}) async-start(bf16[64,16,256]{2,1,0:T(8,128)(2,1)} %bitcast.10), calls=%async_computation | async-start | bytes 1048576 | tf_op jit(solution)/shard_map/all_to_all | solution.py:112
  85.3 2.9 copy-start
  205.2 12.2 %copy-start.3 = (bf16[256,1024]{1,0:T(8,128)(2,1)S(1)}, bf16[256,1024]{1,0:T(8,128)(2,1)}, u32[]{:S(2)}) copy-start(bf16[256,1024]{1,0:T(8,128)(2,1)} %param.7) | copy-start | bytes 1572868
  212.3 25.4 %all-to-all-start.2 = ((bf16[64,2,2048]{2,1,0:T(2,128)(2,1)}), bf16[64,2,2048]{2,1,0:T(2,128)(2,1)S(1)}, u32[]{:S(2)}, u32[]{:S(2)}) async-start(bf16[64,2,2048]{2,1,0:T(2,128)(2,1)} %reshape.104), calls=%async_computation.2 | async-start | bytes 1048576 | tf_op jit(solution)/shard_map/all_to_all | solution.py:115
  217.4 100.3 %all-gather.3.cloned.1.call-start = ((), (), s32[]{:S(2)}) async-start(), calls=%async_computation.3 | async-start | bytes 2621440 | tf_op jit(solution)/shard_map/all_gather | solution.py:122
  217.6 50.8 %collective-permute-start = (bf16[2,1024]{0,1:T(8,128)(2,1)S(1)}, bf16[2,1024]{0,1:T(8,128)(2,1)S(1)}, u32[]{:S(2)}, u32[]{:S(2)}) collective-permute-start(bf16[2,1024]{0,1:T(8,128)(2,1)S(1)} %copy.102), channel_id=1, source_target_pairs={{0,4},{4,8},{8,12},{12,16},{16,20},{20,24},{24,28},{28,32},{32,36}... | collective-permute-start | bytes 12296 | tf_op jit(solution)/shard_map/ppermute | solution.py:14
  267.7 0.7 copy-start.5
  271.4 162.9 %all-gather.5.cloned.1.call-start = ((), (), s32[]{:S(2)}) async-start(), calls=%async_computation.4 | async-start | bytes 8519680 | tf_op jit(solution)/shard_map/all_gather | solution.py:120
Sparse Core Ops, SparseCore 0:
  271.5 46.1 all-gather.2
  321.2 112.9 all-gather.4
where the time goes:
time: 453 us; the launch traced here: 449 us
  waiting for transfers between devices  194 us (43%)
  other arithmetic  98.6 us (22%)
  local copies, waits for them, and re-layouts  55.4 us (12%)
  starting transfers between devices  48.7 us (11%)
  matrix products  37.7 us (8%)
  between operations  14 us (3%)
    all_gather x1, waiting for transfers between devices, body(): weights = lax.all_gather(out_weight, 'seq', axis=0, tiled=True)  117 us
    unnamed x1, other arithmetic  90.8 us
    all_gather x1, waiting for transfers between devices, body(): lax.all_gather(inner, 'tp', axis=1, tiled=True)  45.5 us
    unnamed x20, local copies, waits for them, and re-layouts  25.4 us
    all_to_all x1, starting transfers between devices, body(): lax.all_to_all(gated_cols, 'seq', split_axis=0, concat_axis=2, tiled=True)  18.9 us
    all_to_all x1, waiting for transfers between devices, body(): lax.all_to_all(mixed, 'seq', split_axis=2, concat_axis=0, tiled=True)  16.4 us
    all_to_all x1, starting transfers between devices, body(): lax.all_to_all(filter_cols, 'seq', split_axis=0, concat_axis=2, tiled=True)  15.6 us
    all_to_all x1, local copies, waits for them, and re-layouts, body(): lax.all_to_all(mixed, 'seq', split_axis=2, concat_axis=0, tiled=True)  14.9 us
  transfers between devices with their start and end apart: 8, of which 7 were waited for; matrix products, arithmetic and copies ran while one was open for 11% of the time, Pallas kernels for 0%

commit v1 on v0

v1 whole, which is shorter than its diff:
```python
import math

import numpy as np
import jax
import jax.numpy as jnp
from jax import lax
from jax.sharding import PartitionSpec as P

TRANSFORM_PRECISION = lax.Precision.HIGH


def shifted(value, axis, by):
    size = lax.axis_size(axis)
    pairs = [(i, i + by) for i in range(size) if 0 <= i + by < size]
    return lax.ppermute(value, axis, pairs)


def make_tables(blocks, tokens):
    outer = 2 * blocks
    period = outer * tokens
    k1 = np.arange(outer, dtype=np.int64)
    n1 = np.arange(blocks, dtype=np.int64)
    n2 = np.arange(tokens, dtype=np.int64)
    first = 2.0 * np.pi * ((k1[:, None] * n1[None, :]) % outer) / outer
    first_table = np.concatenate([np.cos(first), -np.sin(first)], 0)
    twist = 2.0 * np.pi * ((k1[:, None] * n2[None, :]) % period) / period
    twist_cos = np.cos(twist)[:, None, :]
    twist_sin = np.sin(twist)[:, None, :]
    inner = 2.0 * np.pi * ((n2[:, None] * n2[None, :]) % tokens) / tokens
    b_cos = np.cos(inner)
    b_sin = np.sin(inner)
    forward = np.block([[b_cos, -b_sin], [b_sin, b_cos]])
    backward = np.block([[b_cos, b_sin], [-b_sin, b_cos]])
    last = 2.0 * np.pi * ((n1[:, None] * k1[None, :]) % outer) / outer
    last_table = np.concatenate([np.cos(last), -np.sin(last)], 1) / period
    as32 = lambda a: jnp.asarray(a, jnp.float32)
    return tuple(as32(a) for a in (first_table, twist_cos, twist_sin, forward, backward, last_table))


def dot(a, b):
    return jnp.dot(a, b, precision=TRANSFORM_PRECISION, preferred_element_type=jnp.float32)


def long_conv(pieces, per_device, tables):
    first_table, twist_cos, twist_sin, forward, backward, last_table = tables
    blocks, both, tokens = pieces.shape
    outer = 2 * blocks
    spec = dot(first_table, pieces.reshape(blocks, both * tokens)).reshape(2, outer, both, tokens)
    s_real, s_imag = spec[0], spec[1]
    w_real = s_real * twist_cos + s_imag * twist_sin
    w_imag = s_imag * twist_cos - s_real * twist_sin
    twisted = jnp.concatenate([w_real, w_imag], -1).reshape(outer * both, 2 * tokens)
    u = dot(twisted, forward).reshape(outer, both, 2 * tokens)
    u_real, u_imag = u[:, :per_device, :tokens], u[:, :per_device, tokens:]
    f_real, f_imag = u[:, per_device:, :tokens], u[:, per_device:, tokens:]
    p_real = u_real * f_real - u_imag * f_imag
    p_imag = u_real * f_imag + u_imag * f_real
    product = jnp.concatenate([p_real, p_imag], -1).reshape(outer * per_device, 2 * tokens)
    q = dot(product, backward).reshape(outer, per_device, 2 * tokens)
    q_real, q_imag = q[..., :tokens], q[..., tokens:]
    r_real = q_real * twist_cos - q_imag * twist_sin
    r_imag = q_real * twist_sin + q_imag * twist_cos
    stacked = jnp.stack([r_real, r_imag], 0).reshape(2 * outer, per_device * tokens)
    result = dot(last_table, stacked)
    return result.reshape(blocks, per_device, tokens).astype(jnp.bfloat16)


def causal_short(rows, tail, taps):
    extended = jnp.concatenate([tail, rows], 0)
    return (
        taps[0] * extended[2:].astype(jnp.float32)
        + taps[1] * extended[1:-1].astype(jnp.float32)
        + taps[2] * extended[:-2].astype(jnp.float32)
    )


def body(query_rows, key_rows, value_rows, short_filter, long_filter, skip_gain, out_weight):
    tokens_here, channels = query_rows.shape
    groups = lax.axis_size("seq")
    per_device = channels // groups
    tables = make_tables(groups, tokens_here)
    tails = shifted((query_rows[-2:], key_rows[-2:], value_rows[-2:]), "seq", 1)
    query_mix = causal_short(query_rows, tails[0], short_filter[:, 0, :])
    key_mix = causal_short(key_rows, tails[1], short_filter[:, 1, :])
    value_mix = causal_short(value_rows, tails[2], short_filter[:, 2, :])
    gated = (key_mix * value_mix).astype(jnp.bfloat16)
    gated_cols = gated.T.reshape(groups, per_device, tokens_here)
    filter_cols = long_filter.T.reshape(groups, per_device, tokens_here)
    outgoing = jnp.concatenate([gated_cols, filter_cols], 1)
    pieces = lax.all_to_all(outgoing, "seq", split_axis=0, concat_axis=0, tiled=True)
    mixed = long_conv(pieces, per_device, tables)
    returned = lax.all_to_all(mixed, "seq", split_axis=0, concat_axis=0, tiled=True)
    conv = returned.reshape(channels, tokens_here).T
    inner = (query_mix * (conv.astype(jnp.float32) + skip_gain * gated.astype(jnp.float32))).astype(
        jnp.bfloat16
    )
    weights = lax.all_gather(out_weight, "seq", axis=0, tiled=True)
    total = jnp.dot(
        lax.all_gather(inner, "tp", axis=1, tiled=True), weights, preferred_element_type=jnp.float32
    )
    return total.astype(jnp.bfloat16)


def solution(mesh):
    placed = (
        P("seq", "tp"),
        P("seq", "tp"),
        P("seq", "tp"),
        P(None, None, "tp"),
        P("seq", "tp"),
        P("tp"),
        P("seq", "tp"),
    )
    return jax.shard_map(
        body, mesh=mesh, in_specs=placed, out_specs=P("seq", "tp"), check_vma=False
    )
```

time: 453 us -> 304 us (0.67)
  other arithmetic: 98.6 us -> 6.97 us
  local copies, waits for them, and re-layouts: 55.4 us -> 16.3 us
  blocking collectives: 0 us -> 38.1 us
  starting transfers between devices: 48.7 us -> 25.6 us
  matrix products: 37.7 us -> 21.4 us
  waiting for transfers between devices: 194 us -> 181 us
    unnamed x1 -> x0, other arithmetic: 90.8 us -> none
    all_to_all x0 -> x1, blocking collectives: none -> 38.1 us  [body(): lax.all_to_all(outgoing, 'seq', split_axis=0, concat_axis=0, tiled=True)]
    all_to_all x3 -> x1, starting transfers between devices: 39.5 us -> 15.5 us  [body(): lax.all_to_all(mixed, 'seq', split_axis=0, concat_axis=0, tiled=True)]
    dot_general x15 -> x4, matrix products: 30.5 us -> 14.2 us  [dot(): jnp.dot(a, b, precision=TRANSFORM_PRECISION, preferred_element_type=jnp.f...]
    unnamed x20 -> x23, local copies, waits for them, and re-layouts: 25.4 us -> 10.3 us
    all_to_all x1 -> x0, local copies, waits for them, and re-layouts: 14.9 us -> none  [body(): lax.all_to_all(mixed, 'seq', split_axis=2, concat_axis=0, tiled=True)]
    all_to_all x3 -> x1, waiting for transfers between devices: 26.5 us -> 11.9 us  [body(): lax.all_to_all(mixed, 'seq', split_axis=0, concat_axis=0, tiled=True)]
    convert_element_type x4 -> x0, local copies, waits for them, and re-layouts: 13.6 us -> none  [the longest x2 12.9 us: convolve(): (result / period).reshape(count, half * factor_b).astype(jnp.bfloat16)]
  transfers between devices with their start and end apart: 8 -> 6, of which waited for: 7 -> 4; matrix products, arithmetic and copies ran while one was open for 11% -> 2% of each run, Pallas kernels for 0% -> 0%
where the time goes in v1:
time: 304 us; the launch traced here: 303 us
  waiting for transfers between devices  181 us (60%)
  blocking collectives  38.1 us (13%)
  starting transfers between devices  25.6 us (8%)
  matrix products  21.4 us (7%)
  local copies, waits for them, and re-layouts  16.3 us (5%)
  between operations  13.7 us (5%)
  other arithmetic  6.97 us (2%)
    all_gather x1, waiting for transfers between devices, body(): weights = lax.all_gather(out_weight, 'seq', axis=0, tiled=True)  117 us
    all_gather x1, waiting for transfers between devices, body(): lax.all_gather(inner, 'tp', axis=1, tiled=True)  47.1 us
    all_to_all x1, blocking collectives, body(): lax.all_to_all(outgoing, 'seq', split_axis=0, concat_axis=0, tiled=True)  38.1 us
    all_to_all x1, starting transfers between devices, body(): lax.all_to_all(mixed, 'seq', split_axis=0, concat_axis=0, tiled=True)  15.5 us
    dot_general x4, matrix products, dot(): jnp.dot(a, b, precision=TRANSFORM_PRECISION, preferred_element_type=jnp.f...  14.2 us
    all_to_all x1, waiting for transfers between devices, body(): lax.all_to_all(mixed, 'seq', split_axis=0, concat_axis=0, tiled=True)  11.9 us
    unnamed x23, local copies, waits for them, and re-layouts  10.3 us
    ppermute x3, starting transfers between devices, shifted(): return lax.ppermute(value, axis, pairs)  10 us
  transfers between devices with their start and end apart: 6, of which 4 were waited for; matrix products, arithmetic and copies ran while one was open for 2% of the time, Pallas kernels for 0%

profile of v1, /device:TPU:1, one launch (start us, length us, event | category | flops | bytes accessed | tf_op | source)
XLA Modules:
  0.0 303.2 jit_solution(137879276982766816)
XLA Ops:
  6.5 0.7 slice.109
  7.3 0.2 copy.23
  7.5 4.6 %collective-permute-start.1 = (bf16[2,1024]{0,1:T(8,128)(2,1)S(1)}, bf16[2,1024]{0,1:T(8,128)(2,1)S(1)}, u32[]{:S(2)}, u32[]{:S(2)}) collective-permute-start(bf16[2,1024]{0,1:T(8,128)(2,1)S(1)} %copy.23), channel_id=1, source_target_pairs={{0,4},{4,8},{8,12},{12,16},{16,20},{20,24},{24,28},{28,32},{32,36}... | collective-permute-start | bytes 12296 | tf_op jit(solution)/shard_map/ppermute | solution.py:15
  12.1 0.7 slice.115
  12.8 0.2 copy.26
  13.0 1.9 collective-permute-start.2
  14.9 0.9 fusion.19
  15.8 1.2 copy.22
  17.1 1.2 copy.25
  18.3 1.2 copy.28
  19.6 0.0 collective-permute-done.1
  19.6 0.0 collective-permute-done.2
  19.6 0.0 copy-start.5
  19.6 1.9 multiply_convert_fusion
  21.5 0.1 pad_maximum_fusion.1
  21.6 38.1 %all_to_all.10 = bf16[64,32,256]{2,1,0:T(8,128)(2,1)S(1)} all-to-all(bf16[64,32,256]{2,1,0:T(8,128)(2,1)S(1)} %pad_maximum_fusion.1), channel_id=1, replica_groups=mesh['seq'=64,'tp'=4] {'seq'}, dimensions={0} | all-to-all | bytes 2097152 | tf_op jit(solution)/shard_map/all_to_all | solution.py:90
  59.7 0.6 copy.36
  60.4 0.0 copy-done.5
  60.4 2.3 fusion.20
  62.7 0.0 copy-start.3
  62.7 0.0 copy-start.4
  62.7 0.6 fusion.18
  63.3 0.3 copy-done.3
  63.6 0.1 copy-done.4
  63.7 0.0 copy-start.1
  63.7 1.2 fusion.4
  64.9 0.0 copy-done.1
  64.9 7.0 %fusion = f32[128,32,512]{2,0,1:T(8,128)S(1)} fusion(f32[512,512,1]{1,0,2:T(8,128)S(1)} %copy-done.1, f32[128,32,256]{2,0,1:T(8,128)S(1)} %get-tuple-element.6, f32[128,32,256]{2,0,1:T(8,128)S(1)} %get-tuple-element.5), kind=kOutput, calls=%fused_computation | convolution fusion | flops 6444548096 | bytes 17825792 | tf_op jit(solution)/shard_map/dot_general | solution.py:41
  72.0 0.0 copy-start
  72.0 0.8 multiply_subtract_fusion
  72.8 0.4 copy-done
  73.2 3.5 %fusion.6 = f32[128,16,512]{2,0,1:T(8,128)S(1)} fusion(f32[512,512,1]{1,0,2:T(8,128)S(1)} %copy-done, f32[128,16,256]{2,0,1:T(8,128)S(1)} %get-tuple-element.8, f32[128,16,256]{2,0,1:T(8,128)S(1)} %get-tuple-element.7), kind=kOutput, calls=%fused_computation.11 | convolution fusion | flops 3222274048 | bytes 9437184 | tf_op jit(solution)/shard_map/dot_general | solution.py:41
  76.7 0.6 subtract_bitcast_fusion
  77.4 0.4 pad_maximum_fusion
  77.7 2.4 copy.33
  80.2 0.0 copy-start.6
  80.2 3.8 %copy.37 = f32[32,8,16,256]{3,1,2,0:T(8,128)S(1)} copy(f32[32,8,16,256]{3,2,1,0:T(8,128)S(1)} %bitcast.65) | data formatting | bytes 8388608
  84.0 0.0 copy-start.2
  84.0 0.0 copy-start.7
  84.0 0.0 copy-done.6
  84.0 1.4 convolution_convert_fusion
  85.4 1.2 copy.38
  86.5 15.5 %all-to-all-start.1 = ((bf16[64,16,256]{2,1,0:T(8,128)(2,1)}), bf16[64,16,256]{2,1,0:T(8,128)(2,1)S(1)}, u32[]{:S(2)}, u32[]{:S(2)}) async-start(bf16[64,16,256]{2,1,0:T(8,128)(2,1)} %bitcast.33), calls=%async_computation.1 | async-start | bytes 1048576 | tf_op jit(solution)/shard_map/all_to_all | solution.py:92
  102.0 0.0 all-gather.3.cloned.1.call-start
  102.0 0.0 copy-done.2
  102.1 0.2 copy.20
  102.3 3.5 %collective-permute-start = (bf16[2,1024]{0,1:T(8,128)(2,1)S(1)}, bf16[2,1024]{0,1:T(8,128)(2,1)S(1)}, u32[]{:S(2)}, u32[]{:S(2)}) collective-permute-start(bf16[2,1024]{0,1:T(8,128)(2,1)S(1)} %copy.20), channel_id=1, source_target_pairs={{0,4},{4,8},{8,12},{12,16},{16,20},{20,24},{24,28},{28,32},{32,36}... | collective-permute-start | bytes 12296 | tf_op jit(solution)/shard_map/ppermute | solution.py:15
  105.8 0.2 copy.19
  106.0 4.8 %collective-permute-done = bf16[2,1024]{0,1:T(8,128)(2,1)S(1)} collective-permute-done((bf16[2,1024]{0,1:T(8,128)(2,1)S(1)}, bf16[2,1024]{0,1:T(8,128)(2,1)S(1)}, u32[]{:S(2)}, u32[]{:S(2)}) %collective-permute-start) | collective-permute-done | bytes 4128 | tf_op jit(solution)/shard_map/ppermute | solution.py:15
  110.8 11.9 %all-to-all-done.1 = bf16[64,16,256]{2,1,0:T(8,128)(2,1)S(1)} async-done(((bf16[64,16,256]{2,1,0:T(8,128)(2,1)}), bf16[64,16,256]{2,1,0:T(8,128)(2,1)S(1)}, u32[]{:S(2)}, u32[]{:S(2)}) %all-to-all-start.1) | async-done | bytes 524320 | tf_op jit(solution)/shard_map/all_to_all | solution.py:92
  122.7 0.0 copy-done.7
  122.7 1.9 fusion.12
  124.6 0.0 all-gather.3.cloned.1.call-update
  124.6 0.0 all-gather.5.cloned.1.call-start
  124.7 0.7 all-gather.5.cloned.1.call-update
  125.4 47.1 %all-gather.3.cloned.1.call-done = bf16[256,4096]{0,1:T(8,128)(2,1)} async-done(((bf16[256,1024]{0,1:T(8,128)(2,1)}), bf16[256,4096]{0,1:T(8,128)(2,1)}) %all-gather.3.cloned.1.call-update) | async-done | bytes 2097168 | tf_op jit(solution)/shard_map/all_gather | solution.py:99
  172.5 116.6 %all-gather.5.cloned.1.call-done = bf16[4096,1024]{1,0:T(8,128)(2,1)} async-done(((bf16[64,1024]{1,0:T(8,128)(2,1)}), bf16[4096,1024]{1,0:T(8,128)(2,1)}) %all-gather.5.cloned.1.call-update) | async-done | bytes 8388624 | tf_op jit(solution)/shard_map/all_gather | solution.py:97
  289.1 7.2 %convolution_convert_fusion.1 = bf16[256,1024]{1,0:T(8,128)(2,1)} fusion(bf16[256,4096]{0,1:T(8,128)(2,1)} %all-gather.3.cloned.1.call-done, bf16[4096,1024]{1,0:T(8,128)(2,1)} %all-gather.5.cloned.1.call-done), kind=kOutput, calls=%fused_computation.20 | convolution fusion | flops 2147745792 | bytes 11010048 | tf_op jit(solution)/shard_map/dot_general | solution.py:98
  (1 shorter events, 0.0 us)
Async XLA Ops:
  7.5 12.1 %collective-permute-start.1 = (bf16[2,1024]{0,1:T(8,128)(2,1)S(1)}, bf16[2,1024]{0,1:T(8,128)(2,1)S(1)}, u32[]{:S(2)}, u32[]{:S(2)}) collective-permute-start(bf16[2,1024]{0,1:T(8,128)(2,1)S(1)} %copy.23), channel_id=1, source_target_pairs={{0,4},{4,8},{8,12},{12,16},{16,20},{20,24},{24,28},{28,32},{32,36}... | collective-permute-start | bytes 12296 | tf_op jit(solution)/shard_map/ppermute | solution.py:15
  13.0 6.6 %collective-permute-start.2 = (bf16[2,1024]{0,1:T(8,128)(2,1)S(1)}, bf16[2,1024]{0,1:T(8,128)(2,1)S(1)}, u32[]{:S(2)}, u32[]{:S(2)}) collective-permute-start(bf16[2,1024]{0,1:T(8,128)(2,1)S(1)} %copy.26), channel_id=1, source_target_pairs={{0,4},{4,8},{8,12},{12,16},{16,20},{20,24},{24,28},{28,32},{32,36}... | collective-permute-start | bytes 12296 | tf_op jit(solution)/shard_map/ppermute | solution.py:15
  19.6 40.8 %copy-start.5 = (f32[256,64]{1,0:T(8,128)S(1)}, f32[256,64]{1,0:T(8,128)}, u32[]{:S(2)}) copy-start(f32[256,64]{1,0:T(8,128)} %constant.12.clone) | copy-start | bytes 196612
  62.7 0.9 copy-start.3
  62.7 1.0 copy-start.4
  63.7 1.3 copy-start.1
  72.0 1.2 copy-start
  80.2 3.8 %copy-start.6 = (f32[64,256]{1,0:T(8,128)S(1)}, f32[64,256]{1,0:T(8,128)}, u32[]{:S(2)}) copy-start(f32[64,256]{1,0:T(8,128)} %constant.17.clone) | copy-start | bytes 196612
  84.0 18.1 %copy-start.2 = (bf16[256,1024]{1,0:T(8,128)(2,1)S(1)}, bf16[256,1024]{1,0:T(8,128)(2,1)}, u32[]{:S(2)}) copy-start(bf16[256,1024]{1,0:T(8,128)(2,1)} %param.13) | copy-start | bytes 1572868
  84.0 38.7 %copy-start.7 = (f32[1024]{0:T(1024)S(1)}, f32[1024]{0:T(1024)}, u32[]{:S(2)}) copy-start(f32[1024]{0:T(1024)} %param.18) | copy-start | bytes 12292
  86.5 36.2 %all-to-all-start.1 = ((bf16[64,16,256]{2,1,0:T(8,128)(2,1)}), bf16[64,16,256]{2,1,0:T(8,128)(2,1)S(1)}, u32[]{:S(2)}, u32[]{:S(2)}) async-start(bf16[64,16,256]{2,1,0:T(8,128)(2,1)} %bitcast.33), calls=%async_computation.1 | async-start | bytes 1048576 | tf_op jit(solution)/shard_map/all_to_all | solution.py:92
  102.0 70.5 %all-gather.3.cloned.1.call-start = ((), (), s32[]{:S(2)}) async-start(), calls=%async_computation.2 | async-start | bytes 2621440 | tf_op jit(solution)/shard_map/all_gather | solution.py:99
  102.3 8.5 %collective-permute-start = (bf16[2,1024]{0,1:T(8,128)(2,1)S(1)}, bf16[2,1024]{0,1:T(8,128)(2,1)S(1)}, u32[]{:S(2)}, u32[]{:S(2)}) collective-permute-start(bf16[2,1024]{0,1:T(8,128)(2,1)S(1)} %copy.20), channel_id=1, source_target_pairs={{0,4},{4,8},{8,12},{12,16},{16,20},{20,24},{24,28},{28,32},{32,36}... | collective-permute-start | bytes 12296 | tf_op jit(solution)/shard_map/ppermute | solution.py:15
  124.6 164.5 %all-gather.5.cloned.1.call-start = ((), (), s32[]{:S(2)}) async-start(), calls=%async_computation.3 | async-start | bytes 8519680 | tf_op jit(solution)/shard_map/all_gather | solution.py:97
Sparse Core Ops, SparseCore 0:
  124.8 47.7 all-gather.2
  176.1 112.9 all-gather.4

commit v2 on v1

--- a/solution.py
+++ b/solution.py
@@ -1,5 +1,3 @@
-import math
-
 import numpy as np
 import jax
 import jax.numpy as jnp
@@ -74,11 +72,12 @@
     )
 
 
-def body(query_rows, key_rows, value_rows, short_filter, long_filter, skip_gain, out_weight):
+def block(query_rows, key_rows, value_rows, short_filter, long_filter, skip_gain, out_weight):
     tokens_here, channels = query_rows.shape
     groups = lax.axis_size("seq")
     per_device = channels // groups
     tables = make_tables(groups, tokens_here)
+    weights = lax.all_gather(out_weight, "seq", axis=0, tiled=True)
     tails = shifted((query_rows[-2:], key_rows[-2:], value_rows[-2:]), "seq", 1)
     query_mix = causal_short(query_rows, tails[0], short_filter[:, 0, :])
     key_mix = causal_short(key_rows, tails[1], short_filter[:, 1, :])
@@ -94,7 +93,6 @@
     inner = (query_mix * (conv.astype(jnp.float32) + skip_gain * gated.astype(jnp.float32))).astype(
         jnp.bfloat16
     )
-    weights = lax.all_gather(out_weight, "seq", axis=0, tiled=True)
     total = jnp.dot(
         lax.all_gather(inner, "tp", axis=1, tiled=True), weights, preferred_element_type=jnp.float32
     )
@@ -112,5 +110,5 @@
         P("seq", "tp"),
     )
     return jax.shard_map(
-        body, mesh=mesh, in_specs=placed, out_specs=P("seq", "tp"), check_vma=False
+        block, mesh=mesh, in_specs=placed, out_specs=P("seq", "tp"), check_vma=False
     )

time: 304 us -> 304 us (level)
  no operation moved by 1% of the time
where the time goes in v2:
time: 304 us; the launch traced here: 303 us
  waiting for transfers between devices  181 us (60%)
  blocking collectives  38.1 us (13%)
  starting transfers between devices  25.6 us (8%)
  matrix products  21.4 us (7%)
  local copies, waits for them, and re-layouts  16.3 us (5%)
  between operations  13.7 us (5%)
  other arithmetic  6.97 us (2%)
    all_gather x1, waiting for transfers between devices, block(): weights = lax.all_gather(out_weight, 'seq', axis=0, tiled=True)  117 us
    all_gather x1, waiting for transfers between devices, block(): lax.all_gather(inner, 'tp', axis=1, tiled=True)  47.1 us
    all_to_all x1, blocking collectives, block(): lax.all_to_all(outgoing, 'seq', split_axis=0, concat_axis=0, tiled=True)  38.1 us
    all_to_all x1, starting transfers between devices, block(): lax.all_to_all(mixed, 'seq', split_axis=0, concat_axis=0, tiled=True)  15.5 us
    dot_general x4, matrix products, dot(): jnp.dot(a, b, precision=TRANSFORM_PRECISION, preferred_element_type=jnp.f...  14.2 us
    all_to_all x1, waiting for transfers between devices, block(): lax.all_to_all(mixed, 'seq', split_axis=0, concat_axis=0, tiled=True)  11.9 us
    unnamed x23, local copies, waits for them, and re-layouts  10.3 us
    ppermute x3, starting transfers between devices, shifted(): return lax.ppermute(value, axis, pairs)  10 us
  transfers between devices with their start and end apart: 6, of which 4 were waited for; matrix products, arithmetic and copies ran while one was open for 2% of the time, Pallas kernels for 0%

profile of v2, /device:TPU:1, one launch (start us, length us, event | category | flops | bytes accessed | tf_op | source)
XLA Modules:
  0.0 303.2 jit_solution(137879276982766816)
XLA Ops:
  6.5 0.7 slice.109
  7.3 0.2 copy.23
  7.5 4.6 %collective-permute-start.1 = (bf16[2,1024]{0,1:T(8,128)(2,1)S(1)}, bf16[2,1024]{0,1:T(8,128)(2,1)S(1)}, u32[]{:S(2)}, u32[]{:S(2)}) collective-permute-start(bf16[2,1024]{0,1:T(8,128)(2,1)S(1)} %copy.23), channel_id=1, source_target_pairs={{0,4},{4,8},{8,12},{12,16},{16,20},{20,24},{24,28},{28,32},{32,36}... | collective-permute-start | bytes 12296 | tf_op jit(solution)/shard_map/ppermute | solution.py:13
  12.1 0.7 slice.115
  12.8 0.2 copy.26
  13.0 1.9 collective-permute-start.2
  14.9 0.9 fusion.19
  15.8 1.2 copy.22
  17.1 1.2 copy.25
  18.3 1.2 copy.28
  19.6 0.0 collective-permute-done.1
  19.6 0.0 collective-permute-done.2
  19.6 0.0 copy-start.5
  19.6 1.9 multiply_convert_fusion
  21.5 0.1 pad_maximum_fusion.1
  21.6 38.1 %all_to_all.10 = bf16[64,32,256]{2,1,0:T(8,128)(2,1)S(1)} all-to-all(bf16[64,32,256]{2,1,0:T(8,128)(2,1)S(1)} %pad_maximum_fusion.1), channel_id=1, replica_groups=mesh['seq'=64,'tp'=4] {'seq'}, dimensions={0} | all-to-all | bytes 2097152 | tf_op jit(solution)/shard_map/all_to_all | solution.py:89
  59.7 0.6 copy.36
  60.4 0.0 copy-done.5
  60.4 2.3 fusion.20
  62.7 0.0 copy-start.3
  62.7 0.0 copy-start.4
  62.7 0.6 fusion.18
  63.3 0.3 copy-done.3
  63.6 0.1 copy-done.4
  63.7 0.0 copy-start.1
  63.7 1.2 fusion.4
  64.9 0.0 copy-done.1
  64.9 7.0 %fusion = f32[128,32,512]{2,0,1:T(8,128)S(1)} fusion(f32[512,512,1]{1,0,2:T(8,128)S(1)} %copy-done.1, f32[128,32,256]{2,0,1:T(8,128)S(1)} %get-tuple-element.6, f32[128,32,256]{2,0,1:T(8,128)S(1)} %get-tuple-element.5), kind=kOutput, calls=%fused_computation | convolution fusion | flops 6444548096 | bytes 17825792 | tf_op jit(solution)/shard_map/dot_general | solution.py:39
  72.0 0.0 copy-start
  72.0 0.8 multiply_subtract_fusion
  72.8 0.4 copy-done
  73.2 3.5 %fusion.6 = f32[128,16,512]{2,0,1:T(8,128)S(1)} fusion(f32[512,512,1]{1,0,2:T(8,128)S(1)} %copy-done, f32[128,16,256]{2,0,1:T(8,128)S(1)} %get-tuple-element.8, f32[128,16,256]{2,0,1:T(8,128)S(1)} %get-tuple-element.7), kind=kOutput, calls=%fused_computation.11 | convolution fusion | flops 3222274048 | bytes 9437184 | tf_op jit(solution)/shard_map/dot_general | solution.py:39
  76.7 0.6 subtract_bitcast_fusion
  77.4 0.4 pad_maximum_fusion
  77.7 2.4 copy.33
  80.2 0.0 copy-start.6
  80.2 3.8 %copy.37 = f32[32,8,16,256]{3,1,2,0:T(8,128)S(1)} copy(f32[32,8,16,256]{3,2,1,0:T(8,128)S(1)} %bitcast.65) | data formatting | bytes 8388608
  84.0 0.0 copy-start.2
  84.0 0.0 copy-start.7
  84.0 0.0 copy-done.6
  84.0 1.4 convolution_convert_fusion
  85.4 1.2 copy.38
  86.5 15.5 %all-to-all-start.1 = ((bf16[64,16,256]{2,1,0:T(8,128)(2,1)}), bf16[64,16,256]{2,1,0:T(8,128)(2,1)S(1)}, u32[]{:S(2)}, u32[]{:S(2)}) async-start(bf16[64,16,256]{2,1,0:T(8,128)(2,1)} %bitcast.33), calls=%async_computation.1 | async-start | bytes 1048576 | tf_op jit(solution)/shard_map/all_to_all | solution.py:91
  102.0 0.0 all-gather.3.cloned.1.call-start
  102.0 0.0 copy-done.2
  102.1 0.2 copy.20
  102.3 3.5 %collective-permute-start = (bf16[2,1024]{0,1:T(8,128)(2,1)S(1)}, bf16[2,1024]{0,1:T(8,128)(2,1)S(1)}, u32[]{:S(2)}, u32[]{:S(2)}) collective-permute-start(bf16[2,1024]{0,1:T(8,128)(2,1)S(1)} %copy.20), channel_id=1, source_target_pairs={{0,4},{4,8},{8,12},{12,16},{16,20},{20,24},{24,28},{28,32},{32,36}... | collective-permute-start | bytes 12296 | tf_op jit(solution)/shard_map/ppermute | solution.py:13
  105.8 0.2 copy.19
  106.0 4.8 %collective-permute-done = bf16[2,1024]{0,1:T(8,128)(2,1)S(1)} collective-permute-done((bf16[2,1024]{0,1:T(8,128)(2,1)S(1)}, bf16[2,1024]{0,1:T(8,128)(2,1)S(1)}, u32[]{:S(2)}, u32[]{:S(2)}) %collective-permute-start) | collective-permute-done | bytes 4128 | tf_op jit(solution)/shard_map/ppermute | solution.py:13
  110.8 11.9 %all-to-all-done.1 = bf16[64,16,256]{2,1,0:T(8,128)(2,1)S(1)} async-done(((bf16[64,16,256]{2,1,0:T(8,128)(2,1)}), bf16[64,16,256]{2,1,0:T(8,128)(2,1)S(1)}, u32[]{:S(2)}, u32[]{:S(2)}) %all-to-all-start.1) | async-done | bytes 524320 | tf_op jit(solution)/shard_map/all_to_all | solution.py:91
  122.7 0.0 copy-done.7
  122.7 1.9 fusion.12
  124.6 0.0 all-gather.3.cloned.1.call-update
  124.6 0.0 all-gather.5.cloned.1.call-start
  124.7 0.7 all-gather.5.cloned.1.call-update
  125.4 47.1 %all-gather.3.cloned.1.call-done = bf16[256,4096]{0,1:T(8,128)(2,1)} async-done(((bf16[256,1024]{0,1:T(8,128)(2,1)}), bf16[256,4096]{0,1:T(8,128)(2,1)}) %all-gather.3.cloned.1.call-update) | async-done | bytes 2097168 | tf_op jit(solution)/shard_map/all_gather | solution.py:97
  172.5 116.6 %all-gather.5.cloned.1.call-done = bf16[4096,1024]{1,0:T(8,128)(2,1)} async-done(((bf16[64,1024]{1,0:T(8,128)(2,1)}), bf16[4096,1024]{1,0:T(8,128)(2,1)}) %all-gather.5.cloned.1.call-update) | async-done | bytes 8388624 | tf_op jit(solution)/shard_map/all_gather | solution.py:80
  289.1 7.2 %convolution_convert_fusion.1 = bf16[256,1024]{1,0:T(8,128)(2,1)} fusion(bf16[256,4096]{0,1:T(8,128)(2,1)} %all-gather.3.cloned.1.call-done, bf16[4096,1024]{1,0:T(8,128)(2,1)} %all-gather.5.cloned.1.call-done), kind=kOutput, calls=%fused_computation.20 | convolution fusion | flops 2147745792 | bytes 11010048 | tf_op jit(solution)/shard_map/dot_general | solution.py:96
  (1 shorter events, 0.0 us)
Async XLA Ops:
  7.5 12.1 %collective-permute-start.1 = (bf16[2,1024]{0,1:T(8,128)(2,1)S(1)}, bf16[2,1024]{0,1:T(8,128)(2,1)S(1)}, u32[]{:S(2)}, u32[]{:S(2)}) collective-permute-start(bf16[2,1024]{0,1:T(8,128)(2,1)S(1)} %copy.23), channel_id=1, source_target_pairs={{0,4},{4,8},{8,12},{12,16},{16,20},{20,24},{24,28},{28,32},{32,36}... | collective-permute-start | bytes 12296 | tf_op jit(solution)/shard_map/ppermute | solution.py:13
  13.0 6.6 %collective-permute-start.2 = (bf16[2,1024]{0,1:T(8,128)(2,1)S(1)}, bf16[2,1024]{0,1:T(8,128)(2,1)S(1)}, u32[]{:S(2)}, u32[]{:S(2)}) collective-permute-start(bf16[2,1024]{0,1:T(8,128)(2,1)S(1)} %copy.26), channel_id=1, source_target_pairs={{0,4},{4,8},{8,12},{12,16},{16,20},{20,24},{24,28},{28,32},{32,36}... | collective-permute-start | bytes 12296 | tf_op jit(solution)/shard_map/ppermute | solution.py:13
  19.6 40.8 %copy-start.5 = (f32[256,64]{1,0:T(8,128)S(1)}, f32[256,64]{1,0:T(8,128)}, u32[]{:S(2)}) copy-start(f32[256,64]{1,0:T(8,128)} %constant.12.clone) | copy-start | bytes 196612
  62.7 0.9 copy-start.3
  62.7 1.0 copy-start.4
  63.7 1.3 copy-start.1
  72.0 1.2 copy-start
  80.2 3.8 %copy-start.6 = (f32[64,256]{1,0:T(8,128)S(1)}, f32[64,256]{1,0:T(8,128)}, u32[]{:S(2)}) copy-start(f32[64,256]{1,0:T(8,128)} %constant.17.clone) | copy-start | bytes 196612
  84.0 18.1 %copy-start.2 = (bf16[256,1024]{1,0:T(8,128)(2,1)S(1)}, bf16[256,1024]{1,0:T(8,128)(2,1)}, u32[]{:S(2)}) copy-start(bf16[256,1024]{1,0:T(8,128)(2,1)} %param.13) | copy-start | bytes 1572868
  84.0 38.7 %copy-start.7 = (f32[1024]{0:T(1024)S(1)}, f32[1024]{0:T(1024)}, u32[]{:S(2)}) copy-start(f32[1024]{0:T(1024)} %param.18) | copy-start | bytes 12292
  86.5 36.2 %all-to-all-start.1 = ((bf16[64,16,256]{2,1,0:T(8,128)(2,1)}), bf16[64,16,256]{2,1,0:T(8,128)(2,1)S(1)}, u32[]{:S(2)}, u32[]{:S(2)}) async-start(bf16[64,16,256]{2,1,0:T(8,128)(2,1)} %bitcast.33), calls=%async_computation.1 | async-start | bytes 1048576 | tf_op jit(solution)/shard_map/all_to_all | solution.py:91
  102.0 70.5 %all-gather.3.cloned.1.call-start = ((), (), s32[]{:S(2)}) async-start(), calls=%async_computation.2 | async-start | bytes 2621440 | tf_op jit(solution)/shard_map/all_gather | solution.py:97
  102.3 8.5 %collective-permute-start = (bf16[2,1024]{0,1:T(8,128)(2,1)S(1)}, bf16[2,1024]{0,1:T(8,128)(2,1)S(1)}, u32[]{:S(2)}, u32[]{:S(2)}) collective-permute-start(bf16[2,1024]{0,1:T(8,128)(2,1)S(1)} %copy.20), channel_id=1, source_target_pairs={{0,4},{4,8},{8,12},{12,16},{16,20},{20,24},{24,28},{28,32},{32,36}... | collective-permute-start | bytes 12296 | tf_op jit(solution)/shard_map/ppermute | solution.py:13
  124.6 164.5 %all-gather.5.cloned.1.call-start = ((), (), s32[]{:S(2)}) async-start(), calls=%async_computation.3 | async-start | bytes 8519680 | tf_op jit(solution)/shard_map/all_gather | solution.py:80
Sparse Core Ops, SparseCore 0:
  124.8 47.7 all-gather.2
  176.1 112.9 all-gather.4

commit v3 on v2

--- a/solution.py
+++ b/solution.py
@@ -72,12 +72,11 @@
     )
 
 
-def block(query_rows, key_rows, value_rows, short_filter, long_filter, skip_gain, out_weight):
+def mixing(query_rows, key_rows, value_rows, short_filter, long_filter, skip_gain):
     tokens_here, channels = query_rows.shape
     groups = lax.axis_size("seq")
     per_device = channels // groups
     tables = make_tables(groups, tokens_here)
-    weights = lax.all_gather(out_weight, "seq", axis=0, tiled=True)
     tails = shifted((query_rows[-2:], key_rows[-2:], value_rows[-2:]), "seq", 1)
     query_mix = causal_short(query_rows, tails[0], short_filter[:, 0, :])
     key_mix = causal_short(key_rows, tails[1], short_filter[:, 1, :])
@@ -90,13 +89,18 @@
     mixed = long_conv(pieces, per_device, tables)
     returned = lax.all_to_all(mixed, "seq", split_axis=0, concat_axis=0, tiled=True)
     conv = returned.reshape(channels, tokens_here).T
-    inner = (query_mix * (conv.astype(jnp.float32) + skip_gain * gated.astype(jnp.float32))).astype(
+    return (query_mix * (conv.astype(jnp.float32) + skip_gain * gated.astype(jnp.float32))).astype(
         jnp.bfloat16
     )
-    total = jnp.dot(
-        lax.all_gather(inner, "tp", axis=1, tiled=True), weights, preferred_element_type=jnp.float32
-    )
-    return total.astype(jnp.bfloat16)
+
+
+def projection(inner, out_weight):
+    halves = lax.all_to_all(out_weight, "core", split_axis=1, concat_axis=0, tiled=True)
+    weights = lax.all_gather(halves, "sq", axis=0, tiled=True)
+    rows = lax.all_gather(inner, "tp", axis=1, tiled=True)
+    rows = lax.all_gather(rows, "core", axis=0, tiled=True)
+    total = jnp.dot(rows, weights, preferred_element_type=jnp.float32).astype(jnp.bfloat16)
+    return lax.all_to_all(total, "core", split_axis=0, concat_axis=1, tiled=True)
 
 
 def solution(mesh):
@@ -109,6 +113,24 @@
         P("tp"),
         P("seq", "tp"),
     )
-    return jax.shard_map(
-        block, mesh=mesh, in_specs=placed, out_specs=P("seq", "tp"), check_vma=False
+    first = jax.shard_map(
+        mixing, mesh=mesh, in_specs=placed[:6], out_specs=P("seq", "tp"), check_vma=False
     )
+    seq, tp = mesh.axis_names
+    cores = 2 if mesh.shape[seq] % 2 == 0 else 1
+    paired = jax.sharding.Mesh(
+        mesh.devices.reshape(mesh.shape[seq] // cores, cores, mesh.shape[tp]), ("sq", "core", "tp")
+    )
+    pair_spec = P(("sq", "core"), "tp")
+    second = jax.shard_map(
+        projection,
+        mesh=paired,
+        in_specs=(pair_spec, pair_spec),
+        out_specs=pair_spec,
+        check_vma=False,
+    )
+
+    def step(*args):
+        return second(first(*args[:6]), args[6])
+
+    return step

time: 304 us -> 321 us (1.056)
  waiting for transfers between devices: 181 us -> 190 us
  blocking collectives: 38.1 us -> 46.7 us
    all_gather x2 -> x3, waiting for transfers between devices: 164 us -> 173 us  [the longest x1 109 us: projection(): weights = lax.all_gather(halves, 'sq', axis=0, tiled=True)]
    all_to_all x1 -> x3, blocking collectives: 38.1 us -> 46.7 us  [the longest x1 38.1 us: mixing(): lax.all_to_all(outgoing, 'seq', split_axis=0, concat_axis=0, tiled=True)]
    unnamed x23 -> x25, local copies, waits for them, and re-layouts: 10.3 us -> 10 us
  transfers between devices with their start and end apart: 6 -> 7, of which waited for: 4 -> 5; matrix products, arithmetic and copies ran while one was open for 2% -> 2% of each run, Pallas kernels for 0% -> 0%
where the time goes in v3:
time: 321 us; the launch traced here: 320 us
  waiting for transfers between devices  190 us (59%)
  blocking collectives  46.7 us (15%)
  starting transfers between devices  25.6 us (8%)
  matrix products  20.4 us (6%)
  local copies, waits for them, and re-layouts  17.2 us (5%)
  between operations  13.4 us (4%)
  other arithmetic  6.97 us (2%)
    all_gather x1, waiting for transfers between devices, projection(): weights = lax.all_gather(halves, 'sq', axis=0, tiled=True)  109 us
    all_gather x1, waiting for transfers between devices, projection(): rows = lax.all_gather(inner, 'tp', axis=1, tiled=True)  43.1 us
    all_to_all x1, blocking collectives, mixing(): lax.all_to_all(outgoing, 'seq', split_axis=0, concat_axis=0, tiled=True)  38.1 us
    all_gather x1, waiting for transfers between devices, projection(): rows = lax.all_gather(rows, 'core', axis=0, tiled=True)  20.6 us
    all_to_all x1, starting transfers between devices, mixing(): lax.all_to_all(mixed, 'seq', split_axis=0, concat_axis=0, tiled=True)  15.4 us
    dot_general x4, matrix products, dot(): jnp.dot(a, b, precision=TRANSFORM_PRECISION, preferred_element_type=jnp.f...  14.6 us
    all_to_all x1, waiting for transfers between devices, mixing(): lax.all_to_all(mixed, 'seq', split_axis=0, concat_axis=0, tiled=True)  11.9 us
    ppermute x3, starting transfers between devices, shifted(): return lax.ppermute(value, axis, pairs)  10 us
  transfers between devices with their start and end apart: 7, of which 5 were waited for; matrix products, arithmetic and copies ran while one was open for 2% of the time, Pallas kernels for 0%

profile of v3, /device:TPU:1, one launch (start us, length us, event | category | flops | bytes accessed | tf_op | source)
XLA Modules:
  0.0 319.9 jit_solution(2433706593347683884)
XLA Ops:
  6.5 0.7 slice.109
  7.3 0.2 copy.59
  7.5 4.6 %collective-permute-start.1 = (bf16[2,1024]{0,1:T(8,128)(2,1)S(1)}, bf16[2,1024]{0,1:T(8,128)(2,1)S(1)}, u32[]{:S(2)}, u32[]{:S(2)}) collective-permute-start(bf16[2,1024]{0,1:T(8,128)(2,1)S(1)} %copy.59), channel_id=1, source_target_pairs={{0,4},{4,8},{8,12},{12,16},{16,20},{20,24},{24,28},{28,32},{32,36}... | collective-permute-start | bytes 12296 | tf_op jit(solution)/shard_map/ppermute | solution.py:13
  12.1 0.7 slice.115
  12.8 0.2 copy.62
  13.0 1.9 collective-permute-start.2
  14.9 0.9 fusion.19
  15.8 1.2 copy.58
  17.1 1.2 copy.61
  18.3 1.2 copy.64
  19.6 0.0 collective-permute-done.1
  19.6 0.0 collective-permute-done.2
  19.6 0.0 copy-start.5
  19.6 1.9 multiply_convert_fusion
  21.5 0.1 pad_maximum_fusion.1
  21.6 38.1 %all_to_all.48 = bf16[64,32,256]{2,1,0:T(8,128)(2,1)S(1)} all-to-all(bf16[64,32,256]{2,1,0:T(8,128)(2,1)S(1)} %pad_maximum_fusion.1), channel_id=1, replica_groups=mesh['sq'=32,'core'=2,'tp'=4] {'sq','core'}, dimensions={0} | all-to-all | bytes 2097152 | tf_op jit(solution)/shard_map/all_to_all | solution.py:88
  59.7 0.6 copy.76
  60.4 0.0 copy-done.5
  60.4 2.3 fusion.20
  62.7 0.0 copy-start.3
  62.7 0.0 copy-start.4
  62.7 0.9 fusion.18
  63.6 0.0 copy-done.3
  63.6 0.0 copy-done.4
  63.7 1.2 fusion.4
  64.9 0.0 copy-done.1
  64.9 7.2 %fusion = f32[128,32,512]{2,0,1:T(8,128)S(1)} fusion(f32[512,512,1]{1,0,2:T(8,128)S(1)} %copy-done.1, f32[128,32,256]{2,0,1:T(8,128)S(1)} %get-tuple-element.7, f32[128,32,256]{2,0,1:T(8,128)S(1)} %get-tuple-element.6), kind=kOutput, calls=%fused_computation | convolution fusion | flops 6444548096 | bytes 17825792 | tf_op jit(solution)/shard_map/dot_general | solution.py:39
  72.1 0.0 copy-start
  72.1 0.8 multiply_subtract_fusion
  72.9 0.4 copy-done
  73.3 3.7 %fusion.6 = f32[128,16,512]{2,0,1:T(8,128)S(1)} fusion(f32[512,512,1]{1,0,2:T(8,128)S(1)} %copy-done, f32[128,16,256]{2,0,1:T(8,128)S(1)} %get-tuple-element.9, f32[128,16,256]{2,0,1:T(8,128)S(1)} %get-tuple-element.8), kind=kOutput, calls=%fused_computation.11 | convolution fusion | flops 3222274048 | bytes 9437184 | tf_op jit(solution)/shard_map/dot_general | solution.py:39
  77.1 0.6 subtract_bitcast_fusion
  77.7 0.4 pad_maximum_fusion
  78.1 2.4 copy.69
  80.5 0.0 copy-start.7
  80.5 3.8 %copy.77 = f32[32,8,16,256]{3,1,2,0:T(8,128)S(1)} copy(f32[32,8,16,256]{3,2,1,0:T(8,128)S(1)} %bitcast.76) | data formatting | bytes 8388608
  84.3 0.0 copy-start.2
  84.3 0.0 copy-start.8
  84.3 0.0 copy-done.7
  84.4 1.4 convolution_convert_fusion
  85.7 0.0 copy-start.6
  85.7 1.2 copy.78
  86.9 15.4 %all-to-all-start.1 = ((bf16[64,16,256]{2,1,0:T(8,128)(2,1)}), bf16[64,16,256]{2,1,0:T(8,128)(2,1)S(1)}, u32[]{:S(2)}, u32[]{:S(2)}) async-start(bf16[64,16,256]{2,1,0:T(8,128)(2,1)} %bitcast.42), calls=%async_computation.1 | async-start | bytes 1048576 | tf_op jit(solution)/shard_map/all_to_all | solution.py:90
  102.3 0.0 all-gather.4.cloned.1.call-start
  102.4 0.0 copy-done.2
  102.4 0.2 copy.56
  102.6 3.5 %collective-permute-start = (bf16[2,1024]{0,1:T(8,128)(2,1)S(1)}, bf16[2,1024]{0,1:T(8,128)(2,1)S(1)}, u32[]{:S(2)}, u32[]{:S(2)}) collective-permute-start(bf16[2,1024]{0,1:T(8,128)(2,1)S(1)} %copy.56), channel_id=1, source_target_pairs={{0,4},{4,8},{8,12},{12,16},{16,20},{20,24},{24,28},{28,32},{32,36}... | collective-permute-start | bytes 12296 | tf_op jit(solution)/shard_map/ppermute | solution.py:13
  106.2 0.2 copy.55
  106.4 4.7 %collective-permute-done = bf16[2,1024]{0,1:T(8,128)(2,1)S(1)} collective-permute-done((bf16[2,1024]{0,1:T(8,128)(2,1)S(1)}, bf16[2,1024]{0,1:T(8,128)(2,1)S(1)}, u32[]{:S(2)}, u32[]{:S(2)}) %collective-permute-start) | collective-permute-done | bytes 4128 | tf_op jit(solution)/shard_map/ppermute | solution.py:13
  111.1 11.9 %all-to-all-done.1 = bf16[64,16,256]{2,1,0:T(8,128)(2,1)S(1)} async-done(((bf16[64,16,256]{2,1,0:T(8,128)(2,1)}), bf16[64,16,256]{2,1,0:T(8,128)(2,1)S(1)}, u32[]{:S(2)}, u32[]{:S(2)}) %all-to-all-start.1) | async-done | bytes 524320 | tf_op jit(solution)/shard_map/all_to_all | solution.py:90
  123.0 0.0 copy-done.8
  123.0 2.0 fusion.12
  125.0 0.0 all-gather.4.cloned.1.call-update
  125.0 0.0 all-gather.8.cloned.1.call-start
  125.1 4.6 %all_to_all.49 = bf16[64,2,512]{2,0,1:T(8,128)(2,1)} all-to-all(bf16[64,2,512]{2,0,1:T(8,128)(2,1)S(1)} %bitcast.87), channel_id=1, replica_groups=mesh['sq'=32,'core'=2,'tp'=4] {'core'}, dimensions={1} | all-to-all | bytes 262144 | tf_op jit(solution)/shard_map/all_to_all | solution.py:98
  129.7 0.0 all-gather.8.cloned.1.call-update
  129.7 0.0 all-gather.6.cloned.1.call-start
  129.8 43.1 %all-gather.4.cloned.1.call-done = bf16[256,4096]{0,1:T(8,128)(2,1)} async-done(((bf16[256,1024]{0,1:T(8,128)(2,1)}), bf16[256,4096]{0,1:T(8,128)(2,1)}) %all-gather.4.cloned.1.call-update) | async-done | bytes 2097168 | tf_op jit(solution)/shard_map/all_gather | solution.py:100
  172.9 0.0 all-gather.6.cloned.1.call-update
  172.9 109.1 %all-gather.8.cloned.1.call-done = bf16[4096,512]{1,0:T(8,128)(2,1)} async-done(((bf16[128,512]{1,0:T(8,128)(2,1)}), bf16[4096,512]{1,0:T(8,128)(2,1)}) %all-gather.8.cloned.1.call-update) | async-done | bytes 4194320 | tf_op jit(solution)/shard_map/all_gather | solution.py:99
  282.0 20.6 %all-gather.6.cloned.1.call-done = bf16[512,4096]{0,1:T(8,128)(2,1)} async-done(((bf16[256,4096]{0,1:T(8,128)(2,1)}), bf16[512,4096]{0,1:T(8,128)(2,1)}) %all-gather.6.cloned.1.call-update) | async-done | bytes 4194320 | tf_op jit(solution)/shard_map/all_gather | solution.py:101
  302.6 5.8 %convolution_convert_fusion.1 = bf16[512,512]{1,0:T(8,128)(2,1)S(1)} fusion(bf16[512,4096]{0,1:T(8,128)(2,1)} %all-gather.6.cloned.1.call-done, bf16[4096,512]{1,0:T(8,128)(2,1)} %all-gather.8.cloned.1.call-done), kind=kOutput, calls=%fused_computation.20 | convolution fusion | flops 2147745792 | bytes 8912896 | tf_op jit(solution)/shard_map/dot_general | solution.py:102
  308.4 4.0 %all_to_all.50 = bf16[2,256,512]{2,1,0:T(8,128)(2,1)S(1)} all-to-all(bf16[2,256,512]{2,1,0:T(8,128)(2,1)S(1)} %bitcast.85), channel_id=1, replica_groups=mesh['sq'=32,'core'=2,'tp'=4] {'core'}, dimensions={0} | all-to-all | bytes 1048576 | tf_op jit(solution)/shard_map/all_to_all | solution.py:103
  312.5 0.9 copy.75
  (4 shorter events, 0.0 us)
Async XLA Ops:
  7.5 12.1 %collective-permute-start.1 = (bf16[2,1024]{0,1:T(8,128)(2,1)S(1)}, bf16[2,1024]{0,1:T(8,128)(2,1)S(1)}, u32[]{:S(2)}, u32[]{:S(2)}) collective-permute-start(bf16[2,1024]{0,1:T(8,128)(2,1)S(1)} %copy.59), channel_id=1, source_target_pairs={{0,4},{4,8},{8,12},{12,16},{16,20},{20,24},{24,28},{28,32},{32,36}... | collective-permute-start | bytes 12296 | tf_op jit(solution)/shard_map/ppermute | solution.py:13
  13.0 6.6 %collective-permute-start.2 = (bf16[2,1024]{0,1:T(8,128)(2,1)S(1)}, bf16[2,1024]{0,1:T(8,128)(2,1)S(1)}, u32[]{:S(2)}, u32[]{:S(2)}) collective-permute-start(bf16[2,1024]{0,1:T(8,128)(2,1)S(1)} %copy.62), channel_id=1, source_target_pairs={{0,4},{4,8},{8,12},{12,16},{16,20},{20,24},{24,28},{28,32},{32,36}... | collective-permute-start | bytes 12296 | tf_op jit(solution)/shard_map/ppermute | solution.py:13
  19.6 40.8 %copy-start.5 = (f32[256,64]{1,0:T(8,128)S(1)}, f32[256,64]{1,0:T(8,128)}, u32[]{:S(2)}) copy-start(f32[256,64]{1,0:T(8,128)} %constant.12.clone) | copy-start | bytes 196612
  62.7 0.9 copy-start.3
  62.7 1.0 copy-start.4
  63.7 1.3 copy-start.1
  72.1 1.2 copy-start
  80.5 3.8 %copy-start.7 = (f32[64,256]{1,0:T(8,128)S(1)}, f32[64,256]{1,0:T(8,128)}, u32[]{:S(2)}) copy-start(f32[64,256]{1,0:T(8,128)} %constant.17.clone) | copy-start | bytes 196612
  84.3 18.1 %copy-start.2 = (bf16[256,1024]{1,0:T(8,128)(2,1)S(1)}, bf16[256,1024]{1,0:T(8,128)(2,1)}, u32[]{:S(2)}) copy-start(bf16[256,1024]{1,0:T(8,128)(2,1)} %param.14) | copy-start | bytes 1572868
  84.3 38.7 %copy-start.8 = (f32[1024]{0:T(1024)S(1)}, f32[1024]{0:T(1024)}, u32[]{:S(2)}) copy-start(f32[1024]{0:T(1024)} %param.19) | copy-start | bytes 12292
  85.7 39.4 %copy-start.6 = (bf16[64,1024]{1,0:T(8,128)(2,1)S(1)}, bf16[64,1024]{1,0:T(8,128)(2,1)}, u32[]{:S(2)}) copy-start(bf16[64,1024]{1,0:T(8,128)(2,1)} %param.20) | copy-start | bytes 393220
  86.9 36.1 %all-to-all-start.1 = ((bf16[64,16,256]{2,1,0:T(8,128)(2,1)}), bf16[64,16,256]{2,1,0:T(8,128)(2,1)S(1)}, u32[]{:S(2)}, u32[]{:S(2)}) async-start(bf16[64,16,256]{2,1,0:T(8,128)(2,1)} %bitcast.42), calls=%async_computation.1 | async-start | bytes 1048576 | tf_op jit(solution)/shard_map/all_to_all | solution.py:90
  102.3 70.6 %all-gather.4.cloned.1.call-start = ((), (), s32[]{:S(2)}) async-start(), calls=%async_computation.4 | async-start | bytes 2621440 | tf_op jit(solution)/shard_map/all_gather | solution.py:100
  102.6 8.5 %collective-permute-start = (bf16[2,1024]{0,1:T(8,128)(2,1)S(1)}, bf16[2,1024]{0,1:T(8,128)(2,1)S(1)}, u32[]{:S(2)}, u32[]{:S(2)}) collective-permute-start(bf16[2,1024]{0,1:T(8,128)(2,1)S(1)} %copy.56), channel_id=1, source_target_pairs={{0,4},{4,8},{8,12},{12,16},{16,20},{20,24},{24,28},{28,32},{32,36}... | collective-permute-start | bytes 12296 | tf_op jit(solution)/shard_map/ppermute | solution.py:13
  125.0 157.0 %all-gather.8.cloned.1.call-start = ((), (), s32[]{:S(2)}) async-start(), calls=%async_computation.6 | async-start | bytes 4325376 | tf_op jit(solution)/shard_map/all_gather | solution.py:99
  129.7 172.9 %all-gather.6.cloned.1.call-start = ((), (), s32[]{:S(2)}) async-start(), calls=%async_computation.5 | async-start | bytes 6291456 | tf_op jit(solution)/shard_map/all_gather | solution.py:101
Sparse Core Ops, SparseCore 0:
  125.1 47.7 all-gather.3
  176.4 105.5 all-gather.7
  283.8 18.7 all-gather.5

commit v4 on v2

--- a/solution.py
+++ b/solution.py
@@ -93,10 +93,24 @@
     inner = (query_mix * (conv.astype(jnp.float32) + skip_gain * gated.astype(jnp.float32))).astype(
         jnp.bfloat16
     )
-    total = jnp.dot(
-        lax.all_gather(inner, "tp", axis=1, tiled=True), weights, preferred_element_type=jnp.float32
-    )
-    return total.astype(jnp.bfloat16)
+    return projection(inner, weights).astype(jnp.bfloat16)
+
+
+def projection(inner, weights):
+    size = lax.axis_size("tp")
+    here = lax.axis_index("tp")
+    width = inner.shape[1]
+
+    def rows_of(source):
+        return lax.dynamic_slice_in_dim(weights, source * width, width, 0)
+
+    arrived = [
+        lax.ppermute(inner, "tp", [(j, (j + k) % size) for j in range(size)]) for k in range(1, size)
+    ]
+    total = jnp.dot(inner, rows_of(here), preferred_element_type=jnp.float32)
+    for k, chunk in enumerate(arrived, 1):
+        total = total + jnp.dot(chunk, rows_of((here - k) % size), preferred_element_type=jnp.float32)
+    return total
 
 
 def solution(mesh):
@@ -109,6 +123,4 @@
         P("tp"),
         P("seq", "tp"),
     )
-    return jax.shard_map(
-        block, mesh=mesh, in_specs=placed, out_specs=P("seq", "tp"), check_vma=False
-    )
+    return jax.shard_map(block, mesh=mesh, in_specs=placed, out_specs=P("seq", "tp"), check_vma=False)

time: 304 us -> 201 us (0.66)
  the two profiles are of different devices: /device:TPU:1 before, /device:TPU:33 now
where the time goes in v4:
time: 201 us
  waiting for transfers between devices  66.4 us (33%)
  blocking collectives  52.5 us (26%)
  matrix products  24.4 us (12%)
  starting transfers between devices  20.8 us (10%)
  local copies, waits for them, and re-layouts  16.3 us (8%)
  between operations  13.8 us (7%)
  other arithmetic  6.28 us (3%)
    all_to_all x1, blocking collectives, block(): lax.all_to_all(outgoing, 'seq', split_axis=0, concat_axis=0, tiled=True)  52.5 us
    ppermute x3, waiting for transfers between devices, projection(): lax.ppermute(inner, 'tp', [(j, (j + k) % size) for j in range(size)])  31.3 us
    all_to_all x1, waiting for transfers between devices, block(): lax.all_to_all(mixed, 'seq', split_axis=0, concat_axis=0, tiled=True)  24.2 us
    dot_general x4, matrix products, dot(): jnp.dot(a, b, precision=TRANSFORM_PRECISION, preferred_element_type=jnp.f...  14.3 us
    unnamed x23, local copies, waits for them, and re-layouts  10 us
    ppermute x3, starting transfers between devices, shifted(): return lax.ppermute(value, axis, pairs)  9.23 us
    dot_general x3, matrix products, projection(): jnp.dot(chunk, rows_of((here - k) % size), preferred_element_type=jnp.flo...  7.75 us
    ppermute x3, starting transfers between devices, projection(): lax.ppermute(inner, 'tp', [(j, (j + k) % size) for j in range(size)])  6.48 us
  transfers between devices with their start and end apart: 8, of which 5 were waited for; matrix products, arithmetic and copies ran while one was open for 22% of the time, Pallas kernels for 0%

profile of v4, /device:TPU:33, one launch (start us, length us, event | category | flops | bytes accessed | tf_op | source)
XLA Modules:
  0.0 200.5 jit_solution(3604731572285190383)
XLA Ops:
  6.5 0.0 all-gather.2.cloned.1.call-start
  6.5 0.7 all-gather.2.cloned.1.call-update
  7.3 0.7 slice.109
  8.0 0.2 copy.23
  8.2 3.8 %collective-permute-start.1 = (bf16[2,1024]{0,1:T(8,128)(2,1)S(1)}, bf16[2,1024]{0,1:T(8,128)(2,1)S(1)}, u32[]{:S(2)}, u32[]{:S(2)}) collective-permute-start(bf16[2,1024]{0,1:T(8,128)(2,1)S(1)} %copy.23), channel_id=1, source_target_pairs={{0,4},{4,8},{8,12},{12,16},{16,20},{20,24},{24,28},{28,32},{32,36}... | collective-permute-start | bytes 12296 | tf_op jit(solution)/shard_map/ppermute | solution.py:13
  12.0 0.7 slice.115
  12.7 0.2 copy.26
  12.9 1.9 collective-permute-start.2
  14.8 0.9 fusion.43
  15.8 1.2 copy.22
  17.0 1.2 copy.25
  18.3 1.2 copy.28
  19.5 0.0 collective-permute-done.1
  19.5 0.0 collective-permute-done.2
  19.5 0.0 copy-start.5
  19.5 1.9 multiply_convert_fusion
  21.4 0.1 pad_maximum_fusion.1
  21.6 52.5 %all_to_all.10 = bf16[64,32,256]{2,1,0:T(8,128)(2,1)S(1)} all-to-all(bf16[64,32,256]{2,1,0:T(8,128)(2,1)S(1)} %pad_maximum_fusion.1), channel_id=1, replica_groups=mesh['seq'=64,'tp'=4] {'seq'}, dimensions={0} | all-to-all | bytes 2097152 | tf_op jit(solution)/shard_map/all_to_all | solution.py:89
  74.1 0.6 copy.36
  74.7 0.0 copy-done.5
  74.8 2.3 %fusion.44 = f32[256,8192]{1,0:T(8,128)S(1)} fusion(f32[256,64]{1,0:T(8,128)S(1)} %copy-done.5, bf16[64,8192]{1,0:T(8,128)(2,1)S(1)} %bitcast.71), kind=kOutput, calls=%fused_computation.58 | convolution fusion | flops 805306368 | bytes 9502720 | tf_op jit(solution)/shard_map/dot_general | solution.py:39
  77.1 0.0 copy-start.3
  77.1 0.0 copy-start.4
  77.1 0.9 fusion.42
  78.0 0.0 copy-done.3
  78.0 0.0 copy-done.4
  78.1 0.0 copy-start.1
  78.1 1.2 fusion.4
  79.3 0.0 copy-done.1
  79.3 7.2 %fusion = f32[128,32,512]{2,0,1:T(8,128)S(1)} fusion(f32[512,512,1]{1,0,2:T(8,128)S(1)} %copy-done.1, f32[128,32,256]{2,0,1:T(8,128)S(1)} %get-tuple-element.6, f32[128,32,256]{2,0,1:T(8,128)S(1)} %get-tuple-element.5), kind=kOutput, calls=%fused_computation | convolution fusion | flops 6444548096 | bytes 17825792 | tf_op jit(solution)/shard_map/dot_general | solution.py:39
  86.5 0.0 copy-start
  86.5 0.8 multiply_subtract_fusion
  87.3 0.4 copy-done
  87.7 3.5 %fusion.6 = f32[128,16,512]{2,0,1:T(8,128)S(1)} fusion(f32[512,512,1]{1,0,2:T(8,128)S(1)} %copy-done, f32[128,16,256]{2,0,1:T(8,128)S(1)} %get-tuple-element.8, f32[128,16,256]{2,0,1:T(8,128)S(1)} %get-tuple-element.7), kind=kOutput, calls=%fused_computation.11 | convolution fusion | flops 3222274048 | bytes 9437184 | tf_op jit(solution)/shard_map/dot_general | solution.py:39
  91.2 0.6 subtract_bitcast_fusion
  91.9 0.4 pad_maximum_fusion
  92.2 2.4 %copy.33 = f32[2,128,16,256]{3,2,1,0:T(8,128)S(1)} copy(f32[2,128,16,256]{3,1,2,0:T(8,128)S(1)} %pad_maximum_fusion) | data formatting | bytes 8388608 | tf_op jit(solution)/shard_map/stack | solution.py:61
  94.7 0.0 copy-start.6
  94.7 3.8 %copy.37 = f32[32,8,16,256]{3,1,2,0:T(8,128)S(1)} copy(f32[32,8,16,256]{3,2,1,0:T(8,128)S(1)} %bitcast.67) | data formatting | bytes 8388608
  98.5 0.0 copy-start.2
  98.5 0.0 copy-start.7
  98.5 0.0 copy-done.6
  98.5 1.3 convolution_convert_fusion
  99.9 1.2 copy.38
  101.0 5.1 %all-to-all-start.1 = ((bf16[64,16,256]{2,1,0:T(8,128)(2,1)}), bf16[64,16,256]{2,1,0:T(8,128)(2,1)S(1)}, u32[]{:S(2)}, u32[]{:S(2)}) async-start(bf16[64,16,256]{2,1,0:T(8,128)(2,1)} %bitcast.33), calls=%async_computation.1 | async-start | bytes 1048576 | tf_op jit(solution)/shard_map/all_to_all | solution.py:91
  106.1 0.0 copy-done.2
  106.1 0.2 copy.20
  106.4 3.5 %collective-permute-start = (bf16[2,1024]{0,1:T(8,128)(2,1)S(1)}, bf16[2,1024]{0,1:T(8,128)(2,1)S(1)}, u32[]{:S(2)}, u32[]{:S(2)}) collective-permute-start(bf16[2,1024]{0,1:T(8,128)(2,1)S(1)} %copy.20), channel_id=1, source_target_pairs={{0,4},{4,8},{8,12},{12,16},{16,20},{20,24},{24,28},{28,32},{32,36}... | collective-permute-start | bytes 12296 | tf_op jit(solution)/shard_map/ppermute | solution.py:13
  109.9 0.2 copy.19
  110.1 4.1 %collective-permute-done = bf16[2,1024]{0,1:T(8,128)(2,1)S(1)} collective-permute-done((bf16[2,1024]{0,1:T(8,128)(2,1)S(1)}, bf16[2,1024]{0,1:T(8,128)(2,1)S(1)}, u32[]{:S(2)}, u32[]{:S(2)}) %collective-permute-start) | collective-permute-done | bytes 4128 | tf_op jit(solution)/shard_map/ppermute | solution.py:13
  114.2 24.2 %all-to-all-done.1 = bf16[64,16,256]{2,1,0:T(8,128)(2,1)S(1)} async-done(((bf16[64,16,256]{2,1,0:T(8,128)(2,1)}), bf16[64,16,256]{2,1,0:T(8,128)(2,1)S(1)}, u32[]{:S(2)}, u32[]{:S(2)}) %all-to-all-start.1) | async-done | bytes 524320 | tf_op jit(solution)/shard_map/all_to_all | solution.py:91
  138.4 0.0 copy-done.7
  138.4 1.3 fusion.32
  139.6 0.1 collective-permute-start.4
  139.8 5.4 %collective-permute-start.5 = (bf16[256,1024]{0,1:T(8,128)(2,1)S(1)}, bf16[256,1024]{0,1:T(8,128)(2,1)S(1)}, u32[]{:S(2)}, u32[]{:S(2)}) collective-permute-start(bf16[256,1024]{0,1:T(8,128)(2,1)S(1)} %fusion.32), channel_id=1, source_target_pairs={{0,3},{1,0},{2,1},{3,2},{4,7},{5,4},{6,5},{7,6},{8,11},{9,8},{10,9... | collective-permute-start | bytes 1572872 | tf_op jit(solution)/shard_map/ppermute | solution.py:108
  145.2 1.0 collective-permute-start.3
  146.2 6.1 %all-gather.2.cloned.1.call-done = bf16[4096,1024]{1,0:T(8,128)(2,1)} async-done(((bf16[64,1024]{1,0:T(8,128)(2,1)}), bf16[4096,1024]{1,0:T(8,128)(2,1)}) %all-gather.2.cloned.1.call-update) | async-done | bytes 8388624 | tf_op jit(solution)/shard_map/all_gather | solution.py:80
  152.3 2.3 %fusion.16 = f32[256,1024]{1,0:T(8,128)S(1)} fusion(bf16[256,1024]{0,1:T(8,128)(2,1)S(1)} %fusion.32, bf16[4096,1024]{1,0:T(8,128)(2,1)} %all-gather.2.cloned.1.call-done, s32[]{:T(128)S(6)} %select_n.27), kind=kOutput, calls=%fused_computation.22 | convolution fusion | flops 536870912 | bytes 3670020 | tf_op jit(solution)/shard_map/dot_general | solution.py:110
  154.6 18.5 %collective-permute-done.4 = bf16[256,1024]{0,1:T(8,128)(2,1)S(1)} collective-permute-done((bf16[256,1024]{0,1:T(8,128)(2,1)S(1)}, bf16[256,1024]{0,1:T(8,128)(2,1)S(1)}, u32[]{:S(2)}, u32[]{:S(2)}) %collective-permute-start.4) | collective-permute-done | bytes 524320 | tf_op jit(solution)/shard_map/ppermute | solution.py:108
  173.1 2.3 %fusion.12 = f32[256,1024]{1,0:T(8,128)S(1)} fusion(bf16[256,1024]{0,1:T(8,128)(2,1)S(1)} %collective-permute-done.4, bf16[4096,1024]{1,0:T(8,128)(2,1)} %all-gather.2.cloned.1.call-done, s32[]{:T(128)S(6)} %select_n.31), kind=kOutput, calls=%fused_computation.18 | convolution fusion | flops 536870912 | bytes 3670020 | tf_op jit(solution)/shard_map/dot_general | solution.py:112
  175.4 12.8 %collective-permute-done.5 = bf16[256,1024]{0,1:T(8,128)(2,1)S(1)} collective-permute-done((bf16[256,1024]{0,1:T(8,128)(2,1)S(1)}, bf16[256,1024]{0,1:T(8,128)(2,1)S(1)}, u32[]{:S(2)}, u32[]{:S(2)}) %collective-permute-start.5) | collective-permute-done | bytes 524320 | tf_op jit(solution)/shard_map/ppermute | solution.py:108
  188.2 2.3 %fusion.10 = f32[256,1024]{1,0:T(8,128)S(1)} fusion(bf16[256,1024]{0,1:T(8,128)(2,1)S(1)} %collective-permute-done.5, bf16[4096,1024]{1,0:T(8,128)(2,1)} %all-gather.2.cloned.1.call-done, s32[]{:T(128)S(6)} %select_n.33), kind=kOutput, calls=%fused_computation.16 | convolution fusion | flops 536870912 | bytes 3670020 | tf_op jit(solution)/shard_map/dot_general | solution.py:112
  190.5 0.0 collective-permute-done.3
  190.5 3.1 %fusion.27 = bf16[256,1024]{1,0:T(8,128)(2,1)} fusion(f32[256,1024]{1,0:T(8,128)S(1)} %fusion.10, f32[256,1024]{1,0:T(8,128)S(1)} %fusion.12, f32[256,1024]{1,0:T(8,128)S(1)} %fusion.16, bf16[256,1024]{0,1:T(8,128)(2,1)S(1)} %collective-permute-done.3, bf16[4096,1024]{1,0:T(8,128)(2,1)} %all-gather.2.cloned.1.call-done, s32[]{:T(128)S(6)} %select_n.29), kind=kOutput, calls=%fused_computation.31 | convolution fusion | flops 537919488 | bytes 6291460 | tf_op jit(solution)/shard_map/dot_general | solution.py:112
  (1 shorter events, 0.0 us)
Async XLA Ops:
  6.5 145.7 %all-gather.2.cloned.1.call-start = ((), (), s32[]{:S(2)}) async-start(), calls=%async_computation.2 | async-start | bytes 8519680 | tf_op jit(solution)/shard_map/all_gather | solution.py:80
  8.2 11.3 %collective-permute-start.1 = (bf16[2,1024]{0,1:T(8,128)(2,1)S(1)}, bf16[2,1024]{0,1:T(8,128)(2,1)S(1)}, u32[]{:S(2)}, u32[]{:S(2)}) collective-permute-start(bf16[2,1024]{0,1:T(8,128)(2,1)S(1)} %copy.23), channel_id=1, source_target_pairs={{0,4},{4,8},{8,12},{12,16},{16,20},{20,24},{24,28},{28,32},{32,36}... | collective-permute-start | bytes 12296 | tf_op jit(solution)/shard_map/ppermute | solution.py:13
  12.9 6.6 %collective-permute-start.2 = (bf16[2,1024]{0,1:T(8,128)(2,1)S(1)}, bf16[2,1024]{0,1:T(8,128)(2,1)S(1)}, u32[]{:S(2)}, u32[]{:S(2)}) collective-permute-start(bf16[2,1024]{0,1:T(8,128)(2,1)S(1)} %copy.26), channel_id=1, source_target_pairs={{0,4},{4,8},{8,12},{12,16},{16,20},{20,24},{24,28},{28,32},{32,36}... | collective-permute-start | bytes 12296 | tf_op jit(solution)/shard_map/ppermute | solution.py:13
  19.5 55.2 %copy-start.5 = (f32[256,64]{1,0:T(8,128)S(1)}, f32[256,64]{1,0:T(8,128)}, u32[]{:S(2)}) copy-start(f32[256,64]{1,0:T(8,128)} %constant.51.clone) | copy-start | bytes 196612
  77.1 0.9 copy-start.3
  77.1 1.0 copy-start.4
  78.1 1.3 copy-start.1
  86.5 1.2 copy-start
  94.7 3.8 %copy-start.6 = (f32[64,256]{1,0:T(8,128)S(1)}, f32[64,256]{1,0:T(8,128)}, u32[]{:S(2)}) copy-start(f32[64,256]{1,0:T(8,128)} %constant.56.clone) | copy-start | bytes 196612
  98.5 7.6 %copy-start.2 = (bf16[256,1024]{1,0:T(8,128)(2,1)S(1)}, bf16[256,1024]{1,0:T(8,128)(2,1)}, u32[]{:S(2)}) copy-start(bf16[256,1024]{1,0:T(8,128)(2,1)} %param.13) | copy-start | bytes 1572868
  98.5 39.9 %copy-start.7 = (f32[1024]{0:T(1024)S(1)}, f32[1024]{0:T(1024)}, u32[]{:S(2)}) copy-start(f32[1024]{0:T(1024)} %param.18) | copy-start | bytes 12292
  101.0 37.3 %all-to-all-start.1 = ((bf16[64,16,256]{2,1,0:T(8,128)(2,1)}), bf16[64,16,256]{2,1,0:T(8,128)(2,1)S(1)}, u32[]{:S(2)}, u32[]{:S(2)}) async-start(bf16[64,16,256]{2,1,0:T(8,128)(2,1)} %bitcast.33), calls=%async_computation.1 | async-start | bytes 1048576 | tf_op jit(solution)/shard_map/all_to_all | solution.py:91
  106.4 7.8 %collective-permute-start = (bf16[2,1024]{0,1:T(8,128)(2,1)S(1)}, bf16[2,1024]{0,1:T(8,128)(2,1)S(1)}, u32[]{:S(2)}, u32[]{:S(2)}) collective-permute-start(bf16[2,1024]{0,1:T(8,128)(2,1)S(1)} %copy.20), channel_id=1, source_target_pairs={{0,4},{4,8},{8,12},{12,16},{16,20},{20,24},{24,28},{28,32},{32,36}... | collective-permute-start | bytes 12296 | tf_op jit(solution)/shard_map/ppermute | solution.py:13
  139.6 33.5 %collective-permute-start.4 = (bf16[256,1024]{0,1:T(8,128)(2,1)S(1)}, bf16[256,1024]{0,1:T(8,128)(2,1)S(1)}, u32[]{:S(2)}, u32[]{:S(2)}) collective-permute-start(bf16[256,1024]{0,1:T(8,128)(2,1)S(1)} %fusion.32), channel_id=1, source_target_pairs={{0,2},{1,3},{2,0},{3,1},{4,6},{5,7},{6,4},{7,5},{8,10},{9,11},{10,... | collective-permute-start | bytes 1572872 | tf_op jit(solution)/shard_map/ppermute | solution.py:108
  139.8 48.4 %collective-permute-start.5 = (bf16[256,1024]{0,1:T(8,128)(2,1)S(1)}, bf16[256,1024]{0,1:T(8,128)(2,1)S(1)}, u32[]{:S(2)}, u32[]{:S(2)}) collective-permute-start(bf16[256,1024]{0,1:T(8,128)(2,1)S(1)} %fusion.32), channel_id=1, source_target_pairs={{0,3},{1,0},{2,1},{3,2},{4,7},{5,4},{6,5},{7,6},{8,11},{9,8},{10,9... | collective-permute-start | bytes 1572872 | tf_op jit(solution)/shard_map/ppermute | solution.py:108
  145.2 45.4 %collective-permute-start.3 = (bf16[256,1024]{0,1:T(8,128)(2,1)S(1)}, bf16[256,1024]{0,1:T(8,128)(2,1)S(1)}, u32[]{:S(2)}, u32[]{:S(2)}) collective-permute-start(bf16[256,1024]{0,1:T(8,128)(2,1)S(1)} %fusion.32), channel_id=1, source_target_pairs={{0,1},{1,2},{2,3},{3,0},{4,5},{5,6},{6,7},{7,4},{8,9},{9,10},{10,1... | collective-permute-start | bytes 1572872 | tf_op jit(solution)/shard_map/ppermute | solution.py:108
Sparse Core Ops, SparseCore 0:
  10.9 141.3 all-gather.1

commit v5 on v4

--- a/solution.py
+++ b/solution.py
@@ -4,7 +4,7 @@
 from jax import lax
 from jax.sharding import PartitionSpec as P
 
-TRANSFORM_PRECISION = lax.Precision.HIGH
+TRANSFORM_PRECISION = lax.Precision.DEFAULT
 
 
 def shifted(value, axis, by):
@@ -30,9 +30,11 @@
     forward = np.block([[b_cos, -b_sin], [b_sin, b_cos]])
     backward = np.block([[b_cos, b_sin], [-b_sin, b_cos]])
     last = 2.0 * np.pi * ((n1[:, None] * k1[None, :]) % outer) / outer
-    last_table = np.concatenate([np.cos(last), -np.sin(last)], 1) / period
+    last_cos = np.cos(last) / period
+    last_sin = -np.sin(last) / period
     as32 = lambda a: jnp.asarray(a, jnp.float32)
-    return tuple(as32(a) for a in (first_table, twist_cos, twist_sin, forward, backward, last_table))
+    tables = (first_table, twist_cos, twist_sin, forward, backward, last_cos, last_sin)
+    return tuple(as32(a) for a in tables)
 
 
 def dot(a, b):
@@ -40,7 +42,7 @@
 
 
 def long_conv(pieces, per_device, tables):
-    first_table, twist_cos, twist_sin, forward, backward, last_table = tables
+    first_table, twist_cos, twist_sin, forward, backward, last_cos, last_sin = tables
     blocks, both, tokens = pieces.shape
     outer = 2 * blocks
     spec = dot(first_table, pieces.reshape(blocks, both * tokens)).reshape(2, outer, both, tokens)
@@ -58,8 +60,8 @@
     q_real, q_imag = q[..., :tokens], q[..., tokens:]
     r_real = q_real * twist_cos - q_imag * twist_sin
     r_imag = q_real * twist_sin + q_imag * twist_cos
-    stacked = jnp.stack([r_real, r_imag], 0).reshape(2 * outer, per_device * tokens)
-    result = dot(last_table, stacked)
+    flat = (outer, per_device * tokens)
+    result = dot(last_cos, r_real.reshape(flat)) + dot(last_sin, r_imag.reshape(flat))
     return result.reshape(blocks, per_device, tokens).astype(jnp.bfloat16)
 
 
@@ -78,15 +80,16 @@
     per_device = channels // groups
     tables = make_tables(groups, tokens_here)
     weights = lax.all_gather(out_weight, "seq", axis=0, tiled=True)
+    filter_cols = long_filter.T.reshape(groups, per_device, tokens_here)
+    filter_piece = lax.all_to_all(filter_cols, "seq", split_axis=0, concat_axis=0, tiled=True)
     tails = shifted((query_rows[-2:], key_rows[-2:], value_rows[-2:]), "seq", 1)
     query_mix = causal_short(query_rows, tails[0], short_filter[:, 0, :])
     key_mix = causal_short(key_rows, tails[1], short_filter[:, 1, :])
     value_mix = causal_short(value_rows, tails[2], short_filter[:, 2, :])
     gated = (key_mix * value_mix).astype(jnp.bfloat16)
     gated_cols = gated.T.reshape(groups, per_device, tokens_here)
-    filter_cols = long_filter.T.reshape(groups, per_device, tokens_here)
-    outgoing = jnp.concatenate([gated_cols, filter_cols], 1)
-    pieces = lax.all_to_all(outgoing, "seq", split_axis=0, concat_axis=0, tiled=True)
+    gated_piece = lax.all_to_all(gated_cols, "seq", split_axis=0, concat_axis=0, tiled=True)
+    pieces = jnp.concatenate([gated_piece, filter_piece], 1)
     mixed = long_conv(pieces, per_device, tables)
     returned = lax.all_to_all(mixed, "seq", split_axis=0, concat_axis=0, tiled=True)
     conv = returned.reshape(channels, tokens_here).T
@@ -123,4 +126,6 @@
         P("tp"),
         P("seq", "tp"),
     )
-    return jax.shard_map(block, mesh=mesh, in_specs=placed, out_specs=P("seq", "tp"), check_vma=False)
+    return jax.shard_map(
+        block, mesh=mesh, in_specs=placed, out_specs=P("seq", "tp"), check_vma=False
+    )

time: 201 us -> 198 us (0.985)
  the two profiles are of different devices: /device:TPU:33 before, /device:TPU:35 now
where the time goes in v5:
time: 198 us; the launch traced here: 197 us
  waiting for transfers between devices  76.9 us (39%)
  blocking collectives  36 us (18%)
  starting transfers between devices  35.9 us (18%)
  matrix products  17.1 us (9%)
  between operations  13.8 us (7%)
  local copies, waits for them, and re-layouts  11.4 us (6%)
  other arithmetic  5.84 us (3%)
    all_to_all x1, blocking collectives, block(): lax.all_to_all(gated_cols, 'seq', split_axis=0, concat_axis=0, tiled=True)  36 us
    ppermute x3, waiting for transfers between devices, projection(): lax.ppermute(inner, 'tp', [(j, (j + k) % size) for j in range(size)])  32.7 us
    all_to_all x1, waiting for transfers between devices, block(): lax.all_to_all(mixed, 'seq', split_axis=0, concat_axis=0, tiled=True)  24.7 us
    all_to_all x1, starting transfers between devices, block(): lax.all_to_all(filter_cols, 'seq', split_axis=0, concat_axis=0, tiled=True)  14 us
    all_to_all x1, waiting for transfers between devices, block(): lax.all_to_all(filter_cols, 'seq', split_axis=0, concat_axis=0, tiled=True)  8.92 us
    ppermute x3, starting transfers between devices, shifted(): return lax.ppermute(value, axis, pairs)  8.77 us
    dot_general x3, matrix products, projection(): jnp.dot(chunk, rows_of((here - k) % size), preferred_element_type=jnp.flo...  7.75 us
    dot_general x5, matrix products, dot(): jnp.dot(a, b, precision=TRANSFORM_PRECISION, preferred_element_type=jnp.f...  7.05 us
  transfers between devices with their start and end apart: 9, of which 7 were waited for; matrix products, arithmetic and copies ran while one was open for 16% of the time, Pallas kernels for 0%

profile of v5, /device:TPU:35, one launch (start us, length us, event | category | flops | bytes accessed | tf_op | source)
XLA Modules:
  0.0 197.0 jit_solution(3223291378387994171)
XLA Ops:
  6.5 0.0 all-gather.2.cloned.1.call-start
  6.5 0.7 all-gather.2.cloned.1.call-update
  7.3 2.0 %copy.29 = bf16[256,1024]{0,1:T(8,128)(2,1)} copy(bf16[256,1024]{1,0:T(8,128)(2,1)} %param.18) | data formatting | bytes 1048576 | tf_op args[4]
  9.3 14.0 %all-to-all-start.1 = ((bf16[64,16,256]{2,1,0:T(8,128)(2,1)}), bf16[64,16,256]{2,1,0:T(8,128)(2,1)S(1)}, u32[]{:S(2)}, u32[]{:S(2)}) async-start(bf16[64,16,256]{2,1,0:T(8,128)(2,1)} %bitcast.12), calls=%async_computation.1 | async-start | bytes 1048576 | tf_op jit(solution)/shard_map/all_to_all | solution.py:84
  23.3 0.7 slice.109
  24.1 0.2 copy.24
  24.3 3.4 %collective-permute-start.1 = (bf16[2,1024]{0,1:T(8,128)(2,1)S(1)}, bf16[2,1024]{0,1:T(8,128)(2,1)S(1)}, u32[]{:S(2)}, u32[]{:S(2)}) collective-permute-start(bf16[2,1024]{0,1:T(8,128)(2,1)S(1)} %copy.24), channel_id=1, source_target_pairs={{0,4},{4,8},{8,12},{12,16},{16,20},{20,24},{24,28},{28,32},{32,36}... | collective-permute-start | bytes 12296 | tf_op jit(solution)/shard_map/ppermute | solution.py:13
  27.7 0.7 slice.115
  28.4 0.2 copy.27
  28.6 2.0 %collective-permute-start.2 = (bf16[2,1024]{0,1:T(8,128)(2,1)S(1)}, bf16[2,1024]{0,1:T(8,128)(2,1)S(1)}, u32[]{:S(2)}, u32[]{:S(2)}) collective-permute-start(bf16[2,1024]{0,1:T(8,128)(2,1)S(1)} %copy.27), channel_id=1, source_target_pairs={{0,4},{4,8},{8,12},{12,16},{16,20},{20,24},{24,28},{28,32},{32,36}... | collective-permute-start | bytes 12296 | tf_op jit(solution)/shard_map/ppermute | solution.py:13
  30.6 0.9 fusion.44
  31.5 1.2 copy.23
  32.8 0.0 copy-done
  32.8 0.0 copy-start.5
  32.8 0.2 copy.26
  33.0 0.0 collective-permute-done.1
  33.0 1.7 collective-permute-done.2
  34.8 1.9 multiply_convert_fusion
  36.6 8.9 %all-to-all-done.1 = bf16[64,16,256]{2,1,0:T(8,128)(2,1)S(1)} async-done(((bf16[64,16,256]{2,1,0:T(8,128)(2,1)}), bf16[64,16,256]{2,1,0:T(8,128)(2,1)S(1)}, u32[]{:S(2)}, u32[]{:S(2)}) %all-to-all-start.1) | async-done | bytes 524320 | tf_op jit(solution)/shard_map/all_to_all | solution.py:84
  45.5 36.0 %all_to_all.15 = bf16[64,16,256]{2,1,0:T(8,128)(2,1)S(1)} all-to-all(bf16[64,16,256]{2,1,0:T(8,128)(2,1)S(1)} %bitcast.65), channel_id=1, replica_groups=mesh['seq'=64,'tp'=4] {'seq'}, dimensions={0} | all-to-all | bytes 1048576 | tf_op jit(solution)/shard_map/all_to_all | solution.py:91
  81.6 0.1 pad_maximum_fusion
  81.7 0.6 copy.38
  82.4 0.0 copy-done.5
  82.4 1.2 fusion.45
  83.6 0.0 copy-start.2
  83.6 0.0 copy-start.3
  83.6 0.9 fusion.43
  84.5 0.0 copy-done.2
  84.5 0.0 copy-done.3
  84.6 1.2 fusion.5
  85.8 0.0 copy-done.9
  85.8 2.4 %fusion = f32[128,32,512]{2,0,1:T(8,128)S(1)} fusion(bf16[512,512,1]{1,0,2:T(8,128)(2,1)S(1)} %copy-done.9, bf16[128,32,256]{2,0,1:T(8,128)(2,1)S(1)} %get-tuple-element.6, bf16[128,32,256]{2,0,1:T(8,128)(2,1)S(1)} %get-tuple-element.5), kind=kOutput, calls=%fused_computation | convolution fusion | flops 2155872256 | bytes 13107200 | tf_op jit(solution)/shard_map/dot_general | solution.py:41
  88.2 0.0 copy-start.4
  88.2 0.8 multiply_subtract_fusion.1
  89.0 0.2 copy-done.4
  89.2 1.3 fusion.7
  90.5 0.0 copy-start.7
  90.5 0.6 multiply_add_fusion
  91.1 0.0 copy-start.6
  91.1 1.4 copy.34
  92.5 0.7 copy.35
  93.1 0.0 copy-start.8
  93.1 0.0 copy-done.7
  93.2 1.7 fusion.46
  94.9 0.5 fusion.4
  95.4 0.9 copy.39
  96.3 6.5 %all-to-all-start.2 = ((bf16[64,16,256]{2,1,0:T(8,128)(2,1)}), bf16[64,16,256]{2,1,0:T(8,128)(2,1)S(1)}, u32[]{:S(2)}, u32[]{:S(2)}) async-start(bf16[64,16,256]{2,1,0:T(8,128)(2,1)} %bitcast.30), calls=%async_computation.2 | async-start | bytes 1048576 | tf_op jit(solution)/shard_map/all_to_all | solution.py:94
  102.8 0.2 copy.21
  103.0 3.4 %collective-permute-start = (bf16[2,1024]{0,1:T(8,128)(2,1)S(1)}, bf16[2,1024]{0,1:T(8,128)(2,1)S(1)}, u32[]{:S(2)}, u32[]{:S(2)}) collective-permute-start(bf16[2,1024]{0,1:T(8,128)(2,1)S(1)} %copy.21), channel_id=1, source_target_pairs={{0,4},{4,8},{8,12},{12,16},{16,20},{20,24},{24,28},{28,32},{32,36}... | collective-permute-start | bytes 12296 | tf_op jit(solution)/shard_map/ppermute | solution.py:13
  106.4 0.2 copy.20
  106.6 3.6 %collective-permute-done = bf16[2,1024]{0,1:T(8,128)(2,1)S(1)} collective-permute-done((bf16[2,1024]{0,1:T(8,128)(2,1)S(1)}, bf16[2,1024]{0,1:T(8,128)(2,1)S(1)}, u32[]{:S(2)}, u32[]{:S(2)}) %collective-permute-start) | collective-permute-done | bytes 4128 | tf_op jit(solution)/shard_map/ppermute | solution.py:13
  110.1 24.7 %all-to-all-done.2 = bf16[64,16,256]{2,1,0:T(8,128)(2,1)S(1)} async-done(((bf16[64,16,256]{2,1,0:T(8,128)(2,1)}), bf16[64,16,256]{2,1,0:T(8,128)(2,1)S(1)}, u32[]{:S(2)}, u32[]{:S(2)}) %all-to-all-start.2) | async-done | bytes 524320 | tf_op jit(solution)/shard_map/all_to_all | solution.py:94
  134.8 1.2 fusion.33
  136.1 0.1 collective-permute-start.4
  136.3 5.7 %collective-permute-start.5 = (bf16[256,1024]{0,1:T(8,128)(2,1)S(1)}, bf16[256,1024]{0,1:T(8,128)(2,1)S(1)}, u32[]{:S(2)}, u32[]{:S(2)}) collective-permute-start(bf16[256,1024]{0,1:T(8,128)(2,1)S(1)} %fusion.33), channel_id=1, source_target_pairs={{0,3},{1,0},{2,1},{3,2},{4,7},{5,4},{6,5},{7,6},{8,11},{9,8},{10,9... | collective-permute-start | bytes 1572872 | tf_op jit(solution)/shard_map/ppermute | solution.py:111
  141.9 0.8 collective-permute-start.3
  142.7 4.6 %all-gather.2.cloned.1.call-done = bf16[4096,1024]{1,0:T(8,128)(2,1)} async-done(((bf16[64,1024]{1,0:T(8,128)(2,1)}), bf16[4096,1024]{1,0:T(8,128)(2,1)}) %all-gather.2.cloned.1.call-update) | async-done | bytes 8388624 | tf_op jit(solution)/shard_map/all_gather | solution.py:82
  147.4 2.3 %fusion.17 = f32[256,1024]{1,0:T(8,128)S(1)} fusion(bf16[256,1024]{0,1:T(8,128)(2,1)S(1)} %fusion.33, bf16[4096,1024]{1,0:T(8,128)(2,1)} %all-gather.2.cloned.1.call-done, s32[]{:T(128)S(6)} %select_n.27), kind=kOutput, calls=%fused_computation.22 | convolution fusion | flops 536870912 | bytes 3670020 | tf_op jit(solution)/shard_map/dot_general | solution.py:113
  149.7 19.9 %collective-permute-done.4 = bf16[256,1024]{0,1:T(8,128)(2,1)S(1)} collective-permute-done((bf16[256,1024]{0,1:T(8,128)(2,1)S(1)}, bf16[256,1024]{0,1:T(8,128)(2,1)S(1)}, u32[]{:S(2)}, u32[]{:S(2)}) %collective-permute-start.4) | collective-permute-done | bytes 524320 | tf_op jit(solution)/shard_map/ppermute | solution.py:111
  169.6 2.3 %fusion.13 = f32[256,1024]{1,0:T(8,128)S(1)} fusion(bf16[256,1024]{0,1:T(8,128)(2,1)S(1)} %collective-permute-done.4, bf16[4096,1024]{1,0:T(8,128)(2,1)} %all-gather.2.cloned.1.call-done, s32[]{:T(128)S(6)} %select_n.31), kind=kOutput, calls=%fused_computation.18 | convolution fusion | flops 536870912 | bytes 3670020 | tf_op jit(solution)/shard_map/dot_general | solution.py:115
  171.9 12.8 %collective-permute-done.5 = bf16[256,1024]{0,1:T(8,128)(2,1)S(1)} collective-permute-done((bf16[256,1024]{0,1:T(8,128)(2,1)S(1)}, bf16[256,1024]{0,1:T(8,128)(2,1)S(1)}, u32[]{:S(2)}, u32[]{:S(2)}) %collective-permute-start.5) | collective-permute-done | bytes 524320 | tf_op jit(solution)/shard_map/ppermute | solution.py:111
  184.7 2.3 %fusion.11 = f32[256,1024]{1,0:T(8,128)S(1)} fusion(bf16[256,1024]{0,1:T(8,128)(2,1)S(1)} %collective-permute-done.5, bf16[4096,1024]{1,0:T(8,128)(2,1)} %all-gather.2.cloned.1.call-done, s32[]{:T(128)S(6)} %select_n.33), kind=kOutput, calls=%fused_computation.16 | convolution fusion | flops 536870912 | bytes 3670020 | tf_op jit(solution)/shard_map/dot_general | solution.py:115
  187.0 0.0 collective-permute-done.3
  187.0 3.1 %fusion.28 = bf16[256,1024]{1,0:T(8,128)(2,1)} fusion(f32[256,1024]{1,0:T(8,128)S(1)} %fusion.11, f32[256,1024]{1,0:T(8,128)S(1)} %fusion.13, f32[256,1024]{1,0:T(8,128)S(1)} %fusion.17, bf16[256,1024]{0,1:T(8,128)(2,1)S(1)} %collective-permute-done.3, bf16[4096,1024]{1,0:T(8,128)(2,1)} %all-gather.2.cloned.1.call-done, s32[]{:T(128)S(6)} %select_n.29), kind=kOutput, calls=%fused_computation.31 | convolution fusion | flops 537919488 | bytes 6291460 | tf_op jit(solution)/shard_map/dot_general | solution.py:115
  (7 shorter events, 0.0 us)
Async XLA Ops:
  6.5 26.3 %copy-start = (bf16[256,1024]{1,0:T(8,128)(2,1)S(1)}, bf16[256,1024]{1,0:T(8,128)(2,1)}, u32[]{:S(2)}) copy-start(bf16[256,1024]{1,0:T(8,128)(2,1)} %param.16) | copy-start | bytes 1572868
  6.5 140.8 %all-gather.2.cloned.1.call-start = ((), (), s32[]{:S(2)}) async-start(), calls=%async_computation.3 | async-start | bytes 8519680 | tf_op jit(solution)/shard_map/all_gather | solution.py:82
  9.3 36.2 %all-to-all-start.1 = ((bf16[64,16,256]{2,1,0:T(8,128)(2,1)}), bf16[64,16,256]{2,1,0:T(8,128)(2,1)S(1)}, u32[]{:S(2)}, u32[]{:S(2)}) async-start(bf16[64,16,256]{2,1,0:T(8,128)(2,1)} %bitcast.12), calls=%async_computation.1 | async-start | bytes 1048576 | tf_op jit(solution)/shard_map/all_to_all | solution.py:84
  24.3 8.8 %collective-permute-start.1 = (bf16[2,1024]{0,1:T(8,128)(2,1)S(1)}, bf16[2,1024]{0,1:T(8,128)(2,1)S(1)}, u32[]{:S(2)}, u32[]{:S(2)}) collective-permute-start(bf16[2,1024]{0,1:T(8,128)(2,1)S(1)} %copy.24), channel_id=1, source_target_pairs={{0,4},{4,8},{8,12},{12,16},{16,20},{20,24},{24,28},{28,32},{32,36}... | collective-permute-start | bytes 12296 | tf_op jit(solution)/shard_map/ppermute | solution.py:13
  28.6 6.2 %collective-permute-start.2 = (bf16[2,1024]{0,1:T(8,128)(2,1)S(1)}, bf16[2,1024]{0,1:T(8,128)(2,1)S(1)}, u32[]{:S(2)}, u32[]{:S(2)}) collective-permute-start(bf16[2,1024]{0,1:T(8,128)(2,1)S(1)} %copy.27), channel_id=1, source_target_pairs={{0,4},{4,8},{8,12},{12,16},{16,20},{20,24},{24,28},{28,32},{32,36}... | collective-permute-start | bytes 12296 | tf_op jit(solution)/shard_map/ppermute | solution.py:13
  32.8 49.6 %copy-start.5 = (bf16[256,64]{1,0:T(8,128)(2,1)S(1)}, bf16[256,64]{1,0:T(8,128)(2,1)}, u32[]{:S(2)}) copy-start(bf16[256,64]{1,0:T(8,128)(2,1)} %constant.117) | copy-start | bytes 98308
  83.6 0.9 copy-start.2
  83.6 1.0 copy-start.3
  84.6 1.2 copy-start.9
  88.2 1.0 copy-start.4
  90.5 2.7 %copy-start.7 = (bf16[64,128]{1,0:T(8,128)(2,1)S(1)}, bf16[64,128]{1,0:T(8,128)(2,1)}, u32[]{:S(2)}) copy-start(bf16[64,128]{1,0:T(8,128)(2,1)} %constant.118) | copy-start | bytes 49156
  91.1 3.8 %copy-start.6 = (bf16[64,128]{1,0:T(8,128)(2,1)S(1)}, bf16[64,128]{1,0:T(8,128)(2,1)}, u32[]{:S(2)}) copy-start(bf16[64,128]{1,0:T(8,128)(2,1)} %constant.119) | copy-start | bytes 49156
  92.5 10.3 %copy-start.1 = (bf16[256,1024]{1,0:T(8,128)(2,1)S(1)}, bf16[256,1024]{1,0:T(8,128)(2,1)}, u32[]{:S(2)}) copy-start(bf16[256,1024]{1,0:T(8,128)(2,1)} %param.14) | copy-start | bytes 1572868
  93.1 41.7 %copy-start.8 = (f32[1024]{0:T(1024)S(1)}, f32[1024]{0:T(1024)}, u32[]{:S(2)}) copy-start(f32[1024]{0:T(1024)} %param.19) | copy-start | bytes 12292
  96.3 38.6 %all-to-all-start.2 = ((bf16[64,16,256]{2,1,0:T(8,128)(2,1)}), bf16[64,16,256]{2,1,0:T(8,128)(2,1)S(1)}, u32[]{:S(2)}, u32[]{:S(2)}) async-start(bf16[64,16,256]{2,1,0:T(8,128)(2,1)} %bitcast.30), calls=%async_computation.2 | async-start | bytes 1048576 | tf_op jit(solution)/shard_map/all_to_all | solution.py:94
  103.0 7.2 %collective-permute-start = (bf16[2,1024]{0,1:T(8,128)(2,1)S(1)}, bf16[2,1024]{0,1:T(8,128)(2,1)S(1)}, u32[]{:S(2)}, u32[]{:S(2)}) collective-permute-start(bf16[2,1024]{0,1:T(8,128)(2,1)S(1)} %copy.21), channel_id=1, source_target_pairs={{0,4},{4,8},{8,12},{12,16},{16,20},{20,24},{24,28},{28,32},{32,36}... | collective-permute-start | bytes 12296 | tf_op jit(solution)/shard_map/ppermute | solution.py:13
  136.1 33.5 %collective-permute-start.4 = (bf16[256,1024]{0,1:T(8,128)(2,1)S(1)}, bf16[256,1024]{0,1:T(8,128)(2,1)S(1)}, u32[]{:S(2)}, u32[]{:S(2)}) collective-permute-start(bf16[256,1024]{0,1:T(8,128)(2,1)S(1)} %fusion.33), channel_id=1, source_target_pairs={{0,2},{1,3},{2,0},{3,1},{4,6},{5,7},{6,4},{7,5},{8,10},{9,11},{10,... | collective-permute-start | bytes 1572872 | tf_op jit(solution)/shard_map/ppermute | solution.py:111
  136.3 48.4 %collective-permute-start.5 = (bf16[256,1024]{0,1:T(8,128)(2,1)S(1)}, bf16[256,1024]{0,1:T(8,128)(2,1)S(1)}, u32[]{:S(2)}, u32[]{:S(2)}) collective-permute-start(bf16[256,1024]{0,1:T(8,128)(2,1)S(1)} %fusion.33), channel_id=1, source_target_pairs={{0,3},{1,0},{2,1},{3,2},{4,7},{5,4},{6,5},{7,6},{8,11},{9,8},{10,9... | collective-permute-start | bytes 1572872 | tf_op jit(solution)/shard_map/ppermute | solution.py:111
  141.9 45.1 %collective-permute-start.3 = (bf16[256,1024]{0,1:T(8,128)(2,1)S(1)}, bf16[256,1024]{0,1:T(8,128)(2,1)S(1)}, u32[]{:S(2)}, u32[]{:S(2)}) collective-permute-start(bf16[256,1024]{0,1:T(8,128)(2,1)S(1)} %fusion.33), channel_id=1, source_target_pairs={{0,1},{1,2},{2,3},{3,0},{4,5},{5,6},{6,7},{7,4},{8,9},{9,10},{10,1... | collective-permute-start | bytes 1572872 | tf_op jit(solution)/shard_map/ppermute | solution.py:111
Sparse Core Ops, SparseCore 0:
  10.9 136.4 all-gather.1

commit v6 on v5

--- a/solution.py
+++ b/solution.py
@@ -4,7 +4,7 @@
 from jax import lax
 from jax.sharding import PartitionSpec as P
 
-TRANSFORM_PRECISION = lax.Precision.DEFAULT
+TRANSFORM_PRECISION = lax.Precision.HIGH
 
 
 def shifted(value, axis, by):
@@ -80,16 +80,15 @@
     per_device = channels // groups
     tables = make_tables(groups, tokens_here)
     weights = lax.all_gather(out_weight, "seq", axis=0, tiled=True)
-    filter_cols = long_filter.T.reshape(groups, per_device, tokens_here)
-    filter_piece = lax.all_to_all(filter_cols, "seq", split_axis=0, concat_axis=0, tiled=True)
     tails = shifted((query_rows[-2:], key_rows[-2:], value_rows[-2:]), "seq", 1)
     query_mix = causal_short(query_rows, tails[0], short_filter[:, 0, :])
     key_mix = causal_short(key_rows, tails[1], short_filter[:, 1, :])
     value_mix = causal_short(value_rows, tails[2], short_filter[:, 2, :])
     gated = (key_mix * value_mix).astype(jnp.bfloat16)
     gated_cols = gated.T.reshape(groups, per_device, tokens_here)
-    gated_piece = lax.all_to_all(gated_cols, "seq", split_axis=0, concat_axis=0, tiled=True)
-    pieces = jnp.concatenate([gated_piece, filter_piece], 1)
+    filter_cols = long_filter.T.reshape(groups, per_device, tokens_here)
+    outgoing = jnp.concatenate([gated_cols, filter_cols], 1)
+    pieces = lax.all_to_all(outgoing, "seq", split_axis=0, concat_axis=0, tiled=True)
     mixed = long_conv(pieces, per_device, tables)
     returned = lax.all_to_all(mixed, "seq", split_axis=0, concat_axis=0, tiled=True)
     conv = returned.reshape(channels, tokens_here).T

time: 198 us -> 204 us (1.030)
  the two profiles are of different devices: /device:TPU:35 before, /device:TPU:33 now
where the time goes in v6:
time: 204 us; the launch traced here: 203 us
  waiting for transfers between devices  69.2 us (34%)
  blocking collectives  52.6 us (26%)
  matrix products  27.1 us (13%)
  starting transfers between devices  19.4 us (10%)
  between operations  13.8 us (7%)
  local copies, waits for them, and re-layouts  13.6 us (7%)
  other arithmetic  7.28 us (4%)
    all_to_all x1, blocking collectives, block(): lax.all_to_all(outgoing, 'seq', split_axis=0, concat_axis=0, tiled=True)  52.6 us
    ppermute x3, waiting for transfers between devices, projection(): lax.ppermute(inner, 'tp', [(j, (j + k) % size) for j in range(size)])  33.7 us
    all_to_all x1, waiting for transfers between devices, block(): lax.all_to_all(mixed, 'seq', split_axis=0, concat_axis=0, tiled=True)  24.7 us
    dot_general x5, matrix products, dot(): jnp.dot(a, b, precision=TRANSFORM_PRECISION, preferred_element_type=jnp.f...  17.1 us
    ppermute x3, starting transfers between devices, shifted(): return lax.ppermute(value, axis, pairs)  9.23 us
    dot_general x3, matrix products, projection(): jnp.dot(chunk, rows_of((here - k) % size), preferred_element_type=jnp.flo...  7.76 us
    unnamed x24, local copies, waits for them, and re-layouts  5.97 us
    all_gather x1, waiting for transfers between devices, block(): weights = lax.all_gather(out_weight, 'seq', axis=0, tiled=True)  5.73 us
  transfers between devices with their start and end apart: 8, of which 5 were waited for; matrix products, arithmetic and copies ran while one was open for 22% of the time, Pallas kernels for 0%

profile of v6, /device:TPU:33, one launch (start us, length us, event | category | flops | bytes accessed | tf_op | source)
XLA Modules:
  0.0 202.9 jit_solution(17226657213630509306)
XLA Ops:
  6.5 0.0 all-gather.2.cloned.1.call-start
  6.5 0.7 all-gather.2.cloned.1.call-update
  7.3 0.7 slice.109
  8.0 0.2 copy.24
  8.2 3.8 %collective-permute-start.1 = (bf16[2,1024]{0,1:T(8,128)(2,1)S(1)}, bf16[2,1024]{0,1:T(8,128)(2,1)S(1)}, u32[]{:S(2)}, u32[]{:S(2)}) collective-permute-start(bf16[2,1024]{0,1:T(8,128)(2,1)S(1)} %copy.24), channel_id=1, source_target_pairs={{0,4},{4,8},{8,12},{12,16},{16,20},{20,24},{24,28},{28,32},{32,36}... | collective-permute-start | bytes 12296 | tf_op jit(solution)/shard_map/ppermute | solution.py:13
  12.0 0.7 slice.115
  12.7 0.2 copy.27
  12.9 1.9 collective-permute-start.2
  14.8 0.9 fusion.44
  15.7 1.2 copy.23
  17.0 1.2 copy.26
  18.2 1.2 copy.29
  19.5 0.0 collective-permute-done.1
  19.5 0.0 collective-permute-done.2
  19.5 0.0 copy-start.5
  19.5 1.9 multiply_convert_fusion
  21.4 0.1 pad_maximum_fusion
  21.6 52.6 %all_to_all.10 = bf16[64,32,256]{2,1,0:T(8,128)(2,1)S(1)} all-to-all(bf16[64,32,256]{2,1,0:T(8,128)(2,1)S(1)} %pad_maximum_fusion), channel_id=1, replica_groups=mesh['seq'=64,'tp'=4] {'seq'}, dimensions={0} | all-to-all | bytes 2097152 | tf_op jit(solution)/shard_map/all_to_all | solution.py:91
  74.1 0.6 copy.38
  74.7 0.0 copy-done.5
  74.8 2.3 %fusion.45 = f32[256,8192]{1,0:T(8,128)S(1)} fusion(f32[256,64]{1,0:T(8,128)S(1)} %copy-done.5, bf16[64,8192]{1,0:T(8,128)(2,1)S(1)} %bitcast.68), kind=kOutput, calls=%fused_computation.58 | convolution fusion | flops 805306368 | bytes 9502720 | tf_op jit(solution)/shard_map/dot_general | solution.py:41
  77.1 0.0 copy-start.3
  77.1 0.0 copy-start.4
  77.1 0.9 fusion.43
  78.0 0.0 copy-done.3
  78.0 0.0 copy-done.4
  78.1 0.0 copy-start.1
  78.1 1.2 fusion.5
  79.3 0.0 copy-done.1
  79.3 7.2 %fusion = f32[128,32,512]{2,0,1:T(8,128)S(1)} fusion(f32[512,512,1]{1,0,2:T(8,128)S(1)} %copy-done.1, f32[128,32,256]{2,0,1:T(8,128)S(1)} %get-tuple-element.6, f32[128,32,256]{2,0,1:T(8,128)S(1)} %get-tuple-element.5), kind=kOutput, calls=%fused_computation | convolution fusion | flops 6444548096 | bytes 17825792 | tf_op jit(solution)/shard_map/dot_general | solution.py:41
  86.5 0.0 copy-start
  86.5 0.8 multiply_subtract_fusion.1
  87.3 0.4 copy-done
  87.7 3.5 %fusion.7 = f32[128,16,512]{2,0,1:T(8,128)S(1)} fusion(f32[512,512,1]{1,0,2:T(8,128)S(1)} %copy-done, f32[128,16,256]{2,0,1:T(8,128)S(1)} %get-tuple-element.8, f32[128,16,256]{2,0,1:T(8,128)S(1)} %get-tuple-element.7), kind=kOutput, calls=%fused_computation.12 | convolution fusion | flops 3222274048 | bytes 9437184 | tf_op jit(solution)/shard_map/dot_general | solution.py:41
  91.2 2.0 multiply_add_fusion
  93.2 1.8 copy.34
  95.1 1.9 copy.35
  97.0 0.0 copy-done.7
  97.0 0.0 copy-start.2
  97.0 2.9 %fusion.46 = f32[4096,64]{0,1:T(8,128)S(1)} fusion(f32[128,4096]{0,1:T(8,128)} %bitcast.66, f32[64,128]{1,0:T(8,128)S(1)} %copy-done.7), kind=kOutput, calls=%fused_computation.59 | convolution fusion | flops 201326592 | bytes 3178496 | tf_op jit(solution)/shard_map/dot_general | solution.py:41
  99.9 0.0 copy-start.8
  99.9 0.0 copy-done.6
  99.9 1.2 fusion.4
  101.1 0.9 copy.39
  102.0 5.7 %all-to-all-start.1 = ((bf16[64,16,256]{2,1,0:T(8,128)(2,1)}), bf16[64,16,256]{2,1,0:T(8,128)(2,1)S(1)}, u32[]{:S(2)}, u32[]{:S(2)}) async-start(bf16[64,16,256]{2,1,0:T(8,128)(2,1)} %bitcast.30), calls=%async_computation.1 | async-start | bytes 1048576 | tf_op jit(solution)/shard_map/all_to_all | solution.py:93
  107.7 0.0 copy-done.2
  107.7 0.2 copy.21
  107.9 3.5 %collective-permute-start = (bf16[2,1024]{0,1:T(8,128)(2,1)S(1)}, bf16[2,1024]{0,1:T(8,128)(2,1)S(1)}, u32[]{:S(2)}, u32[]{:S(2)}) collective-permute-start(bf16[2,1024]{0,1:T(8,128)(2,1)S(1)} %copy.21), channel_id=1, source_target_pairs={{0,4},{4,8},{8,12},{12,16},{16,20},{20,24},{24,28},{28,32},{32,36}... | collective-permute-start | bytes 12296 | tf_op jit(solution)/shard_map/ppermute | solution.py:13
  111.5 0.2 copy.20
  111.7 4.4 %collective-permute-done = bf16[2,1024]{0,1:T(8,128)(2,1)S(1)} collective-permute-done((bf16[2,1024]{0,1:T(8,128)(2,1)S(1)}, bf16[2,1024]{0,1:T(8,128)(2,1)S(1)}, u32[]{:S(2)}, u32[]{:S(2)}) %collective-permute-start) | collective-permute-done | bytes 4128 | tf_op jit(solution)/shard_map/ppermute | solution.py:13
  116.1 24.7 %all-to-all-done.1 = bf16[64,16,256]{2,1,0:T(8,128)(2,1)S(1)} async-done(((bf16[64,16,256]{2,1,0:T(8,128)(2,1)}), bf16[64,16,256]{2,1,0:T(8,128)(2,1)S(1)}, u32[]{:S(2)}, u32[]{:S(2)}) %all-to-all-start.1) | async-done | bytes 524320 | tf_op jit(solution)/shard_map/all_to_all | solution.py:93
  140.8 0.0 copy-done.8
  140.8 1.2 fusion.33
  142.0 0.1 collective-permute-start.4
  142.2 3.3 %collective-permute-start.5 = (bf16[256,1024]{0,1:T(8,128)(2,1)S(1)}, bf16[256,1024]{0,1:T(8,128)(2,1)S(1)}, u32[]{:S(2)}, u32[]{:S(2)}) collective-permute-start(bf16[256,1024]{0,1:T(8,128)(2,1)S(1)} %fusion.33), channel_id=1, source_target_pairs={{0,3},{1,0},{2,1},{3,2},{4,7},{5,4},{6,5},{7,6},{8,11},{9,8},{10,9... | collective-permute-start | bytes 1572872 | tf_op jit(solution)/shard_map/ppermute | solution.py:110
  145.5 1.0 collective-permute-start.3
  146.6 5.7 %all-gather.2.cloned.1.call-done = bf16[4096,1024]{1,0:T(8,128)(2,1)} async-done(((bf16[64,1024]{1,0:T(8,128)(2,1)}), bf16[4096,1024]{1,0:T(8,128)(2,1)}) %all-gather.2.cloned.1.call-update) | async-done | bytes 8388624 | tf_op jit(solution)/shard_map/all_gather | solution.py:82
  152.3 2.3 %fusion.17 = f32[256,1024]{1,0:T(8,128)S(1)} fusion(bf16[256,1024]{0,1:T(8,128)(2,1)S(1)} %fusion.33, bf16[4096,1024]{1,0:T(8,128)(2,1)} %all-gather.2.cloned.1.call-done, s32[]{:T(128)S(6)} %select_n.27), kind=kOutput, calls=%fused_computation.22 | convolution fusion | flops 536870912 | bytes 3670020 | tf_op jit(solution)/shard_map/dot_general | solution.py:112
  154.6 21.2 %collective-permute-done.4 = bf16[256,1024]{0,1:T(8,128)(2,1)S(1)} collective-permute-done((bf16[256,1024]{0,1:T(8,128)(2,1)S(1)}, bf16[256,1024]{0,1:T(8,128)(2,1)S(1)}, u32[]{:S(2)}, u32[]{:S(2)}) %collective-permute-start.4) | collective-permute-done | bytes 524320 | tf_op jit(solution)/shard_map/ppermute | solution.py:110
  175.8 2.3 %fusion.13 = f32[256,1024]{1,0:T(8,128)S(1)} fusion(bf16[256,1024]{0,1:T(8,128)(2,1)S(1)} %collective-permute-done.4, bf16[4096,1024]{1,0:T(8,128)(2,1)} %all-gather.2.cloned.1.call-done, s32[]{:T(128)S(6)} %select_n.31), kind=kOutput, calls=%fused_computation.18 | convolution fusion | flops 536870912 | bytes 3670020 | tf_op jit(solution)/shard_map/dot_general | solution.py:114
  178.1 12.5 %collective-permute-done.5 = bf16[256,1024]{0,1:T(8,128)(2,1)S(1)} collective-permute-done((bf16[256,1024]{0,1:T(8,128)(2,1)S(1)}, bf16[256,1024]{0,1:T(8,128)(2,1)S(1)}, u32[]{:S(2)}, u32[]{:S(2)}) %collective-permute-start.5) | collective-permute-done | bytes 524320 | tf_op jit(solution)/shard_map/ppermute | solution.py:110
  190.6 2.3 %fusion.11 = f32[256,1024]{1,0:T(8,128)S(1)} fusion(bf16[256,1024]{0,1:T(8,128)(2,1)S(1)} %collective-permute-done.5, bf16[4096,1024]{1,0:T(8,128)(2,1)} %all-gather.2.cloned.1.call-done, s32[]{:T(128)S(6)} %select_n.33), kind=kOutput, calls=%fused_computation.16 | convolution fusion | flops 536870912 | bytes 3670020 | tf_op jit(solution)/shard_map/dot_general | solution.py:114
  192.9 0.0 collective-permute-done.3
  192.9 3.1 %fusion.28 = bf16[256,1024]{1,0:T(8,128)(2,1)} fusion(f32[256,1024]{1,0:T(8,128)S(1)} %fusion.11, f32[256,1024]{1,0:T(8,128)S(1)} %fusion.13, f32[256,1024]{1,0:T(8,128)S(1)} %fusion.17, bf16[256,1024]{0,1:T(8,128)(2,1)S(1)} %collective-permute-done.3, bf16[4096,1024]{1,0:T(8,128)(2,1)} %all-gather.2.cloned.1.call-done, s32[]{:T(128)S(6)} %select_n.29), kind=kOutput, calls=%fused_computation.31 | convolution fusion | flops 537919488 | bytes 6291460 | tf_op jit(solution)/shard_map/dot_general | solution.py:114
  (3 shorter events, 0.0 us)
Async XLA Ops:
  6.5 145.8 %all-gather.2.cloned.1.call-start = ((), (), s32[]{:S(2)}) async-start(), calls=%async_computation.2 | async-start | bytes 8519680 | tf_op jit(solution)/shard_map/all_gather | solution.py:82
  8.2 11.3 %collective-permute-start.1 = (bf16[2,1024]{0,1:T(8,128)(2,1)S(1)}, bf16[2,1024]{0,1:T(8,128)(2,1)S(1)}, u32[]{:S(2)}, u32[]{:S(2)}) collective-permute-start(bf16[2,1024]{0,1:T(8,128)(2,1)S(1)} %copy.24), channel_id=1, source_target_pairs={{0,4},{4,8},{8,12},{12,16},{16,20},{20,24},{24,28},{28,32},{32,36}... | collective-permute-start | bytes 12296 | tf_op jit(solution)/shard_map/ppermute | solution.py:13
  12.9 6.6 %collective-permute-start.2 = (bf16[2,1024]{0,1:T(8,128)(2,1)S(1)}, bf16[2,1024]{0,1:T(8,128)(2,1)S(1)}, u32[]{:S(2)}, u32[]{:S(2)}) collective-permute-start(bf16[2,1024]{0,1:T(8,128)(2,1)S(1)} %copy.27), channel_id=1, source_target_pairs={{0,4},{4,8},{8,12},{12,16},{16,20},{20,24},{24,28},{28,32},{32,36}... | collective-permute-start | bytes 12296 | tf_op jit(solution)/shard_map/ppermute | solution.py:13
  19.5 55.2 %copy-start.5 = (f32[256,64]{1,0:T(8,128)S(1)}, f32[256,64]{1,0:T(8,128)}, u32[]{:S(2)}) copy-start(f32[256,64]{1,0:T(8,128)} %constant.53.clone) | copy-start | bytes 196612
  77.1 0.9 copy-start.3
  77.1 1.0 copy-start.4
  78.1 1.3 copy-start.1
  86.5 1.2 copy-start
  93.2 3.8 %copy-start.7 = (f32[64,128]{1,0:T(8,128)S(1)}, f32[64,128]{1,0:T(8,128)}, u32[]{:S(2)}) copy-start(f32[64,128]{1,0:T(8,128)} %constant.58.clone) | copy-start | bytes 98308
  95.1 4.8 %copy-start.6 = (f32[64,128]{1,0:T(8,128)S(1)}, f32[64,128]{1,0:T(8,128)}, u32[]{:S(2)}) copy-start(f32[64,128]{1,0:T(8,128)} %constant.59.clone) | copy-start | bytes 98308
  97.0 10.7 %copy-start.2 = (bf16[256,1024]{1,0:T(8,128)(2,1)S(1)}, bf16[256,1024]{1,0:T(8,128)(2,1)}, u32[]{:S(2)}) copy-start(bf16[256,1024]{1,0:T(8,128)(2,1)} %param.14) | copy-start | bytes 1572868
  99.9 40.9 %copy-start.8 = (f32[1024]{0:T(1024)S(1)}, f32[1024]{0:T(1024)}, u32[]{:S(2)}) copy-start(f32[1024]{0:T(1024)} %param.19) | copy-start | bytes 12292
  102.0 38.8 %all-to-all-start.1 = ((bf16[64,16,256]{2,1,0:T(8,128)(2,1)}), bf16[64,16,256]{2,1,0:T(8,128)(2,1)S(1)}, u32[]{:S(2)}, u32[]{:S(2)}) async-start(bf16[64,16,256]{2,1,0:T(8,128)(2,1)} %bitcast.30), calls=%async_computation.1 | async-start | bytes 1048576 | tf_op jit(solution)/shard_map/all_to_all | solution.py:93
  107.9 8.1 %collective-permute-start = (bf16[2,1024]{0,1:T(8,128)(2,1)S(1)}, bf16[2,1024]{0,1:T(8,128)(2,1)S(1)}, u32[]{:S(2)}, u32[]{:S(2)}) collective-permute-start(bf16[2,1024]{0,1:T(8,128)(2,1)S(1)} %copy.21), channel_id=1, source_target_pairs={{0,4},{4,8},{8,12},{12,16},{16,20},{20,24},{24,28},{28,32},{32,36}... | collective-permute-start | bytes 12296 | tf_op jit(solution)/shard_map/ppermute | solution.py:13
  142.0 33.8 %collective-permute-start.4 = (bf16[256,1024]{0,1:T(8,128)(2,1)S(1)}, bf16[256,1024]{0,1:T(8,128)(2,1)S(1)}, u32[]{:S(2)}, u32[]{:S(2)}) collective-permute-start(bf16[256,1024]{0,1:T(8,128)(2,1)S(1)} %fusion.33), channel_id=1, source_target_pairs={{0,2},{1,3},{2,0},{3,1},{4,6},{5,7},{6,4},{7,5},{8,10},{9,11},{10,... | collective-permute-start | bytes 1572872 | tf_op jit(solution)/shard_map/ppermute | solution.py:110
  142.2 48.4 %collective-permute-start.5 = (bf16[256,1024]{0,1:T(8,128)(2,1)S(1)}, bf16[256,1024]{0,1:T(8,128)(2,1)S(1)}, u32[]{:S(2)}, u32[]{:S(2)}) collective-permute-start(bf16[256,1024]{0,1:T(8,128)(2,1)S(1)} %fusion.33), channel_id=1, source_target_pairs={{0,3},{1,0},{2,1},{3,2},{4,7},{5,4},{6,5},{7,6},{8,11},{9,8},{10,9... | collective-permute-start | bytes 1572872 | tf_op jit(solution)/shard_map/ppermute | solution.py:110
  145.5 47.4 %collective-permute-start.3 = (bf16[256,1024]{0,1:T(8,128)(2,1)S(1)}, bf16[256,1024]{0,1:T(8,128)(2,1)S(1)}, u32[]{:S(2)}, u32[]{:S(2)}) collective-permute-start(bf16[256,1024]{0,1:T(8,128)(2,1)S(1)} %fusion.33), channel_id=1, source_target_pairs={{0,1},{1,2},{2,3},{3,0},{4,5},{5,6},{6,7},{7,4},{8,9},{9,10},{10,1... | collective-permute-start | bytes 1572872 | tf_op jit(solution)/shard_map/ppermute | solution.py:110
Sparse Core Ops, SparseCore 0:
  10.9 141.3 all-gather.1

commit v7 on v6

--- a/solution.py
+++ b/solution.py
@@ -1,3 +1,5 @@
+import math
+
 import numpy as np
 import jax
 import jax.numpy as jnp
@@ -7,8 +9,20 @@
 TRANSFORM_PRECISION = lax.Precision.HIGH
 
 
+SEQ = ("zh", "x", "y", "core")
+SEQ_SIZES = (2, 4, 4, 2)
+
+
+def seq_all_to_all(value):
+    shape = value.shape
+    parts = value.reshape(SEQ_SIZES + shape[1:])
+    for dim in (3, 2, 1, 0):
+        parts = lax.all_to_all(parts, SEQ[dim], split_axis=dim, concat_axis=dim, tiled=True)
+    return parts.reshape(shape)
+
+
 def shifted(value, axis, by):
-    size = lax.axis_size(axis)
+    size = math.prod(SEQ_SIZES)
     pairs = [(i, i + by) for i in range(size) if 0 <= i + by < size]
     return lax.ppermute(value, axis, pairs)
 
@@ -76,11 +90,11 @@
 
 def block(query_rows, key_rows, value_rows, short_filter, long_filter, skip_gain, out_weight):
     tokens_here, channels = query_rows.shape
-    groups = lax.axis_size("seq")
+    groups = math.prod(SEQ_SIZES)
     per_device = channels // groups
     tables = make_tables(groups, tokens_here)
-    weights = lax.all_gather(out_weight, "seq", axis=0, tiled=True)
-    tails = shifted((query_rows[-2:], key_rows[-2:], value_rows[-2:]), "seq", 1)
+    weights = lax.all_gather(out_weight, SEQ, axis=0, tiled=True)
+    tails = shifted((query_rows[-2:], key_rows[-2:], value_rows[-2:]), SEQ, 1)
     query_mix = causal_short(query_rows, tails[0], short_filter[:, 0, :])
     key_mix = causal_short(key_rows, tails[1], short_filter[:, 1, :])
     value_mix = causal_short(value_rows, tails[2], short_filter[:, 2, :])
@@ -88,9 +102,9 @@
     gated_cols = gated.T.reshape(groups, per_device, tokens_here)
     filter_cols = long_filter.T.reshape(groups, per_device, tokens_here)
     outgoing = jnp.concatenate([gated_cols, filter_cols], 1)
-    pieces = lax.all_to_all(outgoing, "seq", split_axis=0, concat_axis=0, tiled=True)
+    pieces = seq_all_to_all(outgoing)
     mixed = long_conv(pieces, per_device, tables)
-    returned = lax.all_to_all(mixed, "seq", split_axis=0, concat_axis=0, tiled=True)
+    returned = seq_all_to_all(mixed)
     conv = returned.reshape(channels, tokens_here).T
     inner = (query_mix * (conv.astype(jnp.float32) + skip_gain * gated.astype(jnp.float32))).astype(
         jnp.bfloat16
@@ -116,15 +130,8 @@
 
 
 def solution(mesh):
-    placed = (
-        P("seq", "tp"),
-        P("seq", "tp"),
-        P("seq", "tp"),
-        P(None, None, "tp"),
-        P("seq", "tp"),
-        P("tp"),
-        P("seq", "tp"),
-    )
-    return jax.shard_map(
-        block, mesh=mesh, in_specs=placed, out_specs=P("seq", "tp"), check_vma=False
-    )
+    _, tp = mesh.axis_names
+    split = jax.sharding.Mesh(mesh.devices.reshape(SEQ_SIZES + (mesh.shape[tp],)), SEQ + ("tp",))
+    rows = P(SEQ, "tp")
+    placed = (rows, rows, rows, P(None, None, "tp"), rows, P("tp"), rows)
+    return jax.shard_map(block, mesh=split, in_specs=placed, out_specs=rows, check_vma=False)

time: 204 us -> 264 us (1.29)
  the two profiles are of different devices: /device:TPU:33 before, /device:TPU:32 now
where the time goes in v7:
time: 264 us; the launch traced here: 263 us
  blocking collectives  140 us (53%)
  waiting for transfers between devices  47 us (18%)
  matrix products  27.1 us (10%)
  local copies, waits for them, and re-layouts  14.3 us (5%)
  between operations  13.8 us (5%)
  starting transfers between devices  13.7 us (5%)
  other arithmetic  7.28 us (3%)
    all_to_all x7, blocking collectives, seq_all_to_all(): lax.all_to_all(parts, SEQ[dim], split_axis=dim, concat_axis=dim, tiled=True)  140 us
    ppermute x3, waiting for transfers between devices, projection(): lax.ppermute(inner, 'tp', [(j, (j + k) % size) for j in range(size)])  37.3 us
    dot_general x5, matrix products, dot(): jnp.dot(a, b, precision=TRANSFORM_PRECISION, preferred_element_type=jnp.f...  17 us
    all_to_all x1, waiting for transfers between devices, seq_all_to_all(): lax.all_to_all(parts, SEQ[dim], split_axis=dim, concat_axis=dim, tiled=True)  8.06 us
    dot_general x3, matrix products, projection(): jnp.dot(chunk, rows_of((here - k) % size), preferred_element_type=jnp.flo...  7.76 us
    ppermute x3, starting transfers between devices, shifted(): return lax.ppermute(value, axis, pairs)  6.83 us
  transfers between devices with their start and end apart: 8, of which 4 were waited for; matrix products, arithmetic and copies ran while one was open for 17% of the time, Pallas kernels for 0%

profile of v7, /device:TPU:32, one launch (start us, length us, event | category | flops | bytes accessed | tf_op | source)
XLA Modules:
  0.0 263.0 jit_solution(1316377141322901813)
XLA Ops:
  6.5 0.7 all-gather.2.cloned.1.call-update
  7.3 0.7 slice.109
  8.0 0.2 copy.64
  8.2 1.8 collective-permute-start.1
  10.0 0.7 slice.115
  10.7 0.2 copy.67
  10.9 3.8 %collective-permute-start.2 = (bf16[2,1024]{0,1:T(8,128)(2,1)S(1)}, bf16[2,1024]{0,1:T(8,128)(2,1)S(1)}, u32[]{:S(2)}, u32[]{:S(2)}) collective-permute-start(bf16[2,1024]{0,1:T(8,128)(2,1)S(1)} %copy.67), channel_id=1, source_target_pairs={{0,4},{4,8},{8,12},{12,16},{16,20},{20,24},{24,28},{28,32},{32,36}... | collective-permute-start | bytes 12296 | tf_op jit(solution)/shard_map/ppermute | solution.py:27
  14.7 0.9 fusion.44
  15.6 1.2 copy.63
  16.8 1.2 copy.66
  18.1 1.2 copy.69
  19.4 1.9 multiply_convert_fusion
  21.3 0.1 pad_maximum_fusion
  21.4 0.1 copy.70
  21.5 4.6 %all_to_all.40 = bf16[2,4,4,2,32,256]{5,4,2,1,0,3:T(8,128)(2,1)S(1)} all-to-all(bf16[2,4,4,2,32,256]{5,4,2,1,0,3:T(8,128)(2,1)S(1)} %copy.70), channel_id=1, replica_groups=mesh['zh'=2,'x'=4,'y'=4,'core'=2,'tp'=4] {'core'}, dimensions={3} | all-to-all | bytes 2097152 | tf_op jit(solution)/shard_map/all_to_all | solution.py:20
  26.1 0.1 copy.71
  26.1 20.3 %all_to_all.41 = bf16[2,4,4,2,32,256]{5,4,3,1,0,2:T(8,128)(2,1)S(1)} all-to-all(bf16[2,4,4,2,32,256]{5,4,3,1,0,2:T(8,128)(2,1)S(1)} %copy.71), channel_id=1, replica_groups=mesh['zh'=2,'x'=4,'y'=4,'core'=2,'tp'=4] {'y'}, dimensions={2} | all-to-all | bytes 2097152 | tf_op jit(solution)/shard_map/all_to_all | solution.py:20
  46.4 0.1 copy.72
  46.6 0.0 copy-start.5
  46.6 27.8 %all_to_all.42 = bf16[2,4,4,2,32,256]{5,4,3,2,0,1:T(8,128)(2,1)S(1)} all-to-all(bf16[2,4,4,2,32,256]{5,4,3,2,0,1:T(8,128)(2,1)S(1)} %copy.72), channel_id=1, replica_groups=mesh['zh'=2,'x'=4,'y'=4,'core'=2,'tp'=4] {'x'}, dimensions={1} | all-to-all | bytes 2097152 | tf_op jit(solution)/shard_map/all_to_all | solution.py:20
  74.4 0.1 copy.73
  74.5 58.8 %all_to_all.43 = bf16[2,4,4,2,32,256]{5,4,3,2,1,0:T(8,128)(2,1)S(1)} all-to-all(bf16[2,4,4,2,32,256]{5,4,3,2,1,0:T(8,128)(2,1)S(1)} %copy.73), channel_id=1, replica_groups=mesh['zh'=2,'x'=4,'y'=4,'core'=2,'tp'=4] {'zh'}, dimensions={0} | all-to-all | bytes 2097152 | tf_op jit(solution)/shard_map/all_to_all | solution.py:20
  133.3 0.6 copy.86
  133.9 2.3 fusion.45
  136.3 0.0 copy-start.3
  136.3 0.0 copy-start.4
  136.3 0.9 fusion.43
  137.2 0.0 copy-done.4
  137.2 1.2 fusion.5
  138.5 0.1 copy-done.1
  138.6 7.2 %fusion = f32[128,32,512]{2,0,1:T(8,128)S(1)} fusion(f32[512,512,1]{1,0,2:T(8,128)S(1)} %copy-done.1, f32[128,32,256]{2,0,1:T(8,128)S(1)} %get-tuple-element.6, f32[128,32,256]{2,0,1:T(8,128)S(1)} %get-tuple-element.5), kind=kOutput, calls=%fused_computation | convolution fusion | flops 6444548096 | bytes 17825792 | tf_op jit(solution)/shard_map/dot_general | solution.py:55
  145.8 0.0 copy-start
  145.8 0.8 multiply_subtract_fusion.1
  146.6 0.4 copy-done
  147.0 3.5 %fusion.7 = f32[128,16,512]{2,0,1:T(8,128)S(1)} fusion(f32[512,512,1]{1,0,2:T(8,128)S(1)} %copy-done, f32[128,16,256]{2,0,1:T(8,128)S(1)} %get-tuple-element.8, f32[128,16,256]{2,0,1:T(8,128)S(1)} %get-tuple-element.7), kind=kOutput, calls=%fused_computation.12 | convolution fusion | flops 3222274048 | bytes 9437184 | tf_op jit(solution)/shard_map/dot_general | solution.py:55
  150.5 2.0 multiply_add_fusion
  152.5 1.8 copy.78
  154.3 1.9 copy.79
  156.3 2.8 %fusion.46 = f32[4096,64]{0,1:T(8,128)S(1)} fusion(f32[128,4096]{0,1:T(8,128)} %bitcast.68, f32[64,128]{1,0:T(8,128)S(1)} %copy-done.7), kind=kOutput, calls=%fused_computation.59 | convolution fusion | flops 201326592 | bytes 3178496 | tf_op jit(solution)/shard_map/dot_general | solution.py:55
  159.1 1.2 fusion.4
  160.3 0.1 copy.87
  160.4 0.0 copy-start.2
  160.4 0.1 copy.80
  160.5 0.0 copy-start.8
  160.5 4.3 %all_to_all.44 = bf16[2,4,4,2,16,256]{5,4,2,1,0,3:T(8,128)(2,1)S(1)} all-to-all(bf16[2,4,4,2,16,256]{5,4,2,1,0,3:T(8,128)(2,1)S(1)} %copy.80), channel_id=1, replica_groups=mesh['zh'=2,'x'=4,'y'=4,'core'=2,'tp'=4] {'core'}, dimensions={3} | all-to-all | bytes 1048576 | tf_op jit(solution)/shard_map/all_to_all | solution.py:20
  164.8 0.1 copy.81
  164.9 12.5 %all_to_all.45 = bf16[2,4,4,2,16,256]{5,4,3,1,0,2:T(8,128)(2,1)S(1)} all-to-all(bf16[2,4,4,2,16,256]{5,4,3,1,0,2:T(8,128)(2,1)S(1)} %copy.81), channel_id=1, replica_groups=mesh['zh'=2,'x'=4,'y'=4,'core'=2,'tp'=4] {'y'}, dimensions={2} | all-to-all | bytes 1048576 | tf_op jit(solution)/shard_map/all_to_all | solution.py:20
  177.4 11.6 %all_to_all.46 = bf16[2,4,4,2,16,256]{5,4,3,2,0,1:T(8,128)(2,1)S(1)} all-to-all(bf16[2,4,4,2,16,256]{5,4,3,2,0,1:T(8,128)(2,1)S(1)} %copy.82), channel_id=1, replica_groups=mesh['zh'=2,'x'=4,'y'=4,'core'=2,'tp'=4] {'x'}, dimensions={1} | all-to-all | bytes 1048576 | tf_op jit(solution)/shard_map/all_to_all | solution.py:20
  189.0 0.8 copy.83
  189.8 3.5 %all-to-all-start.7 = ((bf16[2,4,4,2,16,256]{5,4,3,2,1,0:T(8,128)(2,1)}), bf16[2,4,4,2,16,256]{5,4,3,2,1,0:T(8,128)(2,1)S(1)}, u32[]{:S(2)}, u32[]{:S(2)}) async-start(bf16[2,4,4,2,16,256]{5,4,3,2,1,0:T(8,128)(2,1)} %copy.83), calls=%async_computation.7 | async-start | bytes 1048576 | tf_op jit(solution)/shard_map/all_to_all | solution.py:20
  193.3 0.2 copy.61
  193.5 1.3 collective-permute-start
  194.8 0.2 copy.60
  195.0 0.9 collective-permute-done
  196.0 8.1 %all-to-all-done.7 = bf16[2,4,4,2,16,256]{5,4,3,2,1,0:T(8,128)(2,1)S(1)} async-done(((bf16[2,4,4,2,16,256]{5,4,3,2,1,0:T(8,128)(2,1)}), bf16[2,4,4,2,16,256]{5,4,3,2,1,0:T(8,128)(2,1)S(1)}, u32[]{:S(2)}, u32[]{:S(2)}) %all-to-all-start.7) | async-done | bytes 524320 | tf_op jit(solution)/shard_map/all_to_all | solution.py:20
  204.0 1.2 fusion.33
  205.3 0.1 collective-permute-start.4
  205.5 3.3 %collective-permute-start.5 = (bf16[256,1024]{0,1:T(8,128)(2,1)S(1)}, bf16[256,1024]{0,1:T(8,128)(2,1)S(1)}, u32[]{:S(2)}, u32[]{:S(2)}) collective-permute-start(bf16[256,1024]{0,1:T(8,128)(2,1)S(1)} %fusion.33), channel_id=1, source_target_pairs={{0,3},{1,0},{2,1},{3,2},{4,7},{5,4},{6,5},{7,6},{8,11},{9,8},{10,9... | collective-permute-start | bytes 1572872 | tf_op jit(solution)/shard_map/ppermute | solution.py:124
  208.7 2.3 fusion.17
  211.1 28.6 %collective-permute-done.4 = bf16[256,1024]{0,1:T(8,128)(2,1)S(1)} collective-permute-done((bf16[256,1024]{0,1:T(8,128)(2,1)S(1)}, bf16[256,1024]{0,1:T(8,128)(2,1)S(1)}, u32[]{:S(2)}, u32[]{:S(2)}) %collective-permute-start.4) | collective-permute-done | bytes 524320 | tf_op jit(solution)/shard_map/ppermute | solution.py:124
  239.7 2.3 fusion.13
  242.0 8.7 %collective-permute-done.5 = bf16[256,1024]{0,1:T(8,128)(2,1)S(1)} collective-permute-done((bf16[256,1024]{0,1:T(8,128)(2,1)S(1)}, bf16[256,1024]{0,1:T(8,128)(2,1)S(1)}, u32[]{:S(2)}, u32[]{:S(2)}) %collective-permute-start.5) | collective-permute-done | bytes 524320 | tf_op jit(solution)/shard_map/ppermute | solution.py:124
  250.7 2.3 fusion.11
  253.0 3.1 %fusion.28 = bf16[256,1024]{1,0:T(8,128)(2,1)} fusion(f32[256,1024]{1,0:T(8,128)S(1)} %fusion.11, f32[256,1024]{1,0:T(8,128)S(1)} %fusion.13, f32[256,1024]{1,0:T(8,128)S(1)} %fusion.17, bf16[256,1024]{0,1:T(8,128)(2,1)S(1)} %collective-permute-done.3, bf16[4096,1024]{1,0:T(8,128)(2,1)} %all-gather.2.cloned.1.call-done, s32[]{:T(128)S(6)} %select_n.29), kind=kOutput, calls=%fused_computation.31 | convolution fusion | flops 537919488 | bytes 6291460 | tf_op jit(solution)/shard_map/dot_general | solution.py:128
  (17 shorter events, 0.1 us)
Async XLA Ops:
  6.5 202.2 %all-gather.2.cloned.1.call-start = ((), (), s32[]{:S(2)}) async-start(), calls=%async_computation.8 | async-start | bytes 8519680 | tf_op jit(solution)/shard_map/all_gather | solution.py:96
  8.2 11.1 %collective-permute-start.1 = (bf16[2,1024]{0,1:T(8,128)(2,1)S(1)}, bf16[2,1024]{0,1:T(8,128)(2,1)S(1)}, u32[]{:S(2)}, u32[]{:S(2)}) collective-permute-start(bf16[2,1024]{0,1:T(8,128)(2,1)S(1)} %copy.64), channel_id=1, source_target_pairs={{0,4},{4,8},{8,12},{12,16},{16,20},{20,24},{24,28},{28,32},{32,36}... | collective-permute-start | bytes 12296 | tf_op jit(solution)/shard_map/ppermute | solution.py:27
  10.9 8.5 %collective-permute-start.2 = (bf16[2,1024]{0,1:T(8,128)(2,1)S(1)}, bf16[2,1024]{0,1:T(8,128)(2,1)S(1)}, u32[]{:S(2)}, u32[]{:S(2)}) collective-permute-start(bf16[2,1024]{0,1:T(8,128)(2,1)S(1)} %copy.67), channel_id=1, source_target_pairs={{0,4},{4,8},{8,12},{12,16},{16,20},{20,24},{24,28},{28,32},{32,36}... | collective-permute-start | bytes 12296 | tf_op jit(solution)/shard_map/ppermute | solution.py:27
  46.6 87.4 %copy-start.5 = (f32[256,64]{1,0:T(8,128)S(1)}, f32[256,64]{1,0:T(8,128)}, u32[]{:S(2)}) copy-start(f32[256,64]{1,0:T(8,128)} %constant.53.clone) | copy-start | bytes 196612
  136.3 0.9 copy-start.3
  136.3 1.0 copy-start.4
  137.2 1.4 copy-start.1
  145.8 1.2 copy-start
  152.5 3.8 %copy-start.7 = (f32[64,128]{1,0:T(8,128)S(1)}, f32[64,128]{1,0:T(8,128)}, u32[]{:S(2)}) copy-start(f32[64,128]{1,0:T(8,128)} %constant.58.clone) | copy-start | bytes 98308
  154.3 4.7 %copy-start.6 = (f32[64,128]{1,0:T(8,128)S(1)}, f32[64,128]{1,0:T(8,128)}, u32[]{:S(2)}) copy-start(f32[64,128]{1,0:T(8,128)} %constant.59.clone) | copy-start | bytes 98308
  160.4 32.9 %copy-start.2 = (bf16[256,1024]{1,0:T(8,128)(2,1)S(1)}, bf16[256,1024]{1,0:T(8,128)(2,1)}, u32[]{:S(2)}) copy-start(bf16[256,1024]{1,0:T(8,128)(2,1)} %param.14) | copy-start | bytes 1572868
  160.5 43.5 %copy-start.8 = (f32[1024]{0:T(1024)S(1)}, f32[1024]{0:T(1024)}, u32[]{:S(2)}) copy-start(f32[1024]{0:T(1024)} %param.19) | copy-start | bytes 12292
  189.8 14.2 %all-to-all-start.7 = ((bf16[2,4,4,2,16,256]{5,4,3,2,1,0:T(8,128)(2,1)}), bf16[2,4,4,2,16,256]{5,4,3,2,1,0:T(8,128)(2,1)S(1)}, u32[]{:S(2)}, u32[]{:S(2)}) async-start(bf16[2,4,4,2,16,256]{5,4,3,2,1,0:T(8,128)(2,1)} %copy.83), calls=%async_computation.7 | async-start | bytes 1048576 | tf_op jit(solution)/shard_map/all_to_all | solution.py:20
  193.5 2.4 collective-permute-start
  205.3 34.4 %collective-permute-start.4 = (bf16[256,1024]{0,1:T(8,128)(2,1)S(1)}, bf16[256,1024]{0,1:T(8,128)(2,1)S(1)}, u32[]{:S(2)}, u32[]{:S(2)}) collective-permute-start(bf16[256,1024]{0,1:T(8,128)(2,1)S(1)} %fusion.33), channel_id=1, source_target_pairs={{0,2},{1,3},{2,0},{3,1},{4,6},{5,7},{6,4},{7,5},{8,10},{9,11},{10,... | collective-permute-start | bytes 1572872 | tf_op jit(solution)/shard_map/ppermute | solution.py:124
  205.5 45.2 %collective-permute-start.5 = (bf16[256,1024]{0,1:T(8,128)(2,1)S(1)}, bf16[256,1024]{0,1:T(8,128)(2,1)S(1)}, u32[]{:S(2)}, u32[]{:S(2)}) collective-permute-start(bf16[256,1024]{0,1:T(8,128)(2,1)S(1)} %fusion.33), channel_id=1, source_target_pairs={{0,3},{1,0},{2,1},{3,2},{4,7},{5,4},{6,5},{7,6},{8,11},{9,8},{10,9... | collective-permute-start | bytes 1572872 | tf_op jit(solution)/shard_map/ppermute | solution.py:124
  208.7 44.3 %collective-permute-start.3 = (bf16[256,1024]{0,1:T(8,128)(2,1)S(1)}, bf16[256,1024]{0,1:T(8,128)(2,1)S(1)}, u32[]{:S(2)}, u32[]{:S(2)}) collective-permute-start(bf16[256,1024]{0,1:T(8,128)(2,1)S(1)} %fusion.33), channel_id=1, source_target_pairs={{0,1},{1,2},{2,3},{3,0},{4,5},{5,6},{6,7},{7,4},{8,9},{9,10},{10,1... | collective-permute-start | bytes 1572872 | tf_op jit(solution)/shard_map/ppermute | solution.py:124
Sparse Core Ops, SparseCore 0:
  10.9 134.9 all-gather.1

commit v8 on v6

--- a/solution.py
+++ b/solution.py
@@ -29,12 +29,18 @@
     b_sin = np.sin(inner)
     forward = np.block([[b_cos, -b_sin], [b_sin, b_cos]])
     backward = np.block([[b_cos, b_sin], [-b_sin, b_cos]])
+    half = tokens // 2
+    backward = [
+        np.concatenate([backward[:, h * half : (h + 1) * half], backward[:, tokens + h * half :][:, :half]], 1)
+        for h in range(2)
+    ]
     last = 2.0 * np.pi * ((n1[:, None] * k1[None, :]) % outer) / outer
     last_cos = np.cos(last) / period
     last_sin = -np.sin(last) / period
     as32 = lambda a: jnp.asarray(a, jnp.float32)
-    tables = (first_table, twist_cos, twist_sin, forward, backward, last_cos, last_sin)
-    return tuple(as32(a) for a in tables)
+    tables = (first_table, twist_cos, twist_sin, forward, *backward, last_cos, last_sin)
+    first_table, twist_cos, twist_sin, forward, back_0, back_1, last_cos, last_sin = map(as32, tables)
+    return first_table, twist_cos, twist_sin, forward, (back_0, back_1), last_cos, last_sin
 
 
 def dot(a, b):
@@ -56,13 +62,19 @@
     p_real = u_real * f_real - u_imag * f_imag
     p_imag = u_real * f_imag + u_imag * f_real
     product = jnp.concatenate([p_real, p_imag], -1).reshape(outer * per_device, 2 * tokens)
-    q = dot(product, backward).reshape(outer, per_device, 2 * tokens)
-    q_real, q_imag = q[..., :tokens], q[..., tokens:]
-    r_real = q_real * twist_cos - q_imag * twist_sin
-    r_imag = q_real * twist_sin + q_imag * twist_cos
-    flat = (outer, per_device * tokens)
-    result = dot(last_cos, r_real.reshape(flat)) + dot(last_sin, r_imag.reshape(flat))
-    return result.reshape(blocks, per_device, tokens).astype(jnp.bfloat16)
+    half = tokens // 2
+    halves = []
+    for h, table in enumerate(backward):
+        q = dot(product, table).reshape(outer, per_device, 2 * half)
+        q_real, q_imag = q[..., :half], q[..., half:]
+        t_cos = twist_cos[..., h * half : (h + 1) * half]
+        t_sin = twist_sin[..., h * half : (h + 1) * half]
+        r_real = q_real * t_cos - q_imag * t_sin
+        r_imag = q_real * t_sin + q_imag * t_cos
+        flat = (outer, per_device * half)
+        result = dot(last_cos, r_real.reshape(flat)) + dot(last_sin, r_imag.reshape(flat))
+        halves.append(result.reshape(blocks, per_device, half).astype(jnp.bfloat16))
+    return halves
 
 
 def causal_short(rows, tail, taps):
@@ -90,12 +102,18 @@
     outgoing = jnp.concatenate([gated_cols, filter_cols], 1)
     pieces = lax.all_to_all(outgoing, "seq", split_axis=0, concat_axis=0, tiled=True)
     mixed = long_conv(pieces, per_device, tables)
-    returned = lax.all_to_all(mixed, "seq", split_axis=0, concat_axis=0, tiled=True)
-    conv = returned.reshape(channels, tokens_here).T
-    inner = (query_mix * (conv.astype(jnp.float32) + skip_gain * gated.astype(jnp.float32))).astype(
-        jnp.bfloat16
-    )
-    return projection(inner, weights).astype(jnp.bfloat16)
+    half = tokens_here // 2
+    outputs = []
+    for h, piece in enumerate(mixed):
+        back = lax.all_to_all(piece, "seq", split_axis=0, concat_axis=0, tiled=True)
+        rows = slice(h * half, (h + 1) * half)
+        parts = (back, query_mix[rows], gated[rows], skip_gain)
+        back, mix, skip, gain = lax.optimization_barrier(parts)
+        conv = back.reshape(channels, half).T.astype(jnp.float32)
+        skip = gain * skip.astype(jnp.float32)
+        inner = (mix * (conv + skip)).astype(jnp.bfloat16)
+        outputs.append(projection(inner, weights).astype(jnp.bfloat16))
+    return jnp.concatenate(outputs, 0)
 
 
 def projection(inner, weights):
@@ -125,6 +143,4 @@
         P("tp"),
         P("seq", "tp"),
     )
-    return jax.shard_map(
-        block, mesh=mesh, in_specs=placed, out_specs=P("seq", "tp"), check_vma=False
-    )
+    return jax.shard_map(block, mesh=mesh, in_specs=placed, out_specs=P("seq", "tp"), check_vma=False)

time: 204 us -> 204 us (level)
  the two profiles are of different devices: /device:TPU:33 before, /device:TPU:1 now
where the time goes in v8:
time: 204 us; the launch traced here: 201 us
  starting transfers between devices  85.2 us (42%)
  waiting for transfers between devices  43.6 us (21%)
  matrix products  29.2 us (14%)
  local copies, waits for them, and re-layouts  18.3 us (9%)
  between operations  14 us (7%)
  other arithmetic  10.3 us (5%)
    ppermute x6, starting transfers between devices, projection(): lax.ppermute(inner, 'tp', [(j, (j + k) % size) for j in range(size)])  45.2 us
    dot_general x8, matrix products, dot(): jnp.dot(a, b, precision=TRANSFORM_PRECISION, preferred_element_type=jnp.f...  20.1 us
    ppermute x6, waiting for transfers between devices, projection(): lax.ppermute(inner, 'tp', [(j, (j + k) % size) for j in range(size)])  18.7 us
    all_to_all x1, starting transfers between devices, block(): lax.all_to_all(outgoing, 'seq', split_axis=0, concat_axis=0, tiled=True)  17.1 us
    all_to_all x2, starting transfers between devices, block(): back = lax.all_to_all(piece, 'seq', split_axis=0, concat_axis=0, tiled=True)  12.8 us
    ppermute x3, starting transfers between devices, shifted(): return lax.ppermute(value, axis, pairs)  10 us
    ppermute x3, waiting for transfers between devices, shifted(): return lax.ppermute(value, axis, pairs)  8.98 us
    all_to_all x2, waiting for transfers between devices, block(): back = lax.all_to_all(piece, 'seq', split_axis=0, concat_axis=0, tiled=True)  8.95 us
  transfers between devices with their start and end apart: 13, of which 4 were waited for; matrix products, arithmetic and copies ran while one was open for 28% of the time, Pallas kernels for 0%

profile of v8, /device:TPU:1, one launch (start us, length us, event | category | flops | bytes accessed | tf_op | source)
XLA Modules:
  0.0 200.5 jit_solution(6264061272570860310)
XLA Ops:
  6.5 0.7 all-gather.2.cloned.1.call-update
  7.3 0.7 slice.133
  8.0 0.2 copy.23
  8.2 4.6 %collective-permute-start = (bf16[2,1024]{0,1:T(8,128)(2,1)S(1)}, bf16[2,1024]{0,1:T(8,128)(2,1)S(1)}, u32[]{:S(2)}, u32[]{:S(2)}) collective-permute-start(bf16[2,1024]{0,1:T(8,128)(2,1)S(1)} %copy.23), channel_id=1, source_target_pairs={{0,4},{4,8},{8,12},{12,16},{16,20},{20,24},{24,28},{28,32},{32,36}... | collective-permute-start | bytes 12296 | tf_op jit(solution)/shard_map/ppermute | solution.py:13
  12.8 0.7 slice.139
  13.5 0.2 copy.26
  13.7 1.9 collective-permute-start.1
  15.6 0.9 fusion.75
  16.6 1.2 copy.22
  17.8 1.3 copy.25
  19.1 1.2 copy.28
  20.4 1.9 multiply_convert_fusion
  22.3 1.1 pad_maximum_fusion.3
  23.4 17.1 %all-to-all-start = ((bf16[64,32,256]{2,1,0:T(8,128)(2,1)}), bf16[64,32,256]{2,1,0:T(8,128)(2,1)S(1)}, u32[]{:S(2)}, u32[]{:S(2)}) async-start(bf16[64,32,256]{2,1,0:T(8,128)(2,1)} %pad_maximum_fusion.3), calls=%async_computation | async-start | bytes 2097152 | tf_op jit(solution)/shard_map/all_to_all | solution.py:103
  40.6 0.2 copy.36
  40.8 3.5 %collective-permute-start.2 = (bf16[2,1024]{0,1:T(8,128)(2,1)S(1)}, bf16[2,1024]{0,1:T(8,128)(2,1)S(1)}, u32[]{:S(2)}, u32[]{:S(2)}) collective-permute-start(bf16[2,1024]{0,1:T(8,128)(2,1)S(1)} %copy.36), channel_id=1, source_target_pairs={{0,4},{4,8},{8,12},{12,16},{16,20},{20,24},{24,28},{28,32},{32,36}... | collective-permute-start | bytes 12296 | tf_op jit(solution)/shard_map/ppermute | solution.py:13
  44.4 0.2 copy.35
  44.6 0.8 fusion.74
  45.5 9.0 %collective-permute-done.2 = bf16[2,1024]{0,1:T(8,128)(2,1)S(1)} collective-permute-done((bf16[2,1024]{0,1:T(8,128)(2,1)S(1)}, bf16[2,1024]{0,1:T(8,128)(2,1)S(1)}, u32[]{:S(2)}, u32[]{:S(2)}) %collective-permute-start.2) | collective-permute-done | bytes 4128 | tf_op jit(solution)/shard_map/ppermute | solution.py:13
  54.4 1.1 multiply_add_fusion.2
  55.5 6.3 %all-to-all-done = bf16[64,32,256]{2,1,0:T(8,128)(2,1)S(1)} async-done(((bf16[64,32,256]{2,1,0:T(8,128)(2,1)}), bf16[64,32,256]{2,1,0:T(8,128)(2,1)S(1)}, u32[]{:S(2)}, u32[]{:S(2)}) %all-to-all-start) | async-done | bytes 1048608 | tf_op jit(solution)/shard_map/all_to_all | solution.py:103
  61.8 0.6 copy.42
  62.5 2.3 %fusion.76 = f32[256,8192]{1,0:T(8,128)S(1)} fusion(f32[256,64]{1,0:T(8,128)S(1)} %copy-done.9, bf16[64,8192]{1,0:T(8,128)(2,1)S(1)} %bitcast.94), kind=kOutput, calls=%fused_computation.88 | convolution fusion | flops 805306368 | bytes 9502720 | tf_op jit(solution)/shard_map/dot_general | solution.py:47
  64.8 0.9 fusion.72
  65.7 0.0 copy-done.8
  65.8 1.2 fusion.4
  67.0 7.2 %fusion = f32[128,32,512]{2,0,1:T(8,128)S(1)} fusion(f32[512,512,1]{1,0,2:T(8,128)S(1)} %copy-done.2, f32[128,32,256]{2,0,1:T(8,128)S(1)} %get-tuple-element.22, f32[128,32,256]{2,0,1:T(8,128)S(1)} %get-tuple-element.21), kind=kOutput, calls=%fused_computation | convolution fusion | flops 6444548096 | bytes 17825792 | tf_op jit(solution)/shard_map/dot_general | solution.py:47
  74.2 0.8 multiply_subtract_fusion
  75.0 0.2 copy-done.6
  75.2 1.9 fusion.7
  77.2 1.6 multiply_add_fusion.3
  78.8 2.6 %copy.33 = f32[128,16,128]{0,2,1:T(8,128)} copy(f32[128,16,128]{2,0,1:T(8,128)} %get-tuple-element.28) | data formatting | bytes 2097152 | tf_op jit(solution)/shard_map/sub | solution.py:72
  81.4 2.5 %copy.34 = f32[128,16,128]{0,2,1:T(8,128)} copy(f32[128,16,128]{2,0,1:T(8,128)} %get-tuple-element.27) | data formatting | bytes 2097152 | tf_op jit(solution)/shard_map/add | solution.py:73
  83.9 1.9 fusion.77
  85.8 1.9 fusion.51
  87.7 0.8 copy.43
  88.5 8.4 %all-to-all-start.1 = ((bf16[64,16,128]{2,1,0:T(8,128)(2,1)}), bf16[64,16,128]{2,1,0:T(8,128)(2,1)S(1)}, u32[]{:S(2)}, u32[]{:S(2)}) async-start(bf16[64,16,128]{2,1,0:T(8,128)(2,1)} %bitcast.101), calls=%async_computation.1 | async-start | bytes 524288 | tf_op jit(solution)/shard_map/all_to_all | solution.py:108
  96.9 3.6 %fusion.6 = f32[128,16,256]{2,0,1:T(8,128)S(1)} fusion(f32[512,256,1]{1,0,2:T(8,128)} %constant.81, f32[128,16,256]{2,0,1:T(8,128)} %copy-done.1, f32[128,16,256]{2,0,1:T(8,128)S(1)} %get-tuple-element.23), kind=kOutput, calls=%fused_computation.11 | convolution fusion | flops 1611661312 | bytes 6815744 | tf_op jit(solution)/shard_map/dot_general | solution.py:47
  100.5 1.3 multiply_add_fusion.1
  101.8 0.3 copy.38
  102.1 1.6 copy.39
  103.7 0.7 fusion.78
  104.4 0.7 fusion.50
  105.1 0.8 copy.44
  105.8 8.9 %all-to-all-done.1 = bf16[64,16,128]{2,1,0:T(8,128)(2,1)S(1)} async-done(((bf16[64,16,128]{2,1,0:T(8,128)(2,1)}), bf16[64,16,128]{2,1,0:T(8,128)(2,1)S(1)}, u32[]{:S(2)}, u32[]{:S(2)}) %all-to-all-start.1) | async-done | bytes 262176 | tf_op jit(solution)/shard_map/all_to_all | solution.py:108
  114.8 4.4 %all-to-all-start.2 = ((bf16[64,16,128]{2,1,0:T(8,128)(2,1)}), bf16[64,16,128]{2,1,0:T(8,128)(2,1)S(1)}, u32[]{:S(2)}, u32[]{:S(2)}) async-start(bf16[64,16,128]{2,1,0:T(8,128)(2,1)} %bitcast.39), calls=%async_computation.2 | async-start | bytes 524288 | tf_op jit(solution)/shard_map/all_to_all | solution.py:108
  119.2 0.1 fusion.73
  119.3 0.2 fusion.60
  119.5 28.1 %collective-permute-start.4 = (bf16[128,1024]{0,1:T(8,128)(2,1)S(1)}, bf16[128,1024]{0,1:T(8,128)(2,1)S(1)}, u32[]{:S(2)}, u32[]{:S(2)}) collective-permute-start(bf16[128,1024]{0,1:T(8,128)(2,1)S(1)} %fusion.60), channel_id=1, source_target_pairs={{0,2},{1,3},{2,0},{3,1},{4,6},{5,7},{6,4},{7,5},{8,10},{9,11},{10,... | collective-permute-start | bytes 786440 | tf_op jit(solution)/shard_map/ppermute | solution.py:128
  147.6 1.6 collective-permute-start.5
  149.2 0.2 fusion.57
  149.4 13.8 %collective-permute-start.7 = (bf16[128,1024]{0,1:T(8,128)(2,1)S(1)}, bf16[128,1024]{0,1:T(8,128)(2,1)S(1)}, u32[]{:S(2)}, u32[]{:S(2)}) collective-permute-start(bf16[128,1024]{0,1:T(8,128)(2,1)S(1)} %fusion.57), channel_id=1, source_target_pairs={{0,2},{1,3},{2,0},{3,1},{4,6},{5,7},{6,4},{7,5},{8,10},{9,11},{10,... | collective-permute-start | bytes 786440 | tf_op jit(solution)/shard_map/ppermute | solution.py:128
  163.3 1.5 collective-permute-start.8
  164.8 2.2 %fusion.24 = f32[128,1024]{1,0:T(8,128)S(1)} fusion(bf16[128,1024]{0,1:T(8,128)(2,1)S(1)} %fusion.60, bf16[4096,1024]{1,0:T(8,128)(2,1)} %all-gather.2.cloned.1.call-done, s32[]{:T(128)S(6)} %select_n.37), kind=kOutput, calls=%fused_computation.33 | convolution fusion | flops 268435456 | bytes 2883588 | tf_op jit(solution)/shard_map/dot_general | solution.py:130
  167.0 2.5 %fusion.22 = f32[128,1024]{1,0:T(8,128)S(1)} fusion(bf16[128,1024]{0,1:T(8,128)(2,1)S(1)} %fusion.57, bf16[4096,1024]{1,0:T(8,128)(2,1)} %all-gather.2.cloned.1.call-done, s32[]{:T(128)S(6)} %select_n.37), kind=kOutput, calls=%fused_computation.31 | convolution fusion | flops 268435456 | bytes 2883588 | tf_op jit(solution)/shard_map/dot_general | solution.py:130
  169.6 0.1 collective-permute-start.6
  169.7 2.1 %fusion.16 = f32[128,1024]{1,0:T(8,128)S(1)} fusion(bf16[128,1024]{0,1:T(8,128)(2,1)S(1)} %collective-permute-done.4, bf16[4096,1024]{1,0:T(8,128)(2,1)} %all-gather.2.cloned.1.call-done, s32[]{:T(128)S(6)} %select_n.41), kind=kOutput, calls=%fused_computation.25 | convolution fusion | flops 268435456 | bytes 2883588 | tf_op jit(solution)/shard_map/dot_general | solution.py:132
  171.7 18.7 %collective-permute-done.7 = bf16[128,1024]{0,1:T(8,128)(2,1)S(1)} collective-permute-done((bf16[128,1024]{0,1:T(8,128)(2,1)S(1)}, bf16[128,1024]{0,1:T(8,128)(2,1)S(1)}, u32[]{:S(2)}, u32[]{:S(2)}) %collective-permute-start.7) | collective-permute-done | bytes 262176 | tf_op jit(solution)/shard_map/ppermute | solution.py:128
  190.4 0.5 fusion.14
  190.9 0.5 fusion.12
  191.4 0.5 fusion.10
  191.8 0.5 fusion.44
  192.3 0.5 fusion.47
  192.8 0.8 pad_maximum_fusion.7
  (44 shorter events, 0.1 us)
Async XLA Ops:
  6.5 158.3 %all-gather.2.cloned.1.call-start = ((), (), s32[]{:S(2)}) async-start(), calls=%async_computation.3 | async-start | bytes 8519680 | tf_op jit(solution)/shard_map/all_gather | solution.py:94
  8.2 12.2 %collective-permute-start = (bf16[2,1024]{0,1:T(8,128)(2,1)S(1)}, bf16[2,1024]{0,1:T(8,128)(2,1)S(1)}, u32[]{:S(2)}, u32[]{:S(2)}) collective-permute-start(bf16[2,1024]{0,1:T(8,128)(2,1)S(1)} %copy.23), channel_id=1, source_target_pairs={{0,4},{4,8},{8,12},{12,16},{16,20},{20,24},{24,28},{28,32},{32,36}... | collective-permute-start | bytes 12296 | tf_op jit(solution)/shard_map/ppermute | solution.py:13
  13.7 6.7 %collective-permute-start.1 = (bf16[2,1024]{0,1:T(8,128)(2,1)S(1)}, bf16[2,1024]{0,1:T(8,128)(2,1)S(1)}, u32[]{:S(2)}, u32[]{:S(2)}) collective-permute-start(bf16[2,1024]{0,1:T(8,128)(2,1)S(1)} %copy.26), channel_id=1, source_target_pairs={{0,4},{4,8},{8,12},{12,16},{16,20},{20,24},{24,28},{28,32},{32,36}... | collective-permute-start | bytes 12296 | tf_op jit(solution)/shard_map/ppermute | solution.py:13
  17.8 22.8 %copy-start.5 = (bf16[256,1024]{1,0:T(8,128)(2,1)S(1)}, bf16[256,1024]{1,0:T(8,128)(2,1)}, u32[]{:S(2)}) copy-start(bf16[256,1024]{1,0:T(8,128)(2,1)} %param.15) | copy-start | bytes 1572868
  23.4 39.0 %copy-start.9 = (f32[256,64]{1,0:T(8,128)S(1)}, f32[256,64]{1,0:T(8,128)}, u32[]{:S(2)}) copy-start(f32[256,64]{1,0:T(8,128)} %constant.61.clone) | copy-start | bytes 196612
  23.4 38.4 %all-to-all-start = ((bf16[64,32,256]{2,1,0:T(8,128)(2,1)}), bf16[64,32,256]{2,1,0:T(8,128)(2,1)S(1)}, u32[]{:S(2)}, u32[]{:S(2)}) async-start(bf16[64,32,256]{2,1,0:T(8,128)(2,1)} %pad_maximum_fusion.3), calls=%async_computation | async-start | bytes 2097152 | tf_op jit(solution)/shard_map/all_to_all | solution.py:103
  40.8 13.6 %collective-permute-start.2 = (bf16[2,1024]{0,1:T(8,128)(2,1)S(1)}, bf16[2,1024]{0,1:T(8,128)(2,1)S(1)}, u32[]{:S(2)}, u32[]{:S(2)}) collective-permute-start(bf16[2,1024]{0,1:T(8,128)(2,1)S(1)} %copy.36), channel_id=1, source_target_pairs={{0,4},{4,8},{8,12},{12,16},{16,20},{20,24},{24,28},{28,32},{32,36}... | collective-permute-start | bytes 12296 | tf_op jit(solution)/shard_map/ppermute | solution.py:13
  64.8 0.9 copy-start.7
  64.8 1.0 copy-start.8
  65.8 1.3 copy-start.2
  74.2 1.0 copy-start.6
  75.0 3.8 %copy-start.1 = (f32[128,16,256]{2,0,1:T(8,128)}, f32[128,16,256]{2,0,1:T(8,128)S(1)}, u32[]{:S(2)}) copy-start(f32[128,16,256]{2,0,1:T(8,128)S(1)} %get-tuple-element.24) | copy-start | bytes 6291460
  75.0 2.1 %copy-start.14 = (f32[128,128]{1,0:T(8,128)S(1)}, f32[128,128]{1,0:T(8,128)}, u32[]{:S(2)}) copy-start(f32[128,128]{1,0:T(8,128)} %constant.72) | copy-start | bytes 196612
  75.0 2.1 %copy-start.15 = (f32[128,128]{1,0:T(8,128)S(1)}, f32[128,128]{1,0:T(8,128)}, u32[]{:S(2)}) copy-start(f32[128,128]{1,0:T(8,128)} %constant.74) | copy-start | bytes 196612
  77.2 6.8 %copy-start.11 = (f32[64,128]{1,0:T(8,128)S(1)}, f32[64,128]{1,0:T(8,128)}, u32[]{:S(2)}) copy-start(f32[64,128]{1,0:T(8,128)} %constant.67.clone) | copy-start | bytes 98308
  77.2 8.6 %copy-start.10 = (f32[64,128]{1,0:T(8,128)S(1)}, f32[64,128]{1,0:T(8,128)}, u32[]{:S(2)}) copy-start(f32[64,128]{1,0:T(8,128)} %constant.68.clone) | copy-start | bytes 98308
  87.7 12.8 %copy-start.12 = (f32[128,128]{1,0:T(8,128)S(1)}, f32[128,128]{1,0:T(8,128)}, u32[]{:S(2)}) copy-start(f32[128,128]{1,0:T(8,128)} %constant.76) | copy-start | bytes 196612
  88.5 26.3 %all-to-all-start.1 = ((bf16[64,16,128]{2,1,0:T(8,128)(2,1)}), bf16[64,16,128]{2,1,0:T(8,128)(2,1)S(1)}, u32[]{:S(2)}, u32[]{:S(2)}) async-start(bf16[64,16,128]{2,1,0:T(8,128)(2,1)} %bitcast.101), calls=%async_computation.1 | async-start | bytes 524288 | tf_op jit(solution)/shard_map/all_to_all | solution.py:108
  96.9 3.6 %copy-start.13 = (f32[128,128]{1,0:T(8,128)S(1)}, f32[128,128]{1,0:T(8,128)}, u32[]{:S(2)}) copy-start(f32[128,128]{1,0:T(8,128)} %constant.78) | copy-start | bytes 196612
  102.1 17.2 %copy-start.16 = (f32[1024]{0:T(1024)S(1)}, f32[1024]{0:T(1024)}, u32[]{:S(2)}) copy-start(f32[1024]{0:T(1024)} %param.20) | copy-start | bytes 12292
  104.4 14.9 %copy-start.4 = (bf16[128,1024]{0,1:T(8,128)(2,1)S(1)}, bf16[128,1024]{0,1:T(8,128)(2,1)}, u32[]{:S(2)}) copy-start(bf16[128,1024]{0,1:T(8,128)(2,1)} %get-tuple-element.16) | copy-start | bytes 786436
  104.4 44.8 %copy-start.3 = (bf16[128,1024]{0,1:T(8,128)(2,1)S(1)}, bf16[128,1024]{0,1:T(8,128)(2,1)}, u32[]{:S(2)}) copy-start(bf16[128,1024]{0,1:T(8,128)(2,1)} %get-tuple-element.20) | copy-start | bytes 786436
  114.8 34.4 %all-to-all-start.2 = ((bf16[64,16,128]{2,1,0:T(8,128)(2,1)}), bf16[64,16,128]{2,1,0:T(8,128)(2,1)S(1)}, u32[]{:S(2)}, u32[]{:S(2)}) async-start(bf16[64,16,128]{2,1,0:T(8,128)(2,1)} %bitcast.39), calls=%async_computation.2 | async-start | bytes 524288 | tf_op jit(solution)/shard_map/all_to_all | solution.py:108
  119.5 50.1 %collective-permute-start.4 = (bf16[128,1024]{0,1:T(8,128)(2,1)S(1)}, bf16[128,1024]{0,1:T(8,128)(2,1)S(1)}, u32[]{:S(2)}, u32[]{:S(2)}) collective-permute-start(bf16[128,1024]{0,1:T(8,128)(2,1)S(1)} %fusion.60), channel_id=1, source_target_pairs={{0,2},{1,3},{2,0},{3,1},{4,6},{5,7},{6,4},{7,5},{8,10},{9,11},{10,... | collective-permute-start | bytes 786440 | tf_op jit(solution)/shard_map/ppermute | solution.py:128
  147.6 43.3 %collective-permute-start.5 = (bf16[128,1024]{0,1:T(8,128)(2,1)S(1)}, bf16[128,1024]{0,1:T(8,128)(2,1)S(1)}, u32[]{:S(2)}, u32[]{:S(2)}) collective-permute-start(bf16[128,1024]{0,1:T(8,128)(2,1)S(1)} %fusion.60), channel_id=1, source_target_pairs={{0,3},{1,0},{2,1},{3,2},{4,7},{5,4},{6,5},{7,6},{8,11},{9,8},{10,9... | collective-permute-start | bytes 786440 | tf_op jit(solution)/shard_map/ppermute | solution.py:128
  149.2 42.6 %collective-permute-start.3 = (bf16[128,1024]{0,1:T(8,128)(2,1)S(1)}, bf16[128,1024]{0,1:T(8,128)(2,1)S(1)}, u32[]{:S(2)}, u32[]{:S(2)}) collective-permute-start(bf16[128,1024]{0,1:T(8,128)(2,1)S(1)} %fusion.60), channel_id=1, source_target_pairs={{0,1},{1,2},{2,3},{3,0},{4,5},{5,6},{6,7},{7,4},{8,9},{9,10},{10,1... | collective-permute-start | bytes 786440 | tf_op jit(solution)/shard_map/ppermute | solution.py:128
  149.4 41.0 %collective-permute-start.7 = (bf16[128,1024]{0,1:T(8,128)(2,1)S(1)}, bf16[128,1024]{0,1:T(8,128)(2,1)S(1)}, u32[]{:S(2)}, u32[]{:S(2)}) collective-permute-start(bf16[128,1024]{0,1:T(8,128)(2,1)S(1)} %fusion.57), channel_id=1, source_target_pairs={{0,2},{1,3},{2,0},{3,1},{4,6},{5,7},{6,4},{7,5},{8,10},{9,11},{10,... | collective-permute-start | bytes 786440 | tf_op jit(solution)/shard_map/ppermute | solution.py:128
  163.3 28.1 %collective-permute-start.8 = (bf16[128,1024]{0,1:T(8,128)(2,1)S(1)}, bf16[128,1024]{0,1:T(8,128)(2,1)S(1)}, u32[]{:S(2)}, u32[]{:S(2)}) collective-permute-start(bf16[128,1024]{0,1:T(8,128)(2,1)S(1)} %fusion.57), channel_id=1, source_target_pairs={{0,3},{1,0},{2,1},{3,2},{4,7},{5,4},{6,5},{7,6},{8,11},{9,8},{10,9... | collective-permute-start | bytes 786440 | tf_op jit(solution)/shard_map/ppermute | solution.py:128
  164.8 25.6 %copy-start = (bf16[4096,1024]{1,0:T(8,128)(2,1)S(1)}, bf16[4096,1024]{1,0:T(8,128)(2,1)}, u32[]{:S(2)}) copy-start(bf16[4096,1024]{1,0:T(8,128)(2,1)} %all-gather.2.cloned.1.call-done) | copy-start | bytes 25165828
  169.6 22.8 %collective-permute-start.6 = (bf16[128,1024]{0,1:T(8,128)(2,1)S(1)}, bf16[128,1024]{0,1:T(8,128)(2,1)S(1)}, u32[]{:S(2)}, u32[]{:S(2)}) collective-permute-start(bf16[128,1024]{0,1:T(8,128)(2,1)S(1)} %fusion.57), channel_id=1, source_target_pairs={{0,1},{1,2},{2,3},{3,0},{4,5},{5,6},{6,7},{7,4},{8,9},{9,10},{10,1... | collective-permute-start | bytes 786440 | tf_op jit(solution)/shard_map/ppermute | solution.py:128
Sparse Core Ops, SparseCore 0:
  10.9 142.5 all-gather.1

commit v9 on v6

--- a/solution.py
+++ b/solution.py
@@ -33,7 +33,11 @@
     last_cos = np.cos(last) / period
     last_sin = -np.sin(last) / period
     as32 = lambda a: jnp.asarray(a, jnp.float32)
-    tables = (first_table, twist_cos, twist_sin, forward, backward, last_cos, last_sin)
+    twist_cos_t = np.cos(twist).T[None]
+    twist_sin_t = np.sin(twist).T[None]
+    tables = (
+        first_table, twist_cos, twist_sin, forward, backward.T, twist_cos_t, twist_sin_t, last_cos, last_sin
+    )
     return tuple(as32(a) for a in tables)
 
 
@@ -41,8 +45,12 @@
     return jnp.dot(a, b, precision=TRANSFORM_PRECISION, preferred_element_type=jnp.float32)
 
 
+def einsum(form, a, b):
+    return jnp.einsum(form, a, b, precision=TRANSFORM_PRECISION, preferred_element_type=jnp.float32)
+
+
 def long_conv(pieces, per_device, tables):
-    first_table, twist_cos, twist_sin, forward, backward, last_cos, last_sin = tables
+    first_table, twist_cos, twist_sin, forward, backward, back_cos, back_sin, last_cos, last_sin = tables
     blocks, both, tokens = pieces.shape
     outer = 2 * blocks
     spec = dot(first_table, pieces.reshape(blocks, both * tokens)).reshape(2, outer, both, tokens)
@@ -55,14 +63,13 @@
     f_real, f_imag = u[:, per_device:, :tokens], u[:, per_device:, tokens:]
     p_real = u_real * f_real - u_imag * f_imag
     p_imag = u_real * f_imag + u_imag * f_real
-    product = jnp.concatenate([p_real, p_imag], -1).reshape(outer * per_device, 2 * tokens)
-    q = dot(product, backward).reshape(outer, per_device, 2 * tokens)
-    q_real, q_imag = q[..., :tokens], q[..., tokens:]
-    r_real = q_real * twist_cos - q_imag * twist_sin
-    r_imag = q_real * twist_sin + q_imag * twist_cos
-    flat = (outer, per_device * tokens)
-    result = dot(last_cos, r_real.reshape(flat)) + dot(last_sin, r_imag.reshape(flat))
-    return result.reshape(blocks, per_device, tokens).astype(jnp.bfloat16)
+    product = jnp.concatenate([p_real, p_imag], -1)
+    q = einsum("nq,kcq->cnk", backward, product)
+    q_real, q_imag = q[:, :tokens], q[:, tokens:]
+    r_real = q_real * back_cos - q_imag * back_sin
+    r_imag = q_real * back_sin + q_imag * back_cos
+    result = einsum("cnk,mk->cnm", r_real, last_cos) + einsum("cnk,mk->cnm", r_imag, last_sin)
+    return result.astype(jnp.bfloat16).transpose(2, 0, 1)
 
 
 def causal_short(rows, tail, taps):
@@ -125,6 +132,4 @@
         P("tp"),
         P("seq", "tp"),
     )
-    return jax.shard_map(
-        block, mesh=mesh, in_specs=placed, out_specs=P("seq", "tp"), check_vma=False
-    )
+    return jax.shard_map(block, mesh=mesh, in_specs=placed, out_specs=P("seq", "tp"), check_vma=False)

time: 204 us -> 198 us (0.971)
  the two profiles are of different devices: /device:TPU:33 before, /device:TPU:63 now
where the time goes in v9:
time: 198 us; the launch traced here: 197 us
  waiting for transfers between devices  75.6 us (38%)
  blocking collectives  40.3 us (20%)
  starting transfers between devices  27.9 us (14%)
  matrix products  24.9 us (13%)
  between operations  13.8 us (7%)
  local copies, waits for them, and re-layouts  9.64 us (5%)
  other arithmetic  5.26 us (3%)
    all_to_all x1, blocking collectives, block(): lax.all_to_all(outgoing, 'seq', split_axis=0, concat_axis=0, tiled=True)  40.3 us
    ppermute x3, waiting for transfers between devices, shifted(): return lax.ppermute(value, axis, pairs)  37 us
    ppermute x3, waiting for transfers between devices, projection(): lax.ppermute(inner, 'tp', [(j, (j + k) % size) for j in range(size)])  30.9 us
    ppermute x3, starting transfers between devices, shifted(): return lax.ppermute(value, axis, pairs)  17.3 us
    dot_general x2, matrix products, dot(): jnp.dot(a, b, precision=TRANSFORM_PRECISION, preferred_element_type=jnp.f...  9.5 us
    all_to_all x1, starting transfers between devices, block(): lax.all_to_all(mixed, 'seq', split_axis=0, concat_axis=0, tiled=True)  7.88 us
    dot_general x3, matrix products, projection(): jnp.dot(chunk, rows_of((here - k) % size), preferred_element_type=jnp.flo...  7.75 us
    all_gather x1, waiting for transfers between devices, block(): weights = lax.all_gather(out_weight, 'seq', axis=0, tiled=True)  6.91 us
  transfers between devices with their start and end apart: 8, of which 6 were waited for; matrix products, arithmetic and copies ran while one was open for 19% of the time, Pallas kernels for 0%

profile of v9, /device:TPU:63, one launch (start us, length us, event | category | flops | bytes accessed | tf_op | source)
XLA Modules:
  0.0 197.3 jit_solution(751187997748330516)
XLA Ops:
  6.5 0.0 all-gather.2.cloned.1.call-start
  6.5 0.7 all-gather.2.cloned.1.call-update
  7.3 0.7 slice.109
  8.0 0.2 copy.44
  8.2 8.1 %collective-permute-start.1 = (bf16[2,1024]{0,1:T(8,128)(2,1)S(1)}, bf16[2,1024]{0,1:T(8,128)(2,1)S(1)}, u32[]{:S(2)}, u32[]{:S(2)}) collective-permute-start(bf16[2,1024]{0,1:T(8,128)(2,1)S(1)} %copy.44), channel_id=1, source_target_pairs={{0,4},{4,8},{8,12},{12,16},{16,20},{20,24},{24,28},{28,32},{32,36}... | collective-permute-start | bytes 12296 | tf_op jit(solution)/shard_map/ppermute | solution.py:13
  16.3 0.7 slice.115
  17.0 0.2 copy.47
  17.2 1.9 collective-permute-start.2
  19.1 0.9 fusion.71
  20.0 1.2 copy.43
  21.3 1.2 copy.46
  22.5 1.2 copy.49
  23.8 1.4 collective-permute-done.1
  25.2 3.7 %collective-permute-done.2 = bf16[2,1024]{0,1:T(8,128)(2,1)S(1)} collective-permute-done((bf16[2,1024]{0,1:T(8,128)(2,1)S(1)}, bf16[2,1024]{0,1:T(8,128)(2,1)S(1)}, u32[]{:S(2)}, u32[]{:S(2)}) %collective-permute-start.2) | collective-permute-done | bytes 4128 | tf_op jit(solution)/shard_map/ppermute | solution.py:13
  28.9 0.0 copy-start.6
  28.9 1.9 multiply_convert_fusion
  30.8 0.1 pad_maximum_fusion
  30.9 40.3 %all_to_all.10 = bf16[64,32,256]{2,1,0:T(8,128)(2,1)S(1)} all-to-all(bf16[64,32,256]{2,1,0:T(8,128)(2,1)S(1)} %pad_maximum_fusion), channel_id=1, replica_groups=mesh['seq'=64,'tp'=4] {'seq'}, dimensions={0} | all-to-all | bytes 2097152 | tf_op jit(solution)/shard_map/all_to_all | solution.py:98
  71.1 0.6 copy.61
  71.8 0.0 copy-done.6
  71.8 2.3 %fusion.72 = f32[256,8192]{1,0:T(8,128)S(1)} fusion(f32[256,64]{1,0:T(8,128)S(1)} %copy-done.6, bf16[64,8192]{1,0:T(8,128)(2,1)S(1)} %bitcast.64), kind=kOutput, calls=%fused_computation.74 | convolution fusion | flops 805306368 | bytes 9502720 | tf_op jit(solution)/shard_map/dot_general | solution.py:45
  74.1 0.0 copy-start.4
  74.1 0.0 copy-start.5
  74.1 0.9 fusion.70
  75.0 0.0 copy-done.4
  75.1 0.0 copy-done.5
  75.1 1.2 fusion.4
  76.3 0.0 copy-done
  76.4 7.2 %fusion = f32[128,32,512]{2,0,1:T(8,128)S(1)} fusion(f32[512,512,1]{1,0,2:T(8,128)S(1)} %copy-done, f32[128,32,256]{2,0,1:T(8,128)S(1)} %get-tuple-element.6, f32[128,32,256]{2,0,1:T(8,128)S(1)} %get-tuple-element.5), kind=kOutput, calls=%fused_computation | convolution fusion | flops 6444548096 | bytes 17825792 | tf_op jit(solution)/shard_map/dot_general | solution.py:45
  83.5 0.8 multiply_subtract_fusion
  84.3 0.0 copy-start.2
  84.3 0.0 copy-start.3
  84.4 0.0 copy-start.8
  84.4 0.0 copy-start.7
  84.4 3.5 %fusion.10 = f32[16,512,128]{1,2,0:T(8,128)S(1)} fusion(f32[512,512,1]{1,0,2:T(8,128)S(1)} %copy-done, f32[128,16,256]{2,0,1:T(8,128)S(1)} %get-tuple-element.8, f32[128,16,256]{2,0,1:T(8,128)S(1)} %get-tuple-element.7), kind=kOutput, calls=%fused_computation.14 | convolution fusion | flops 3222274048 | bytes 9437184 | tf_op jit(solution)/shard_map/nq,kcq->cnk/dot_general | solution.py:49
  87.9 0.0 copy-done.2
  87.9 0.0 copy-done.3
  87.9 0.0 copy-done.8
  87.9 0.0 copy-start.1
  87.9 0.9 fusion.21
  88.8 0.0 copy-done.7
  88.8 0.0 copy-start.9
  88.8 0.9 fusion.51
  89.8 1.1 copy.56
  90.9 7.9 %all-to-all-start.1 = ((bf16[64,16,256]{2,1,0:T(8,128)(2,1)}), bf16[64,16,256]{2,1,0:T(8,128)(2,1)S(1)}, u32[]{:S(2)}, u32[]{:S(2)}) async-start(bf16[64,16,256]{2,1,0:T(8,128)(2,1)} %copy.56), calls=%async_computation.1 | async-start | bytes 1048576 | tf_op jit(solution)/shard_map/all_to_all | solution.py:100
  98.8 0.0 copy-done.1
  98.8 0.2 copy.41
  99.0 7.3 %collective-permute-start = (bf16[2,1024]{0,1:T(8,128)(2,1)S(1)}, bf16[2,1024]{0,1:T(8,128)(2,1)S(1)}, u32[]{:S(2)}, u32[]{:S(2)}) collective-permute-start(bf16[2,1024]{0,1:T(8,128)(2,1)S(1)} %copy.41), channel_id=1, source_target_pairs={{0,4},{4,8},{8,12},{12,16},{16,20},{20,24},{24,28},{28,32},{32,36}... | collective-permute-start | bytes 12296 | tf_op jit(solution)/shard_map/ppermute | solution.py:13
  106.3 0.2 copy.40
  106.5 32.0 %collective-permute-done = bf16[2,1024]{0,1:T(8,128)(2,1)S(1)} collective-permute-done((bf16[2,1024]{0,1:T(8,128)(2,1)S(1)}, bf16[2,1024]{0,1:T(8,128)(2,1)S(1)}, u32[]{:S(2)}, u32[]{:S(2)}) %collective-permute-start) | collective-permute-done | bytes 4128 | tf_op jit(solution)/shard_map/ppermute | solution.py:13
  138.5 0.0 all-to-all-done.1
  138.5 0.0 copy-done.9
  138.5 1.3 fusion.56
  139.7 0.1 collective-permute-start.4
  139.9 2.7 %collective-permute-start.5 = (bf16[256,1024]{0,1:T(8,128)(2,1)S(1)}, bf16[256,1024]{0,1:T(8,128)(2,1)S(1)}, u32[]{:S(2)}, u32[]{:S(2)}) collective-permute-start(bf16[256,1024]{0,1:T(8,128)(2,1)S(1)} %fusion.56), channel_id=1, source_target_pairs={{0,3},{1,0},{2,1},{3,2},{4,7},{5,4},{6,5},{7,6},{8,11},{9,8},{10,9... | collective-permute-start | bytes 1572872 | tf_op jit(solution)/shard_map/ppermute | solution.py:117
  142.6 0.0 collective-permute-start.3
  142.6 6.9 %all-gather.2.cloned.1.call-done = bf16[4096,1024]{1,0:T(8,128)(2,1)} async-done(((bf16[64,1024]{1,0:T(8,128)(2,1)}), bf16[4096,1024]{1,0:T(8,128)(2,1)}) %all-gather.2.cloned.1.call-update) | async-done | bytes 8388624 | tf_op jit(solution)/shard_map/all_gather | solution.py:89
  149.5 2.3 %fusion.19 = f32[256,1024]{1,0:T(8,128)S(1)} fusion(bf16[256,1024]{0,1:T(8,128)(2,1)S(1)} %fusion.56, bf16[4096,1024]{1,0:T(8,128)(2,1)} %all-gather.2.cloned.1.call-done, s32[]{:T(128)S(6)} %select_n.27), kind=kOutput, calls=%fused_computation.21 | convolution fusion | flops 536870912 | bytes 3670020 | tf_op jit(solution)/shard_map/dot_general | solution.py:119
  151.8 22.1 %collective-permute-done.4 = bf16[256,1024]{0,1:T(8,128)(2,1)S(1)} collective-permute-done((bf16[256,1024]{0,1:T(8,128)(2,1)S(1)}, bf16[256,1024]{0,1:T(8,128)(2,1)S(1)}, u32[]{:S(2)}, u32[]{:S(2)}) %collective-permute-start.4) | collective-permute-done | bytes 524320 | tf_op jit(solution)/shard_map/ppermute | solution.py:117
  173.8 2.3 %fusion.15 = f32[256,1024]{1,0:T(8,128)S(1)} fusion(bf16[256,1024]{0,1:T(8,128)(2,1)S(1)} %collective-permute-done.4, bf16[4096,1024]{1,0:T(8,128)(2,1)} %all-gather.2.cloned.1.call-done, s32[]{:T(128)S(6)} %select_n.31), kind=kOutput, calls=%fused_computation.17 | convolution fusion | flops 536870912 | bytes 3670020 | tf_op jit(solution)/shard_map/dot_general | solution.py:121
  176.2 8.8 %collective-permute-done.5 = bf16[256,1024]{0,1:T(8,128)(2,1)S(1)} collective-permute-done((bf16[256,1024]{0,1:T(8,128)(2,1)S(1)}, bf16[256,1024]{0,1:T(8,128)(2,1)S(1)}, u32[]{:S(2)}, u32[]{:S(2)}) %collective-permute-start.5) | collective-permute-done | bytes 524320 | tf_op jit(solution)/shard_map/ppermute | solution.py:117
  185.0 2.3 %fusion.13 = f32[256,1024]{1,0:T(8,128)S(1)} fusion(bf16[256,1024]{0,1:T(8,128)(2,1)S(1)} %collective-permute-done.5, bf16[4096,1024]{1,0:T(8,128)(2,1)} %all-gather.2.cloned.1.call-done, s32[]{:T(128)S(6)} %select_n.33), kind=kOutput, calls=%fused_computation.15 | convolution fusion | flops 536870912 | bytes 3670020 | tf_op jit(solution)/shard_map/dot_general | solution.py:121
  187.3 0.0 collective-permute-done.3
  187.3 3.1 %fusion.48 = bf16[256,1024]{1,0:T(8,128)(2,1)} fusion(f32[256,1024]{1,0:T(8,128)S(1)} %fusion.13, f32[256,1024]{1,0:T(8,128)S(1)} %fusion.15, f32[256,1024]{1,0:T(8,128)S(1)} %fusion.19, bf16[256,1024]{0,1:T(8,128)(2,1)S(1)} %collective-permute-done.3, bf16[4096,1024]{1,0:T(8,128)(2,1)} %all-gather.2.cloned.1.call-done, s32[]{:T(128)S(6)} %select_n.29), kind=kOutput, calls=%fused_computation.42 | convolution fusion | flops 537919488 | bytes 6291460 | tf_op jit(solution)/shard_map/dot_general | solution.py:121
  (2 shorter events, 0.0 us)
Async XLA Ops:
  6.5 142.9 %all-gather.2.cloned.1.call-start = ((), (), s32[]{:S(2)}) async-start(), calls=%async_computation.2 | async-start | bytes 8519680 | tf_op jit(solution)/shard_map/all_gather | solution.py:89
  8.2 17.0 %collective-permute-start.1 = (bf16[2,1024]{0,1:T(8,128)(2,1)S(1)}, bf16[2,1024]{0,1:T(8,128)(2,1)S(1)}, u32[]{:S(2)}, u32[]{:S(2)}) collective-permute-start(bf16[2,1024]{0,1:T(8,128)(2,1)S(1)} %copy.44), channel_id=1, source_target_pairs={{0,4},{4,8},{8,12},{12,16},{16,20},{20,24},{24,28},{28,32},{32,36}... | collective-permute-start | bytes 12296 | tf_op jit(solution)/shard_map/ppermute | solution.py:13
  17.2 11.7 %collective-permute-start.2 = (bf16[2,1024]{0,1:T(8,128)(2,1)S(1)}, bf16[2,1024]{0,1:T(8,128)(2,1)S(1)}, u32[]{:S(2)}, u32[]{:S(2)}) collective-permute-start(bf16[2,1024]{0,1:T(8,128)(2,1)S(1)} %copy.47), channel_id=1, source_target_pairs={{0,4},{4,8},{8,12},{12,16},{16,20},{20,24},{24,28},{28,32},{32,36}... | collective-permute-start | bytes 12296 | tf_op jit(solution)/shard_map/ppermute | solution.py:13
  28.9 42.9 %copy-start.6 = (f32[256,64]{1,0:T(8,128)S(1)}, f32[256,64]{1,0:T(8,128)}, u32[]{:S(2)}) copy-start(f32[256,64]{1,0:T(8,128)} %constant.55.clone) | copy-start | bytes 196612
  74.1 0.9 copy-start.4
  74.1 1.0 copy-start.5
  75.1 1.3 copy-start
  84.3 3.6 %copy-start.2 = (f32[256,128]{0,1:T(8,128)S(1)}, f32[256,128]{0,1:T(8,128)}, u32[]{:S(2)}) copy-start(f32[256,128]{0,1:T(8,128)} %constant.65) | copy-start | bytes 393220
  84.3 3.6 %copy-start.3 = (f32[256,128]{0,1:T(8,128)S(1)}, f32[256,128]{0,1:T(8,128)}, u32[]{:S(2)}) copy-start(f32[256,128]{0,1:T(8,128)} %constant.66) | copy-start | bytes 393220
  84.4 3.6 %copy-start.8 = (f32[64,128,1]{1,0,2:T(8,128)S(1)}, f32[64,128,1]{1,0,2:T(8,128)}, u32[]{:S(2)}) copy-start(f32[64,128,1]{1,0,2:T(8,128)} %constant.69) | copy-start | bytes 98308
  84.4 4.5 %copy-start.7 = (f32[64,128,1]{1,0,2:T(8,128)S(1)}, f32[64,128,1]{1,0,2:T(8,128)}, u32[]{:S(2)}) copy-start(f32[64,128,1]{1,0,2:T(8,128)} %constant.68) | copy-start | bytes 98308
  87.9 10.8 %copy-start.1 = (bf16[256,1024]{1,0:T(8,128)(2,1)S(1)}, bf16[256,1024]{1,0:T(8,128)(2,1)}, u32[]{:S(2)}) copy-start(bf16[256,1024]{1,0:T(8,128)(2,1)} %param.16) | copy-start | bytes 1572868
  88.8 49.6 %copy-start.9 = (f32[1024]{0:T(1024)S(1)}, f32[1024]{0:T(1024)}, u32[]{:S(2)}) copy-start(f32[1024]{0:T(1024)} %param.21) | copy-start | bytes 12292
  90.9 47.6 %all-to-all-start.1 = ((bf16[64,16,256]{2,1,0:T(8,128)(2,1)}), bf16[64,16,256]{2,1,0:T(8,128)(2,1)S(1)}, u32[]{:S(2)}, u32[]{:S(2)}) async-start(bf16[64,16,256]{2,1,0:T(8,128)(2,1)} %copy.56), calls=%async_computation.1 | async-start | bytes 1048576 | tf_op jit(solution)/shard_map/all_to_all | solution.py:100
  99.0 39.5 %collective-permute-start = (bf16[2,1024]{0,1:T(8,128)(2,1)S(1)}, bf16[2,1024]{0,1:T(8,128)(2,1)S(1)}, u32[]{:S(2)}, u32[]{:S(2)}) collective-permute-start(bf16[2,1024]{0,1:T(8,128)(2,1)S(1)} %copy.41), channel_id=1, source_target_pairs={{0,4},{4,8},{8,12},{12,16},{16,20},{20,24},{24,28},{28,32},{32,36}... | collective-permute-start | bytes 12296 | tf_op jit(solution)/shard_map/ppermute | solution.py:13
  139.7 34.1 %collective-permute-start.4 = (bf16[256,1024]{0,1:T(8,128)(2,1)S(1)}, bf16[256,1024]{0,1:T(8,128)(2,1)S(1)}, u32[]{:S(2)}, u32[]{:S(2)}) collective-permute-start(bf16[256,1024]{0,1:T(8,128)(2,1)S(1)} %fusion.56), channel_id=1, source_target_pairs={{0,2},{1,3},{2,0},{3,1},{4,6},{5,7},{6,4},{7,5},{8,10},{9,11},{10,... | collective-permute-start | bytes 1572872 | tf_op jit(solution)/shard_map/ppermute | solution.py:117
  139.9 45.1 %collective-permute-start.5 = (bf16[256,1024]{0,1:T(8,128)(2,1)S(1)}, bf16[256,1024]{0,1:T(8,128)(2,1)S(1)}, u32[]{:S(2)}, u32[]{:S(2)}) collective-permute-start(bf16[256,1024]{0,1:T(8,128)(2,1)S(1)} %fusion.56), channel_id=1, source_target_pairs={{0,3},{1,0},{2,1},{3,2},{4,7},{5,4},{6,5},{7,6},{8,11},{9,8},{10,9... | collective-permute-start | bytes 1572872 | tf_op jit(solution)/shard_map/ppermute | solution.py:117
  142.6 44.8 %collective-permute-start.3 = (bf16[256,1024]{0,1:T(8,128)(2,1)S(1)}, bf16[256,1024]{0,1:T(8,128)(2,1)S(1)}, u32[]{:S(2)}, u32[]{:S(2)}) collective-permute-start(bf16[256,1024]{0,1:T(8,128)(2,1)S(1)} %fusion.56), channel_id=1, source_target_pairs={{0,1},{1,2},{2,3},{3,0},{4,5},{5,6},{6,7},{7,4},{8,9},{9,10},{10,1... | collective-permute-start | bytes 1572872 | tf_op jit(solution)/shard_map/ppermute | solution.py:117
Sparse Core Ops, SparseCore 0:
  10.9 138.5 all-gather.1

commit v10 on v9

--- a/solution.py
+++ b/solution.py
@@ -27,7 +27,7 @@
     inner = 2.0 * np.pi * ((n2[:, None] * n2[None, :]) % tokens) / tokens
     b_cos = np.cos(inner)
     b_sin = np.sin(inner)
-    forward = np.block([[b_cos, -b_sin], [b_sin, b_cos]])
+    forward = (b_cos, -b_sin - b_cos, b_cos - b_sin)
     backward = np.block([[b_cos, b_sin], [-b_sin, b_cos]])
     last = 2.0 * np.pi * ((n1[:, None] * k1[None, :]) % outer) / outer
     last_cos = np.cos(last) / period
@@ -38,7 +38,7 @@
     tables = (
         first_table, twist_cos, twist_sin, forward, backward.T, twist_cos_t, twist_sin_t, last_cos, last_sin
     )
-    return tuple(as32(a) for a in tables)
+    return tuple(tuple(map(as32, a)) if isinstance(a, tuple) else as32(a) for a in tables)
 
 
 def dot(a, b):
@@ -57,10 +57,14 @@
     s_real, s_imag = spec[0], spec[1]
     w_real = s_real * twist_cos + s_imag * twist_sin
     w_imag = s_imag * twist_cos - s_real * twist_sin
-    twisted = jnp.concatenate([w_real, w_imag], -1).reshape(outer * both, 2 * tokens)
-    u = dot(twisted, forward).reshape(outer, both, 2 * tokens)
-    u_real, u_imag = u[:, :per_device, :tokens], u[:, :per_device, tokens:]
-    f_real, f_imag = u[:, per_device:, :tokens], u[:, per_device:, tokens:]
+    flat = (outer * both, tokens)
+    w_real, w_imag = w_real.reshape(flat), w_imag.reshape(flat)
+    plain, low, high = forward
+    first = dot(w_real + w_imag, plain)
+    whole_real = (first - dot(w_imag, high)).reshape(outer, both, tokens)
+    whole_imag = (first + dot(w_real, low)).reshape(outer, both, tokens)
+    u_real, u_imag = whole_real[:, :per_device], whole_imag[:, :per_device]
+    f_real, f_imag = whole_real[:, per_device:], whole_imag[:, per_device:]
     p_real = u_real * f_real - u_imag * f_imag
     p_imag = u_real * f_imag + u_imag * f_real
     product = jnp.concatenate([p_real, p_imag], -1)

time: 198 us -> 206 us (1.040)
  the two profiles are of different devices: /device:TPU:63 before, /device:TPU:33 now
where the time goes in v10:
time: 206 us; the launch traced here: 205 us
  waiting for transfers between devices  62.5 us (30%)
  blocking collectives  52.6 us (26%)
  local copies, waits for them, and re-layouts  23.4 us (11%)
  matrix products  23.3 us (11%)
  starting transfers between devices  17 us (8%)
  between operations  13.8 us (7%)
  other arithmetic  12.9 us (6%)
    all_to_all x1, blocking collectives, block(): lax.all_to_all(outgoing, 'seq', split_axis=0, concat_axis=0, tiled=True)  52.6 us
    ppermute x3, waiting for transfers between devices, projection(): lax.ppermute(inner, 'tp', [(j, (j + k) % size) for j in range(size)])  41.4 us
    all_to_all x1, waiting for transfers between devices, block(): lax.all_to_all(mixed, 'seq', split_axis=0, concat_axis=0, tiled=True)  16.1 us
    squeeze x2, local copies, waits for them, and re-layouts, long_conv(): s_real, s_imag = (spec[0], spec[1])  9.81 us
    ppermute x3, starting transfers between devices, shifted(): return lax.ppermute(value, axis, pairs)  9.23 us
    dot_general x4, matrix products, dot(): jnp.dot(a, b, precision=TRANSFORM_PRECISION, preferred_element_type=jnp.f...  7.92 us
    dot_general x3, matrix products, projection(): jnp.dot(chunk, rows_of((here - k) % size), preferred_element_type=jnp.flo...  7.78 us
    dot_general x3, matrix products, einsum(): jnp.einsum(form, a, b, precision=TRANSFORM_PRECISION, preferred_element_t...  5.33 us
  transfers between devices with their start and end apart: 8, of which 4 were waited for; matrix products, arithmetic and copies ran while one was open for 27% of the time, Pallas kernels for 0%

profile of v10, /device:TPU:33, one launch (start us, length us, event | category | flops | bytes accessed | tf_op | source)
XLA Modules:
  0.0 205.5 jit_solution(14051764419332862546)
XLA Ops:
  6.5 0.0 all-gather.2.cloned.1.call-start
  6.5 0.7 all-gather.2.cloned.1.call-update
  7.3 0.7 slice.109
  8.0 0.2 copy.46
  8.2 3.8 %collective-permute-start.1 = (bf16[2,1024]{0,1:T(8,128)(2,1)S(1)}, bf16[2,1024]{0,1:T(8,128)(2,1)S(1)}, u32[]{:S(2)}, u32[]{:S(2)}) collective-permute-start(bf16[2,1024]{0,1:T(8,128)(2,1)S(1)} %copy.46), channel_id=1, source_target_pairs={{0,4},{4,8},{8,12},{12,16},{16,20},{20,24},{24,28},{28,32},{32,36}... | collective-permute-start | bytes 12296 | tf_op jit(solution)/shard_map/ppermute | solution.py:13
  12.0 0.7 slice.115
  12.7 0.2 copy.49
  12.9 1.9 collective-permute-start.2
  14.8 0.9 fusion.70
  15.7 1.2 copy.45
  17.0 1.2 copy.48
  18.2 1.2 copy.51
  19.5 0.0 collective-permute-done.1
  19.5 0.0 collective-permute-done.2
  19.5 0.0 copy-start.9
  19.5 1.9 multiply_convert_fusion
  21.4 0.1 pad_maximum_fusion
  21.6 52.6 %all_to_all.10 = bf16[64,32,256]{2,1,0:T(8,128)(2,1)S(1)} all-to-all(bf16[64,32,256]{2,1,0:T(8,128)(2,1)S(1)} %pad_maximum_fusion), channel_id=1, replica_groups=mesh['seq'=64,'tp'=4] {'seq'}, dimensions={0} | all-to-all | bytes 2097152 | tf_op jit(solution)/shard_map/all_to_all | solution.py:102
  74.1 0.6 copy.65
  74.7 2.3 %fusion.71 = f32[256,8192]{1,0:T(8,128)S(1)} fusion(f32[256,64]{1,0:T(8,128)S(1)} %copy-done.9, bf16[64,8192]{1,0:T(8,128)(2,1)S(1)} %bitcast.68), kind=kOutput, calls=%fused_computation.75 | convolution fusion | flops 805306368 | bytes 9502720 | tf_op jit(solution)/shard_map/dot_general | solution.py:45
  77.1 3.8 %fusion.67 = (f32[128,8192]{1,0:T(8,128)}, f32[128,8192]{1,0:T(8,128)}) fusion(f32[256,8192]{1,0:T(8,128)S(1)} %fusion.71), kind=kLoop, calls=%fused_computation.71 | loop fusion | bytes 16777216 | tf_op jit(solution)/shard_map/slice | solution.py:57
  80.9 4.9 %squeeze.10 = f32[4096,256]{1,0:T(8,128)} reshape(f32[128,8192]{1,0:T(8,128)} %get-tuple-element.9) | data formatting | bytes 8388608 | tf_op jit(solution)/shard_map/squeeze | solution.py:57
  85.8 4.9 %squeeze.4 = f32[4096,256]{1,0:T(8,128)} reshape(f32[128,8192]{1,0:T(8,128)} %get-tuple-element.10) | data formatting | bytes 8388608 | tf_op jit(solution)/shard_map/squeeze | solution.py:57
  90.7 0.0 copy-done.8
  90.7 4.9 %fusion.1 = (f32[4096,256]{1,0:T(8,128)S(1)}, f32[4096,256]{1,0:T(8,128)S(1)}) fusion(f32[4096,256]{1,0:T(8,128)} %squeeze.10, f32[4096,256]{1,0:T(8,128)} %squeeze.4, f32[128,256]{1,0:T(8,128)S(1)} %copy-done.8, f32[128,256]{1,0:T(8,128)S(1)} %copy-done.7), kind=kLoop, calls=%fused_computation.7 | loop fusion | flops 6291456 | bytes 17039360 | tf_op jit(solution)/shard_map/sub | solution.py:59
  95.7 0.0 copy-start.5
  95.7 1.8 fusion.6
  97.5 0.0 copy-start.4
  97.5 1.9 convolution_add_fusion
  99.4 1.9 convolution_subtract_fusion
  101.3 1.0 fusion.68
  102.3 0.0 copy-start
  102.4 4.7 %multiply_subtract_fusion = (f32[128,16,256]{2,0,1:T(8,128)S(1)}, f32[128,16,256]{2,0,1:T(8,128)S(1)}) fusion(f32[128,16,256]{2,1,0:T(8,128)S(1)} %get-tuple-element.24, f32[128,16,256]{2,1,0:T(8,128)S(1)} %get-tuple-element.25, f32[128,16,256]{2,1,0:T(8,128)S(1)} %get-tuple-element.12, f32[128,16,256]{2,1,0:T(8,128)S(1)} %get-tuple-element.11), kind=kLoop, calls=%fused_computation.32 | loop fusion | flops 3145728 | bytes 12582912 | tf_op jit(solution)/shard_map/sub | solution.py:68
  107.0 0.0 copy-done
  107.1 0.0 copy-start.2
  107.1 0.0 copy-start.3
  107.1 0.0 copy-start.11
  107.1 0.0 copy-start.10
  107.1 3.5 %fusion.8 = f32[16,512,128]{1,2,0:T(8,128)S(1)} fusion(f32[512,512,1]{1,0,2:T(8,128)S(1)} %copy-done, f32[128,16,256]{2,0,1:T(8,128)S(1)} %get-tuple-element.8, f32[128,16,256]{2,0,1:T(8,128)S(1)} %get-tuple-element.7), kind=kOutput, calls=%fused_computation.14 | convolution fusion | flops 3222274048 | bytes 9437184 | tf_op jit(solution)/shard_map/nq,kcq->cnk/dot_general | solution.py:49
  110.6 0.0 copy-done.2
  110.6 0.0 copy-done.3
  110.6 0.0 copy-done.11
  110.7 0.0 copy-start.1
  110.7 0.9 fusion.19
  111.6 0.0 copy-start.12
  111.6 0.9 fusion.49
  112.5 1.1 copy.58
  113.6 5.3 %all-to-all-start.1 = ((bf16[64,16,256]{2,1,0:T(8,128)(2,1)}), bf16[64,16,256]{2,1,0:T(8,128)(2,1)S(1)}, u32[]{:S(2)}, u32[]{:S(2)}) async-start(bf16[64,16,256]{2,1,0:T(8,128)(2,1)} %copy.58), calls=%async_computation.1 | async-start | bytes 1048576 | tf_op jit(solution)/shard_map/all_to_all | solution.py:104
  118.9 0.2 copy.43
  119.2 3.5 %collective-permute-start = (bf16[2,1024]{0,1:T(8,128)(2,1)S(1)}, bf16[2,1024]{0,1:T(8,128)(2,1)S(1)}, u32[]{:S(2)}, u32[]{:S(2)}) collective-permute-start(bf16[2,1024]{0,1:T(8,128)(2,1)S(1)} %copy.43), channel_id=1, source_target_pairs={{0,4},{4,8},{8,12},{12,16},{16,20},{20,24},{24,28},{28,32},{32,36}... | collective-permute-start | bytes 12296 | tf_op jit(solution)/shard_map/ppermute | solution.py:13
  122.7 0.2 copy.42
  122.9 4.3 %collective-permute-done = bf16[2,1024]{0,1:T(8,128)(2,1)S(1)} collective-permute-done((bf16[2,1024]{0,1:T(8,128)(2,1)S(1)}, bf16[2,1024]{0,1:T(8,128)(2,1)S(1)}, u32[]{:S(2)}, u32[]{:S(2)}) %collective-permute-start) | collective-permute-done | bytes 4128 | tf_op jit(solution)/shard_map/ppermute | solution.py:13
  127.2 16.1 %all-to-all-done.1 = bf16[64,16,256]{2,1,0:T(8,128)(2,1)S(1)} async-done(((bf16[64,16,256]{2,1,0:T(8,128)(2,1)}), bf16[64,16,256]{2,1,0:T(8,128)(2,1)S(1)}, u32[]{:S(2)}, u32[]{:S(2)}) %all-to-all-start.1) | async-done | bytes 524320 | tf_op jit(solution)/shard_map/all_to_all | solution.py:104
  143.4 1.3 fusion.54
  144.6 0.1 collective-permute-start.4
  144.8 1.4 collective-permute-start.5
  146.2 1.0 collective-permute-start.3
  147.2 2.3 %fusion.17 = f32[256,1024]{1,0:T(8,128)S(1)} fusion(bf16[256,1024]{0,1:T(8,128)(2,1)S(1)} %fusion.54, bf16[4096,1024]{1,0:T(8,128)(2,1)} %all-gather.2.cloned.1.call-done, s32[]{:T(128)S(6)} %select_n.27), kind=kOutput, calls=%fused_computation.21 | convolution fusion | flops 536870912 | bytes 3670020 | tf_op jit(solution)/shard_map/dot_general | solution.py:123
  149.5 29.0 %collective-permute-done.4 = bf16[256,1024]{0,1:T(8,128)(2,1)S(1)} collective-permute-done((bf16[256,1024]{0,1:T(8,128)(2,1)S(1)}, bf16[256,1024]{0,1:T(8,128)(2,1)S(1)}, u32[]{:S(2)}, u32[]{:S(2)}) %collective-permute-start.4) | collective-permute-done | bytes 524320 | tf_op jit(solution)/shard_map/ppermute | solution.py:121
  178.5 2.3 %fusion.13 = f32[256,1024]{1,0:T(8,128)S(1)} fusion(bf16[256,1024]{0,1:T(8,128)(2,1)S(1)} %collective-permute-done.4, bf16[4096,1024]{1,0:T(8,128)(2,1)} %all-gather.2.cloned.1.call-done, s32[]{:T(128)S(6)} %select_n.31), kind=kOutput, calls=%fused_computation.17 | convolution fusion | flops 536870912 | bytes 3670020 | tf_op jit(solution)/shard_map/dot_general | solution.py:125
  180.8 12.4 %collective-permute-done.5 = bf16[256,1024]{0,1:T(8,128)(2,1)S(1)} collective-permute-done((bf16[256,1024]{0,1:T(8,128)(2,1)S(1)}, bf16[256,1024]{0,1:T(8,128)(2,1)S(1)}, u32[]{:S(2)}, u32[]{:S(2)}) %collective-permute-start.5) | collective-permute-done | bytes 524320 | tf_op jit(solution)/shard_map/ppermute | solution.py:121
  193.2 2.3 %fusion.11 = f32[256,1024]{1,0:T(8,128)S(1)} fusion(bf16[256,1024]{0,1:T(8,128)(2,1)S(1)} %collective-permute-done.5, bf16[4096,1024]{1,0:T(8,128)(2,1)} %all-gather.2.cloned.1.call-done, s32[]{:T(128)S(6)} %select_n.33), kind=kOutput, calls=%fused_computation.15 | convolution fusion | flops 536870912 | bytes 3670020 | tf_op jit(solution)/shard_map/dot_general | solution.py:125
  195.5 0.0 collective-permute-done.3
  195.5 3.1 %fusion.46 = bf16[256,1024]{1,0:T(8,128)(2,1)} fusion(f32[256,1024]{1,0:T(8,128)S(1)} %fusion.11, f32[256,1024]{1,0:T(8,128)S(1)} %fusion.13, f32[256,1024]{1,0:T(8,128)S(1)} %fusion.17, bf16[256,1024]{0,1:T(8,128)(2,1)S(1)} %collective-permute-done.3, bf16[4096,1024]{1,0:T(8,128)(2,1)} %all-gather.2.cloned.1.call-done, s32[]{:T(128)S(6)} %select_n.29), kind=kOutput, calls=%fused_computation.42 | convolution fusion | flops 537919488 | bytes 6291460 | tf_op jit(solution)/shard_map/dot_general | solution.py:125
  (13 shorter events, 0.0 us)
Async XLA Ops:
  6.5 140.7 %all-gather.2.cloned.1.call-start = ((), (), s32[]{:S(2)}) async-start(), calls=%async_computation.2 | async-start | bytes 8519680 | tf_op jit(solution)/shard_map/all_gather | solution.py:93
  8.2 11.3 %collective-permute-start.1 = (bf16[2,1024]{0,1:T(8,128)(2,1)S(1)}, bf16[2,1024]{0,1:T(8,128)(2,1)S(1)}, u32[]{:S(2)}, u32[]{:S(2)}) collective-permute-start(bf16[2,1024]{0,1:T(8,128)(2,1)S(1)} %copy.46), channel_id=1, source_target_pairs={{0,4},{4,8},{8,12},{12,16},{16,20},{20,24},{24,28},{28,32},{32,36}... | collective-permute-start | bytes 12296 | tf_op jit(solution)/shard_map/ppermute | solution.py:13
  12.9 6.6 %collective-permute-start.2 = (bf16[2,1024]{0,1:T(8,128)(2,1)S(1)}, bf16[2,1024]{0,1:T(8,128)(2,1)S(1)}, u32[]{:S(2)}, u32[]{:S(2)}) collective-permute-start(bf16[2,1024]{0,1:T(8,128)(2,1)S(1)} %copy.49), channel_id=1, source_target_pairs={{0,4},{4,8},{8,12},{12,16},{16,20},{20,24},{24,28},{28,32},{32,36}... | collective-permute-start | bytes 12296 | tf_op jit(solution)/shard_map/ppermute | solution.py:13
  19.5 55.2 %copy-start.9 = (f32[256,64]{1,0:T(8,128)S(1)}, f32[256,64]{1,0:T(8,128)}, u32[]{:S(2)}) copy-start(f32[256,64]{1,0:T(8,128)} %constant.61.clone) | copy-start | bytes 196612
  85.8 4.9 %copy-start.7 = (f32[128,256]{1,0:T(8,128)S(1)}, f32[128,256]{1,0:T(8,128)}, u32[]{:S(2)}) copy-start(f32[128,256]{1,0:T(8,128)} %constant.72) | copy-start | bytes 393220
  85.8 4.9 %copy-start.8 = (f32[128,256]{1,0:T(8,128)S(1)}, f32[128,256]{1,0:T(8,128)}, u32[]{:S(2)}) copy-start(f32[128,256]{1,0:T(8,128)} %constant.73) | copy-start | bytes 393220
  90.7 4.9 %copy-start.6 = (f32[256,256]{1,0:T(8,128)S(1)}, f32[256,256]{1,0:T(8,128)}, u32[]{:S(2)}) copy-start(f32[256,256]{1,0:T(8,128)} %constant.64.clone) | copy-start | bytes 786436
  95.7 1.8 copy-start.5
  97.5 1.9 copy-start.4
  102.3 4.7 %copy-start = (f32[512,512,1]{1,0,2:T(8,128)S(1)}, f32[512,512,1]{1,0,2:T(8,128)}, u32[]{:S(2)}) copy-start(f32[512,512,1]{1,0,2:T(8,128)} %constant.76) | copy-start | bytes 3145732
  107.1 3.6 %copy-start.2 = (f32[256,128]{0,1:T(8,128)S(1)}, f32[256,128]{0,1:T(8,128)}, u32[]{:S(2)}) copy-start(f32[256,128]{0,1:T(8,128)} %constant.74) | copy-start | bytes 393220
  107.1 3.6 %copy-start.3 = (f32[256,128]{0,1:T(8,128)S(1)}, f32[256,128]{0,1:T(8,128)}, u32[]{:S(2)}) copy-start(f32[256,128]{0,1:T(8,128)} %constant.75) | copy-start | bytes 393220
  107.1 3.6 %copy-start.11 = (f32[64,128,1]{1,0,2:T(8,128)S(1)}, f32[64,128,1]{1,0,2:T(8,128)}, u32[]{:S(2)}) copy-start(f32[64,128,1]{1,0,2:T(8,128)} %constant.78) | copy-start | bytes 98308
  107.1 4.5 %copy-start.10 = (f32[64,128,1]{1,0,2:T(8,128)S(1)}, f32[64,128,1]{1,0,2:T(8,128)}, u32[]{:S(2)}) copy-start(f32[64,128,1]{1,0,2:T(8,128)} %constant.77) | copy-start | bytes 98308
  110.7 8.3 %copy-start.1 = (bf16[256,1024]{1,0:T(8,128)(2,1)S(1)}, bf16[256,1024]{1,0:T(8,128)(2,1)}, u32[]{:S(2)}) copy-start(bf16[256,1024]{1,0:T(8,128)(2,1)} %param.18) | copy-start | bytes 1572868
  111.6 31.8 %copy-start.12 = (f32[1024]{0:T(1024)S(1)}, f32[1024]{0:T(1024)}, u32[]{:S(2)}) copy-start(f32[1024]{0:T(1024)} %param.23) | copy-start | bytes 12292
  113.6 29.7 %all-to-all-start.1 = ((bf16[64,16,256]{2,1,0:T(8,128)(2,1)}), bf16[64,16,256]{2,1,0:T(8,128)(2,1)S(1)}, u32[]{:S(2)}, u32[]{:S(2)}) async-start(bf16[64,16,256]{2,1,0:T(8,128)(2,1)} %copy.58), calls=%async_computation.1 | async-start | bytes 1048576 | tf_op jit(solution)/shard_map/all_to_all | solution.py:104
  119.2 8.1 %collective-permute-start = (bf16[2,1024]{0,1:T(8,128)(2,1)S(1)}, bf16[2,1024]{0,1:T(8,128)(2,1)S(1)}, u32[]{:S(2)}, u32[]{:S(2)}) collective-permute-start(bf16[2,1024]{0,1:T(8,128)(2,1)S(1)} %copy.43), channel_id=1, source_target_pairs={{0,4},{4,8},{8,12},{12,16},{16,20},{20,24},{24,28},{28,32},{32,36}... | collective-permute-start | bytes 12296 | tf_op jit(solution)/shard_map/ppermute | solution.py:13
  144.6 33.9 %collective-permute-start.4 = (bf16[256,1024]{0,1:T(8,128)(2,1)S(1)}, bf16[256,1024]{0,1:T(8,128)(2,1)S(1)}, u32[]{:S(2)}, u32[]{:S(2)}) collective-permute-start(bf16[256,1024]{0,1:T(8,128)(2,1)S(1)} %fusion.54), channel_id=1, source_target_pairs={{0,2},{1,3},{2,0},{3,1},{4,6},{5,7},{6,4},{7,5},{8,10},{9,11},{10,... | collective-permute-start | bytes 1572872 | tf_op jit(solution)/shard_map/ppermute | solution.py:121
  144.8 48.4 %collective-permute-start.5 = (bf16[256,1024]{0,1:T(8,128)(2,1)S(1)}, bf16[256,1024]{0,1:T(8,128)(2,1)S(1)}, u32[]{:S(2)}, u32[]{:S(2)}) collective-permute-start(bf16[256,1024]{0,1:T(8,128)(2,1)S(1)} %fusion.54), channel_id=1, source_target_pairs={{0,3},{1,0},{2,1},{3,2},{4,7},{5,4},{6,5},{7,6},{8,11},{9,8},{10,9... | collective-permute-start | bytes 1572872 | tf_op jit(solution)/shard_map/ppermute | solution.py:121
  146.2 49.4 %collective-permute-start.3 = (bf16[256,1024]{0,1:T(8,128)(2,1)S(1)}, bf16[256,1024]{0,1:T(8,128)(2,1)S(1)}, u32[]{:S(2)}, u32[]{:S(2)}) collective-permute-start(bf16[256,1024]{0,1:T(8,128)(2,1)S(1)} %fusion.54), channel_id=1, source_target_pairs={{0,1},{1,2},{2,3},{3,0},{4,5},{5,6},{6,7},{7,4},{8,9},{9,10},{10,1... | collective-permute-start | bytes 1572872 | tf_op jit(solution)/shard_map/ppermute | solution.py:121
Sparse Core Ops, SparseCore 0:
  10.9 135.6 all-gather.1

commit v11 on v9

--- a/solution.py
+++ b/solution.py
@@ -16,7 +16,8 @@
 def make_tables(blocks, tokens):
     outer = 2 * blocks
     period = outer * tokens
-    k1 = np.arange(outer, dtype=np.int64)
+    k1 = np.arange(blocks + 1, dtype=np.int64)
+    weight = np.where((k1 == 0) | (k1 == blocks), 1.0, 2.0)
     n1 = np.arange(blocks, dtype=np.int64)
     n2 = np.arange(tokens, dtype=np.int64)
     first = 2.0 * np.pi * ((k1[:, None] * n1[None, :]) % outer) / outer
@@ -30,8 +31,8 @@
     forward = np.block([[b_cos, -b_sin], [b_sin, b_cos]])
     backward = np.block([[b_cos, b_sin], [-b_sin, b_cos]])
     last = 2.0 * np.pi * ((n1[:, None] * k1[None, :]) % outer) / outer
-    last_cos = np.cos(last) / period
-    last_sin = -np.sin(last) / period
+    last_cos = weight * np.cos(last) / period
+    last_sin = -weight * np.sin(last) / period
     as32 = lambda a: jnp.asarray(a, jnp.float32)
     twist_cos_t = np.cos(twist).T[None]
     twist_sin_t = np.sin(twist).T[None]
@@ -52,7 +53,7 @@
 def long_conv(pieces, per_device, tables):
     first_table, twist_cos, twist_sin, forward, backward, back_cos, back_sin, last_cos, last_sin = tables
     blocks, both, tokens = pieces.shape
-    outer = 2 * blocks
+    outer = first_table.shape[0] // 2
     spec = dot(first_table, pieces.reshape(blocks, both * tokens)).reshape(2, outer, both, tokens)
     s_real, s_imag = spec[0], spec[1]
     w_real = s_real * twist_cos + s_imag * twist_sin
@@ -87,7 +88,8 @@
     per_device = channels // groups
     tables = make_tables(groups, tokens_here)
     weights = lax.all_gather(out_weight, "seq", axis=0, tiled=True)
-    tails = shifted((query_rows[-2:], key_rows[-2:], value_rows[-2:]), "seq", 1)
+    ends = jnp.concatenate([query_rows[-2:], key_rows[-2:], value_rows[-2:]], 0)
+    tails = jnp.split(shifted(ends, "seq", 1), 3, 0)
     query_mix = causal_short(query_rows, tails[0], short_filter[:, 0, :])
     key_mix = causal_short(key_rows, tails[1], short_filter[:, 1, :])
     value_mix = causal_short(value_rows, tails[2], short_filter[:, 2, :])

time: 198 us -> 197 us (level)
  the two profiles are of different devices: /device:TPU:63 before, /device:TPU:33 now
where the time goes in v11:
time: 197 us; the launch traced here: 196 us
  waiting for transfers between devices  82.2 us (42%)
  blocking collectives  53.8 us (27%)
  matrix products  19.3 us (10%)
  between operations  13.8 us (7%)
  starting transfers between devices  11.5 us (6%)
  local copies, waits for them, and re-layouts  10.7 us (5%)
  other arithmetic  4.95 us (3%)
    all_to_all x1, blocking collectives, block(): lax.all_to_all(outgoing, 'seq', split_axis=0, concat_axis=0, tiled=True)  53.8 us
    all_to_all x1, waiting for transfers between devices, block(): lax.all_to_all(mixed, 'seq', split_axis=0, concat_axis=0, tiled=True)  38 us
    ppermute x3, waiting for transfers between devices, projection(): lax.ppermute(inner, 'tp', [(j, (j + k) % size) for j in range(size)])  23.9 us
    all_gather x1, waiting for transfers between devices, block(): weights = lax.all_gather(out_weight, 'seq', axis=0, tiled=True)  19.6 us
    dot_general x3, matrix products, projection(): jnp.dot(chunk, rows_of((here - k) % size), preferred_element_type=jnp.flo...  7.76 us
    unnamed x29, local copies, waits for them, and re-layouts  5.74 us
    all_to_all x1, starting transfers between devices, block(): lax.all_to_all(mixed, 'seq', split_axis=0, concat_axis=0, tiled=True)  5.08 us
    dot_general x2, matrix products, dot(): jnp.dot(a, b, precision=TRANSFORM_PRECISION, preferred_element_type=jnp.f...  4.8 us
  transfers between devices with their start and end apart: 6, of which 4 were waited for; matrix products, arithmetic and copies ran while one was open for 16% of the time, Pallas kernels for 0%

profile of v11, /device:TPU:33, one launch (start us, length us, event | category | flops | bytes accessed | tf_op | source)
XLA Modules:
  0.0 196.3 jit_solution(9268329649648642168)
XLA Ops:
  6.5 0.0 all-gather.2.cloned.1.call-start
  6.5 0.7 all-gather.2.cloned.1.call-update
  7.3 0.7 slice.103
  8.0 0.7 slice.104
  8.7 0.7 slice.105
  9.5 0.2 copy.33
  9.7 3.8 %collective-permute-start = (bf16[6,1024]{0,1:T(8,128)(2,1)S(1)}, bf16[6,1024]{0,1:T(8,128)(2,1)S(1)}, u32[]{:S(2)}, u32[]{:S(2)}) collective-permute-start(bf16[6,1024]{0,1:T(8,128)(2,1)S(1)} %copy.33), channel_id=1, source_target_pairs={{0,4},{4,8},{8,12},{12,16},{16,20},{20,24},{24,28},{28,32},{32,36}... | collective-permute-start | bytes 36872 | tf_op jit(solution)/shard_map/ppermute | solution.py:13
  13.4 0.9 fusion.50
  14.4 1.2 copy.35
  15.6 1.2 copy.37
  16.9 0.0 copy-done.2
  16.9 0.2 copy.39
  17.1 0.0 collective-permute-done
  17.1 0.2 fusion.49
  17.3 1.9 multiply_convert_fusion
  19.2 0.1 pad_maximum_fusion
  19.3 0.0 copy-start.7
  19.3 53.8 %all_to_all.10 = bf16[64,32,256]{2,1,0:T(8,128)(2,1)S(1)} all-to-all(bf16[64,32,256]{2,1,0:T(8,128)(2,1)S(1)} %pad_maximum_fusion), channel_id=1, replica_groups=mesh['seq'=64,'tp'=4] {'seq'}, dimensions={0} | all-to-all | bytes 2097152 | tf_op jit(solution)/shard_map/all_to_all | solution.py:100
  73.2 0.6 copy.43
  73.8 0.0 copy-done.7
  73.8 1.3 fusion.51
  75.1 0.4 fusion.48
  75.5 0.7 copy.44
  76.2 0.0 copy-start.5
  76.2 0.0 copy-start.6
  76.2 0.7 copy.45
  77.0 0.1 copy-done.5
  77.1 0.0 copy-done.6
  77.1 1.0 multiply_add_fusion
  78.2 0.2 copy-done
  78.4 3.5 %fusion = f32[65,32,512]{2,1,0:T(8,128)S(1)} fusion(f32[512,512,1]{1,0,2:T(8,128)S(1)} %copy-done, f32[65,32,256]{2,1,0:T(8,128)S(1)} %get-tuple-element.6, f32[65,32,256]{2,1,0:T(8,128)S(1)} %get-tuple-element.5), kind=kOutput, calls=%fused_computation | convolution fusion | flops 3272622080 | bytes 9568256 | tf_op jit(solution)/shard_map/dot_general | solution.py:46
  81.9 0.3 multiply_subtract_fusion.2
  82.2 0.0 copy-start.3
  82.2 0.0 copy-start.4
  82.2 1.9 fusion.16
  84.1 0.0 copy-done.3
  84.1 0.0 copy-done.4
  84.1 0.0 copy-start.9
  84.1 0.4 multiply_add_fusion.1
  84.5 0.0 copy-start.8
  84.5 0.4 copy-done.9
  84.9 1.2 fusion.34
  86.0 0.0 copy-done.8
  86.0 0.0 copy-start.1
  86.1 1.4 fusion.32
  87.5 0.0 copy-start.10
  87.5 1.1 copy.42
  88.6 5.1 %all-to-all-start.1 = ((bf16[64,16,256]{2,1,0:T(8,128)(2,1)}), bf16[64,16,256]{2,1,0:T(8,128)(2,1)S(1)}, u32[]{:S(2)}, u32[]{:S(2)}) async-start(bf16[64,16,256]{2,1,0:T(8,128)(2,1)} %copy.42), calls=%async_computation.1 | async-start | bytes 1048576 | tf_op jit(solution)/shard_map/all_to_all | solution.py:102
  93.6 0.0 copy-done.1
  93.7 0.2 copy.32
  93.9 38.0 %all-to-all-done.1 = bf16[64,16,256]{2,1,0:T(8,128)(2,1)S(1)} async-done(((bf16[64,16,256]{2,1,0:T(8,128)(2,1)}), bf16[64,16,256]{2,1,0:T(8,128)(2,1)S(1)}, u32[]{:S(2)}, u32[]{:S(2)}) %all-to-all-start.1) | async-done | bytes 524320 | tf_op jit(solution)/shard_map/all_to_all | solution.py:102
  131.9 0.0 copy-done.10
  131.9 1.2 fusion.38
  133.2 0.1 collective-permute-start.2
  133.3 2.5 %collective-permute-start.3 = (bf16[256,1024]{0,1:T(8,128)(2,1)S(1)}, bf16[256,1024]{0,1:T(8,128)(2,1)S(1)}, u32[]{:S(2)}, u32[]{:S(2)}) collective-permute-start(bf16[256,1024]{0,1:T(8,128)(2,1)S(1)} %fusion.38), channel_id=1, source_target_pairs={{0,3},{1,0},{2,1},{3,2},{4,7},{5,4},{6,5},{7,6},{8,11},{9,8},{10,9... | collective-permute-start | bytes 1572872 | tf_op jit(solution)/shard_map/ppermute | solution.py:119
  135.8 0.0 collective-permute-start.1
  135.8 19.6 %all-gather.2.cloned.1.call-done = bf16[4096,1024]{1,0:T(8,128)(2,1)} async-done(((bf16[64,1024]{1,0:T(8,128)(2,1)}), bf16[4096,1024]{1,0:T(8,128)(2,1)}) %all-gather.2.cloned.1.call-update) | async-done | bytes 8388624 | tf_op jit(solution)/shard_map/all_gather | solution.py:90
  155.4 2.3 %fusion.14 = f32[256,1024]{1,0:T(8,128)S(1)} fusion(bf16[256,1024]{0,1:T(8,128)(2,1)S(1)} %fusion.38, bf16[4096,1024]{1,0:T(8,128)(2,1)} %all-gather.2.cloned.1.call-done, s32[]{:T(128)S(6)} %select_n.27), kind=kOutput, calls=%fused_computation.16 | convolution fusion | flops 536870912 | bytes 3670020 | tf_op jit(solution)/shard_map/dot_general | solution.py:121
  157.8 12.6 %collective-permute-done.2 = bf16[256,1024]{0,1:T(8,128)(2,1)S(1)} collective-permute-done((bf16[256,1024]{0,1:T(8,128)(2,1)S(1)}, bf16[256,1024]{0,1:T(8,128)(2,1)S(1)}, u32[]{:S(2)}, u32[]{:S(2)}) %collective-permute-start.2) | collective-permute-done | bytes 524320 | tf_op jit(solution)/shard_map/ppermute | solution.py:119
  170.3 2.3 %fusion.10 = f32[256,1024]{1,0:T(8,128)S(1)} fusion(bf16[256,1024]{0,1:T(8,128)(2,1)S(1)} %collective-permute-done.2, bf16[4096,1024]{1,0:T(8,128)(2,1)} %all-gather.2.cloned.1.call-done, s32[]{:T(128)S(6)} %select_n.31), kind=kOutput, calls=%fused_computation.12 | convolution fusion | flops 536870912 | bytes 3670020 | tf_op jit(solution)/shard_map/dot_general | solution.py:123
  172.7 11.3 %collective-permute-done.3 = bf16[256,1024]{0,1:T(8,128)(2,1)S(1)} collective-permute-done((bf16[256,1024]{0,1:T(8,128)(2,1)S(1)}, bf16[256,1024]{0,1:T(8,128)(2,1)S(1)}, u32[]{:S(2)}, u32[]{:S(2)}) %collective-permute-start.3) | collective-permute-done | bytes 524320 | tf_op jit(solution)/shard_map/ppermute | solution.py:119
  184.0 2.3 %fusion.8 = f32[256,1024]{1,0:T(8,128)S(1)} fusion(bf16[256,1024]{0,1:T(8,128)(2,1)S(1)} %collective-permute-done.3, bf16[4096,1024]{1,0:T(8,128)(2,1)} %all-gather.2.cloned.1.call-done, s32[]{:T(128)S(6)} %select_n.33), kind=kOutput, calls=%fused_computation.10 | convolution fusion | flops 536870912 | bytes 3670020 | tf_op jit(solution)/shard_map/dot_general | solution.py:123
  186.3 0.0 collective-permute-done.1
  186.3 3.1 %fusion.28 = bf16[256,1024]{1,0:T(8,128)(2,1)} fusion(f32[256,1024]{1,0:T(8,128)S(1)} %fusion.8, f32[256,1024]{1,0:T(8,128)S(1)} %fusion.10, f32[256,1024]{1,0:T(8,128)S(1)} %fusion.14, bf16[256,1024]{0,1:T(8,128)(2,1)S(1)} %collective-permute-done.1, bf16[4096,1024]{1,0:T(8,128)(2,1)} %all-gather.2.cloned.1.call-done, s32[]{:T(128)S(6)} %select_n.29), kind=kOutput, calls=%fused_computation.23 | convolution fusion | flops 537919488 | bytes 6291460 | tf_op jit(solution)/shard_map/dot_general | solution.py:123
  (3 shorter events, 0.0 us)
Async XLA Ops:
  6.5 10.3 %copy-start.2 = (bf16[256,1024]{1,0:T(8,128)(2,1)S(1)}, bf16[256,1024]{1,0:T(8,128)(2,1)}, u32[]{:S(2)}) copy-start(bf16[256,1024]{1,0:T(8,128)(2,1)} %param.20) | copy-start | bytes 1572868
  6.5 148.9 %all-gather.2.cloned.1.call-start = ((), (), s32[]{:S(2)}) async-start(), calls=%async_computation.2 | async-start | bytes 8519680 | tf_op jit(solution)/shard_map/all_gather | solution.py:90
  9.7 7.4 %collective-permute-start = (bf16[6,1024]{0,1:T(8,128)(2,1)S(1)}, bf16[6,1024]{0,1:T(8,128)(2,1)S(1)}, u32[]{:S(2)}, u32[]{:S(2)}) collective-permute-start(bf16[6,1024]{0,1:T(8,128)(2,1)S(1)} %copy.33), channel_id=1, source_target_pairs={{0,4},{4,8},{8,12},{12,16},{16,20},{20,24},{24,28},{28,32},{32,36}... | collective-permute-start | bytes 36872 | tf_op jit(solution)/shard_map/ppermute | solution.py:13
  19.3 54.5 %copy-start.7 = (f32[130,64]{1,0:T(8,128)S(1)}, f32[130,64]{1,0:T(8,128)}, u32[]{:S(2)}) copy-start(f32[130,64]{1,0:T(8,128)} %constant.55.clone) | copy-start | bytes 99844
  76.2 0.9 copy-start.5
  76.2 0.9 copy-start.6
  77.1 1.2 copy-start
  82.2 1.9 copy-start.3
  82.2 1.9 copy-start.4
  84.1 0.8 copy-start.9
  84.5 1.5 copy-start.8
  86.0 7.6 %copy-start.1 = (bf16[256,1024]{1,0:T(8,128)(2,1)S(1)}, bf16[256,1024]{1,0:T(8,128)(2,1)}, u32[]{:S(2)}) copy-start(bf16[256,1024]{1,0:T(8,128)(2,1)} %param.16) | copy-start | bytes 1572868
  87.5 44.4 %copy-start.10 = (f32[1024]{0:T(1024)S(1)}, f32[1024]{0:T(1024)}, u32[]{:S(2)}) copy-start(f32[1024]{0:T(1024)} %param.21) | copy-start | bytes 12292
  88.6 43.3 %all-to-all-start.1 = ((bf16[64,16,256]{2,1,0:T(8,128)(2,1)}), bf16[64,16,256]{2,1,0:T(8,128)(2,1)S(1)}, u32[]{:S(2)}, u32[]{:S(2)}) async-start(bf16[64,16,256]{2,1,0:T(8,128)(2,1)} %copy.42), calls=%async_computation.1 | async-start | bytes 1048576 | tf_op jit(solution)/shard_map/all_to_all | solution.py:102
  133.2 37.2 %collective-permute-start.2 = (bf16[256,1024]{0,1:T(8,128)(2,1)S(1)}, bf16[256,1024]{0,1:T(8,128)(2,1)S(1)}, u32[]{:S(2)}, u32[]{:S(2)}) collective-permute-start(bf16[256,1024]{0,1:T(8,128)(2,1)S(1)} %fusion.38), channel_id=1, source_target_pairs={{0,2},{1,3},{2,0},{3,1},{4,6},{5,7},{6,4},{7,5},{8,10},{9,11},{10,... | collective-permute-start | bytes 1572872 | tf_op jit(solution)/shard_map/ppermute | solution.py:119
  133.3 50.6 %collective-permute-start.3 = (bf16[256,1024]{0,1:T(8,128)(2,1)S(1)}, bf16[256,1024]{0,1:T(8,128)(2,1)S(1)}, u32[]{:S(2)}, u32[]{:S(2)}) collective-permute-start(bf16[256,1024]{0,1:T(8,128)(2,1)S(1)} %fusion.38), channel_id=1, source_target_pairs={{0,3},{1,0},{2,1},{3,2},{4,7},{5,4},{6,5},{7,6},{8,11},{9,8},{10,9... | collective-permute-start | bytes 1572872 | tf_op jit(solution)/shard_map/ppermute | solution.py:119
  135.8 50.5 %collective-permute-start.1 = (bf16[256,1024]{0,1:T(8,128)(2,1)S(1)}, bf16[256,1024]{0,1:T(8,128)(2,1)S(1)}, u32[]{:S(2)}, u32[]{:S(2)}) collective-permute-start(bf16[256,1024]{0,1:T(8,128)(2,1)S(1)} %fusion.38), channel_id=1, source_target_pairs={{0,1},{1,2},{2,3},{3,0},{4,5},{5,6},{6,7},{7,4},{8,9},{9,10},{10,1... | collective-permute-start | bytes 1572872 | tf_op jit(solution)/shard_map/ppermute | solution.py:119
Sparse Core Ops, SparseCore 0:
  10.9 144.4 all-gather.1

commit v12 on v11

--- a/solution.py
+++ b/solution.py
@@ -39,7 +39,10 @@
     tables = (
         first_table, twist_cos, twist_sin, forward, backward.T, twist_cos_t, twist_sin_t, last_cos, last_sin
     )
-    return tuple(as32(a) for a in tables)
+    first_table, *rest = map(as32, tables)
+    first_high = first_table.astype(jnp.bfloat16)
+    first_low = (first_table - first_high.astype(jnp.float32)).astype(jnp.bfloat16)
+    return ((first_high, first_low), *rest)
 
 
 def dot(a, b):
@@ -53,8 +56,10 @@
 def long_conv(pieces, per_device, tables):
     first_table, twist_cos, twist_sin, forward, backward, back_cos, back_sin, last_cos, last_sin = tables
     blocks, both, tokens = pieces.shape
-    outer = first_table.shape[0] // 2
-    spec = dot(first_table, pieces.reshape(blocks, both * tokens)).reshape(2, outer, both, tokens)
+    outer = first_table[0].shape[0] // 2
+    values = pieces.reshape(blocks, both * tokens)
+    spec = sum(jnp.dot(t, values, preferred_element_type=jnp.float32) for t in first_table)
+    spec = spec.reshape(2, outer, both, tokens)
     s_real, s_imag = spec[0], spec[1]
     w_real = s_real * twist_cos + s_imag * twist_sin
     w_imag = s_imag * twist_cos - s_real * twist_sin
@@ -88,8 +93,7 @@
     per_device = channels // groups
     tables = make_tables(groups, tokens_here)
     weights = lax.all_gather(out_weight, "seq", axis=0, tiled=True)
-    ends = jnp.concatenate([query_rows[-2:], key_rows[-2:], value_rows[-2:]], 0)
-    tails = jnp.split(shifted(ends, "seq", 1), 3, 0)
+    tails = shifted((query_rows[-2:], key_rows[-2:], value_rows[-2:]), "seq", 1)
     query_mix = causal_short(query_rows, tails[0], short_filter[:, 0, :])
     key_mix = causal_short(key_rows, tails[1], short_filter[:, 1, :])
     value_mix = causal_short(value_rows, tails[2], short_filter[:, 2, :])

time: 197 us -> 198 us (level)
  the two profiles are of different devices: /device:TPU:33 before, /device:TPU:63 now
where the time goes in v12:
time: 198 us; the launch traced here: 197 us
  waiting for transfers between devices  81.6 us (41%)
  blocking collectives  40.4 us (20%)
  starting transfers between devices  26.8 us (14%)
  matrix products  19.5 us (10%)
  between operations  13.8 us (7%)
  local copies, waits for them, and re-layouts  9.23 us (5%)
  other arithmetic  6.17 us (3%)
    ppermute x3, waiting for transfers between devices, shifted(): return lax.ppermute(value, axis, pairs)  40.5 us
    all_to_all x1, blocking collectives, block(): lax.all_to_all(outgoing, 'seq', split_axis=0, concat_axis=0, tiled=True)  40.4 us
    ppermute x3, waiting for transfers between devices, projection(): lax.ppermute(inner, 'tp', [(j, (j + k) % size) for j in range(size)])  28.1 us
    ppermute x3, starting transfers between devices, shifted(): return lax.ppermute(value, axis, pairs)  17.3 us
    all_gather x1, waiting for transfers between devices, block(): weights = lax.all_gather(out_weight, 'seq', axis=0, tiled=True)  12.3 us
    all_to_all x1, starting transfers between devices, block(): lax.all_to_all(mixed, 'seq', split_axis=0, concat_axis=0, tiled=True)  7.87 us
    dot_general x3, matrix products, projection(): jnp.dot(chunk, rows_of((here - k) % size), preferred_element_type=jnp.flo...  7.76 us
    unnamed x33, local copies, waits for them, and re-layouts  4.76 us
  transfers between devices with their start and end apart: 8, of which 6 were waited for; matrix products, arithmetic and copies ran while one was open for 16% of the time, Pallas kernels for 0%

profile of v12, /device:TPU:63, one launch (start us, length us, event | category | flops | bytes accessed | tf_op | source)
XLA Modules:
  0.0 197.5 jit_solution(14236612421836543218)
XLA Ops:
  6.5 0.0 all-gather.2.cloned.1.call-start
  6.5 0.7 all-gather.2.cloned.1.call-update
  7.3 0.7 slice.109
  8.0 0.2 copy.36
  8.2 8.1 %collective-permute-start.1 = (bf16[2,1024]{0,1:T(8,128)(2,1)S(1)}, bf16[2,1024]{0,1:T(8,128)(2,1)S(1)}, u32[]{:S(2)}, u32[]{:S(2)}) collective-permute-start(bf16[2,1024]{0,1:T(8,128)(2,1)S(1)} %copy.36), channel_id=1, source_target_pairs={{0,4},{4,8},{8,12},{12,16},{16,20},{20,24},{24,28},{28,32},{32,36}... | collective-permute-start | bytes 12296 | tf_op jit(solution)/shard_map/ppermute | solution.py:13
  16.3 0.7 slice.115
  17.0 0.2 copy.39
  17.2 1.9 collective-permute-start.2
  19.1 0.9 fusion.49
  20.0 1.2 copy.35
  21.3 0.2 copy.38
  21.5 0.2 copy.41
  21.7 3.4 %collective-permute-done.1 = bf16[2,1024]{0,1:T(8,128)(2,1)S(1)} collective-permute-done((bf16[2,1024]{0,1:T(8,128)(2,1)S(1)}, bf16[2,1024]{0,1:T(8,128)(2,1)S(1)}, u32[]{:S(2)}, u32[]{:S(2)}) %collective-permute-start.1) | collective-permute-done | bytes 4128 | tf_op jit(solution)/shard_map/ppermute | solution.py:13
  25.2 3.7 %collective-permute-done.2 = bf16[2,1024]{0,1:T(8,128)(2,1)} collective-permute-done((bf16[2,1024]{0,1:T(8,128)(2,1)S(1)}, bf16[2,1024]{0,1:T(8,128)(2,1)}, u32[]{:S(2)}, u32[]{:S(2)}) %collective-permute-start.2) | collective-permute-done | bytes 4128 | tf_op jit(solution)/shard_map/ppermute | solution.py:13
  28.9 3.2 %multiply_convert_fusion = bf16[256,1024]{0,1:T(8,128)(2,1)S(1)} fusion(bf16[256,1024]{0,1:T(8,128)(2,1)S(1)} %copy.38, bf16[256,1024]{0,1:T(8,128)(2,1)S(1)} %copy.35, bf16[2,1024]{0,1:T(8,128)(2,1)} %collective-permute-done.2, bf16[2,1024]{0,1:T(8,128)(2,1)S(1)} %collective-permute-done.1, f32[1024]{0:T(1024)S(1)} %bitcast.69, f32[1024]{0:T(1024)S(1)} %bitcast.70, ...), kind=kLoop, calls=%fused_computation.39 | loop fusion | flops 7864320 | bytes 1605632 | tf_op jit(solution)/shard_map/convert_element_type | solution.py:100
  32.1 0.1 pad_maximum_fusion
  32.2 0.0 copy-start.8
  32.2 40.4 %all_to_all.10 = bf16[64,32,256]{2,1,0:T(8,128)(2,1)S(1)} all-to-all(bf16[64,32,256]{2,1,0:T(8,128)(2,1)S(1)} %pad_maximum_fusion), channel_id=1, replica_groups=mesh['seq'=64,'tp'=4] {'seq'}, dimensions={0} | all-to-all | bytes 2097152 | tf_op jit(solution)/shard_map/all_to_all | solution.py:104
  72.6 0.6 copy.45
  73.2 0.0 copy-start.9
  73.2 0.7 fusion.50
  73.9 0.0 copy-done.9
  74.0 0.7 convolution_add_fusion
  74.7 0.4 fusion.48
  75.1 0.7 copy.46
  75.8 0.0 copy-start.6
  75.8 0.0 copy-start.7
  75.8 0.7 copy.47
  76.6 0.1 copy-done.6
  76.7 0.0 copy-done.7
  76.8 1.0 multiply_add_fusion
  77.8 0.2 copy-done
  78.0 3.5 %fusion = f32[65,32,512]{2,1,0:T(8,128)S(1)} fusion(f32[512,512,1]{1,0,2:T(8,128)S(1)} %copy-done, f32[65,32,256]{2,1,0:T(8,128)S(1)} %get-tuple-element.6, f32[65,32,256]{2,1,0:T(8,128)S(1)} %get-tuple-element.5), kind=kOutput, calls=%fused_computation.1 | convolution fusion | flops 3272622080 | bytes 9568256 | tf_op jit(solution)/shard_map/dot_general | solution.py:49
  81.5 0.3 multiply_subtract_fusion.2
  81.8 0.0 copy-start.4
  81.8 0.0 copy-start.5
  81.8 1.9 fusion.16
  83.7 0.0 copy-start.11
  83.7 0.3 multiply_add_fusion.1
  84.1 0.0 copy-start.10
  84.1 0.4 copy-done.11
  84.5 1.2 fusion.34
  85.6 0.0 copy-start.2
  85.7 1.4 fusion.32
  87.1 0.0 copy-start.12
  87.1 1.1 copy.44
  88.2 7.9 %all-to-all-start.1 = ((bf16[64,16,256]{2,1,0:T(8,128)(2,1)}), bf16[64,16,256]{2,1,0:T(8,128)(2,1)S(1)}, u32[]{:S(2)}, u32[]{:S(2)}) async-start(bf16[64,16,256]{2,1,0:T(8,128)(2,1)} %copy.44), calls=%async_computation.1 | async-start | bytes 1048576 | tf_op jit(solution)/shard_map/all_to_all | solution.py:106
  96.1 0.2 copy.33
  96.3 7.3 %collective-permute-start = (bf16[2,1024]{0,1:T(8,128)(2,1)S(1)}, bf16[2,1024]{0,1:T(8,128)(2,1)S(1)}, u32[]{:S(2)}, u32[]{:S(2)}) collective-permute-start(bf16[2,1024]{0,1:T(8,128)(2,1)S(1)} %copy.33), channel_id=1, source_target_pairs={{0,4},{4,8},{8,12},{12,16},{16,20},{20,24},{24,28},{28,32},{32,36}... | collective-permute-start | bytes 12296 | tf_op jit(solution)/shard_map/ppermute | solution.py:13
  103.6 0.2 copy.32
  103.8 33.4 %collective-permute-done = bf16[2,1024]{0,1:T(8,128)(2,1)S(1)} collective-permute-done((bf16[2,1024]{0,1:T(8,128)(2,1)S(1)}, bf16[2,1024]{0,1:T(8,128)(2,1)S(1)}, u32[]{:S(2)}, u32[]{:S(2)}) %collective-permute-start) | collective-permute-done | bytes 4128 | tf_op jit(solution)/shard_map/ppermute | solution.py:13
  137.2 0.0 all-to-all-done.1
  137.2 1.2 fusion.38
  138.4 0.1 collective-permute-start.4
  138.6 0.1 collective-permute-start.5
  138.7 1.5 collective-permute-start.3
  140.1 12.3 %all-gather.2.cloned.1.call-done = bf16[4096,1024]{1,0:T(8,128)(2,1)} async-done(((bf16[64,1024]{1,0:T(8,128)(2,1)}), bf16[4096,1024]{1,0:T(8,128)(2,1)}) %all-gather.2.cloned.1.call-update) | async-done | bytes 8388624 | tf_op jit(solution)/shard_map/all_gather | solution.py:95
  152.4 2.3 %fusion.14 = f32[256,1024]{1,0:T(8,128)S(1)} fusion(bf16[256,1024]{0,1:T(8,128)(2,1)S(1)} %fusion.38, bf16[4096,1024]{1,0:T(8,128)(2,1)} %all-gather.2.cloned.1.call-done, s32[]{:T(128)S(6)} %select_n.27), kind=kOutput, calls=%fused_computation.17 | convolution fusion | flops 536870912 | bytes 3670020 | tf_op jit(solution)/shard_map/dot_general | solution.py:125
  154.7 11.6 %collective-permute-done.4 = bf16[256,1024]{0,1:T(8,128)(2,1)S(1)} collective-permute-done((bf16[256,1024]{0,1:T(8,128)(2,1)S(1)}, bf16[256,1024]{0,1:T(8,128)(2,1)S(1)}, u32[]{:S(2)}, u32[]{:S(2)}) %collective-permute-start.4) | collective-permute-done | bytes 524320 | tf_op jit(solution)/shard_map/ppermute | solution.py:123
  166.3 2.3 %fusion.10 = f32[256,1024]{1,0:T(8,128)S(1)} fusion(bf16[256,1024]{0,1:T(8,128)(2,1)S(1)} %collective-permute-done.4, bf16[4096,1024]{1,0:T(8,128)(2,1)} %all-gather.2.cloned.1.call-done, s32[]{:T(128)S(6)} %select_n.31), kind=kOutput, calls=%fused_computation.13 | convolution fusion | flops 536870912 | bytes 3670020 | tf_op jit(solution)/shard_map/dot_general | solution.py:127
  168.6 16.5 %collective-permute-done.5 = bf16[256,1024]{0,1:T(8,128)(2,1)S(1)} collective-permute-done((bf16[256,1024]{0,1:T(8,128)(2,1)S(1)}, bf16[256,1024]{0,1:T(8,128)(2,1)S(1)}, u32[]{:S(2)}, u32[]{:S(2)}) %collective-permute-start.5) | collective-permute-done | bytes 524320 | tf_op jit(solution)/shard_map/ppermute | solution.py:123
  185.2 2.3 %fusion.8 = f32[256,1024]{1,0:T(8,128)S(1)} fusion(bf16[256,1024]{0,1:T(8,128)(2,1)S(1)} %collective-permute-done.5, bf16[4096,1024]{1,0:T(8,128)(2,1)} %all-gather.2.cloned.1.call-done, s32[]{:T(128)S(6)} %select_n.33), kind=kOutput, calls=%fused_computation.11 | convolution fusion | flops 536870912 | bytes 3670020 | tf_op jit(solution)/shard_map/dot_general | solution.py:127
  187.5 0.0 collective-permute-done.3
  187.5 3.1 %fusion.28 = bf16[256,1024]{1,0:T(8,128)(2,1)} fusion(f32[256,1024]{1,0:T(8,128)S(1)} %fusion.8, f32[256,1024]{1,0:T(8,128)S(1)} %fusion.10, f32[256,1024]{1,0:T(8,128)S(1)} %fusion.14, bf16[256,1024]{0,1:T(8,128)(2,1)S(1)} %collective-permute-done.3, bf16[4096,1024]{1,0:T(8,128)(2,1)} %all-gather.2.cloned.1.call-done, s32[]{:T(128)S(6)} %select_n.29), kind=kOutput, calls=%fused_computation.24 | convolution fusion | flops 537919488 | bytes 6291460 | tf_op jit(solution)/shard_map/dot_general | solution.py:127
  (12 shorter events, 0.0 us)
Async XLA Ops:
  6.5 14.8 %copy-start.1 = (bf16[256,1024]{1,0:T(8,128)(2,1)S(1)}, bf16[256,1024]{1,0:T(8,128)(2,1)}, u32[]{:S(2)}) copy-start(bf16[256,1024]{1,0:T(8,128)(2,1)} %param.18) | copy-start | bytes 1572868
  6.5 15.0 %copy-start.3 = (bf16[256,1024]{1,0:T(8,128)(2,1)S(1)}, bf16[256,1024]{1,0:T(8,128)(2,1)}, u32[]{:S(2)}) copy-start(bf16[256,1024]{1,0:T(8,128)(2,1)} %param.20) | copy-start | bytes 1572868
  6.5 145.9 %all-gather.2.cloned.1.call-start = ((), (), s32[]{:S(2)}) async-start(), calls=%async_computation.2 | async-start | bytes 8519680 | tf_op jit(solution)/shard_map/all_gather | solution.py:95
  8.2 17.0 %collective-permute-start.1 = (bf16[2,1024]{0,1:T(8,128)(2,1)S(1)}, bf16[2,1024]{0,1:T(8,128)(2,1)S(1)}, u32[]{:S(2)}, u32[]{:S(2)}) collective-permute-start(bf16[2,1024]{0,1:T(8,128)(2,1)S(1)} %copy.36), channel_id=1, source_target_pairs={{0,4},{4,8},{8,12},{12,16},{16,20},{20,24},{24,28},{28,32},{32,36}... | collective-permute-start | bytes 12296 | tf_op jit(solution)/shard_map/ppermute | solution.py:13
  17.2 11.7 %collective-permute-start.2 = (bf16[2,1024]{0,1:T(8,128)(2,1)S(1)}, bf16[2,1024]{0,1:T(8,128)(2,1)}, u32[]{:S(2)}, u32[]{:S(2)}) collective-permute-start(bf16[2,1024]{0,1:T(8,128)(2,1)S(1)} %copy.39), channel_id=1, source_target_pairs={{0,4},{4,8},{8,12},{12,16},{16,20},{20,24},{24,28},{28,32},{32,36}... | collective-permute-start | bytes 12296 | tf_op jit(solution)/shard_map/ppermute | solution.py:13
  32.2 41.0 %copy-start.8 = (bf16[130,64]{1,0:T(8,128)(2,1)S(1)}, bf16[130,64]{1,0:T(8,128)(2,1)}, u32[]{:S(2)}) copy-start(bf16[130,64]{1,0:T(8,128)(2,1)} %constant.63) | copy-start | bytes 49924
  73.2 0.8 copy-start.9
  75.8 0.9 copy-start.6
  75.8 0.9 copy-start.7
  76.8 1.2 copy-start
  81.8 1.9 copy-start.4
  81.8 1.9 copy-start.5
  83.7 0.8 copy-start.11
  84.1 1.6 copy-start.10
  85.6 10.4 %copy-start.2 = (bf16[256,1024]{1,0:T(8,128)(2,1)S(1)}, bf16[256,1024]{1,0:T(8,128)(2,1)}, u32[]{:S(2)}) copy-start(bf16[256,1024]{1,0:T(8,128)(2,1)} %param.16) | copy-start | bytes 1572868
  87.1 50.1 %copy-start.12 = (f32[1024]{0:T(1024)S(1)}, f32[1024]{0:T(1024)}, u32[]{:S(2)}) copy-start(f32[1024]{0:T(1024)} %param.21) | copy-start | bytes 12292
  88.2 49.0 %all-to-all-start.1 = ((bf16[64,16,256]{2,1,0:T(8,128)(2,1)}), bf16[64,16,256]{2,1,0:T(8,128)(2,1)S(1)}, u32[]{:S(2)}, u32[]{:S(2)}) async-start(bf16[64,16,256]{2,1,0:T(8,128)(2,1)} %copy.44), calls=%async_computation.1 | async-start | bytes 1048576 | tf_op jit(solution)/shard_map/all_to_all | solution.py:106
  96.3 40.9 %collective-permute-start = (bf16[2,1024]{0,1:T(8,128)(2,1)S(1)}, bf16[2,1024]{0,1:T(8,128)(2,1)S(1)}, u32[]{:S(2)}, u32[]{:S(2)}) collective-permute-start(bf16[2,1024]{0,1:T(8,128)(2,1)S(1)} %copy.33), channel_id=1, source_target_pairs={{0,4},{4,8},{8,12},{12,16},{16,20},{20,24},{24,28},{28,32},{32,36}... | collective-permute-start | bytes 12296 | tf_op jit(solution)/shard_map/ppermute | solution.py:13
  138.4 27.9 %collective-permute-start.4 = (bf16[256,1024]{0,1:T(8,128)(2,1)S(1)}, bf16[256,1024]{0,1:T(8,128)(2,1)S(1)}, u32[]{:S(2)}, u32[]{:S(2)}) collective-permute-start(bf16[256,1024]{0,1:T(8,128)(2,1)S(1)} %fusion.38), channel_id=1, source_target_pairs={{0,2},{1,3},{2,0},{3,1},{4,6},{5,7},{6,4},{7,5},{8,10},{9,11},{10,... | collective-permute-start | bytes 1572872 | tf_op jit(solution)/shard_map/ppermute | solution.py:123
  138.6 46.6 %collective-permute-start.5 = (bf16[256,1024]{0,1:T(8,128)(2,1)S(1)}, bf16[256,1024]{0,1:T(8,128)(2,1)S(1)}, u32[]{:S(2)}, u32[]{:S(2)}) collective-permute-start(bf16[256,1024]{0,1:T(8,128)(2,1)S(1)} %fusion.38), channel_id=1, source_target_pairs={{0,3},{1,0},{2,1},{3,2},{4,7},{5,4},{6,5},{7,6},{8,11},{9,8},{10,9... | collective-permute-start | bytes 1572872 | tf_op jit(solution)/shard_map/ppermute | solution.py:123
  138.7 48.8 %collective-permute-start.3 = (bf16[256,1024]{0,1:T(8,128)(2,1)S(1)}, bf16[256,1024]{0,1:T(8,128)(2,1)S(1)}, u32[]{:S(2)}, u32[]{:S(2)}) collective-permute-start(bf16[256,1024]{0,1:T(8,128)(2,1)S(1)} %fusion.38), channel_id=1, source_target_pairs={{0,1},{1,2},{2,3},{3,0},{4,5},{5,6},{6,7},{7,4},{8,9},{9,10},{10,1... | collective-permute-start | bytes 1572872 | tf_op jit(solution)/shard_map/ppermute | solution.py:123
Sparse Core Ops, SparseCore 0:
  10.9 141.4 all-gather.1
